TPU v7x, 512 devices: a whole 4x8x8 slice. The times are simulated.
512 devices in a mesh: seq: 16 (over z, y_lo), wt: 32 (over x, y_hi, core).
Axes of the slice: x: 4, y: 8 (y_hi: 4, y_lo: 2; y = y_hi * 2 + y_lo), z: 8, core: 2. Of those that a mesh axis runs over, the one named last changes fastest.
Arguments:
- tokens_in: bfloat16 [3584, 4608], P('seq', 'wt'), may hold values from -6 to 6
- norm_gain: float32 [4608], P('wt'), may hold values from 0.25 to 1.75
- positions: int32 [3584], P('seq'), may hold values from 0 to 2687, as said below
- blocks: bfloat16 [32, 64, 128, 128], P('wt'), may hold values from -0.125 to 0.125
- slot_code: int32 [32, 64], P('wt'), may hold values from -1 to 2303, as said below
- out_grad: bfloat16 [3584, 4096], P('seq', 'wt'), may hold values from -6 to 6
Outputs:
- attn_out: bfloat16 [3584, 4096], P('seq', 'wt')
- tokens_grad: bfloat16 [3584, 4608], P('seq', 'wt')
- gain_grad: float32 [4608], P('wt')
- block_grads: bfloat16 [32, 64, 128, 128], P('wt')
Inputs may be any that keep to these rules, and one draw needn't show every extreme that they name: Positions count the tokens of each document from 0: positions[0] = 0 and every later entry is either 0 (a new document starts) or the entry before plus one. The longest document has exactly 2688 tokens. slot_code[o, s] is -1 for an empty slot, else u * 2 * 36 + p with head u and 0 <= p < 72; no value other than -1 appears twice. One owner holds at most 2 blocks for one head; in every draw some owner holds 2 blocks for every head and some head has 2 blocks at every owner.
All inputs are finite; a program needn't handle non-finite values.
Results may differ from a plain program's by a relative error of at most 0.023.
Values may be sent and summed in bfloat16 or wider, within the bound.
No kernel may reach another device: no remote copies, remote signals or barrier semaphores. Data moves between devices by JAX's collectives and lax.ppermute only.
A program may use at most 64 MiB of HBM per device.

v0:
```python
import jax
import jax.numpy as jnp
from jax import lax
from jax.sharding import PartitionSpec as P

D = 4608
HD = 128
BLK = 128
CAP = 2


query_scale = 144.0 ** (-0.5)
soft_cap = 50.0
norm_eps = 1e-06


def from_partner(block, axis, stride):
    count = lax.axis_size(axis)
    route = []
    for low in range(count):
        high = low | 1 << stride
        if high != low and high < count:
            route += [(low, high), (high, low)]
    return lax.ppermute(block, axis, route)


def shifted(value, axis, steps):
    count = lax.axis_size(axis)
    initial, last = (max(0, -steps), min(count, count - steps))
    return lax.ppermute(value, axis, [(source, source + steps) for source in range(initial, last)])


def rope_tables(positions, head_width):
    half_width = head_width // 2
    frequency = 10000.0 ** (-2.0 * jnp.arange(half_width, dtype=jnp.float32) / head_width)
    angles = positions.astype(jnp.float32)[:, None] * frequency[None, :]
    return (jnp.cos(angles), jnp.sin(angles))


def rotate(vector, cos_table, sin_table):
    half_width = vector.shape[-1] // 2
    first_half = vector[..., :half_width]
    second_half = vector[..., half_width:]
    return jnp.concatenate(
        [
            first_half * cos_table - second_half * sin_table,
            first_half * sin_table + second_half * cos_table,
        ],
        axis=-1,
    )


def contract(left, right):
    return lax.dot_general(
        left, right, (((1,), (1,)), ((), ())), preferred_element_type=jnp.float32
    )


def contract_rows(left, right):
    return lax.dot_general(
        left, right, (((0,), (0,)), ((), ())), preferred_element_type=jnp.float32
    )


def body(tokens_in, norm_gain, positions, blocks, slot_code, out_grad):
    tok_rows = tokens_in.shape[0]
    groups = lax.axis_size("wt")
    slab_index = lax.axis_index("seq")
    is_even = lax.axis_index("wt") % 2 == 0
    tokens_f32 = tokens_in.astype(jnp.float32)
    squares = lax.psum(jnp.sum(tokens_f32 * tokens_f32, axis=1), "wt")
    inv_rms = lax.rsqrt(squares / D + norm_eps)
    scaled = tokens_f32 * inv_rms[:, None]
    normed_part = (scaled * norm_gain[None, :]).astype(jnp.bfloat16)
    normed = lax.all_gather(normed_part, "wt", axis=1, tiled=True)
    pos_count = 2 * (D // BLK)
    row_blocks = pos_count // 2
    slot_codes = slot_code[0]
    is_live = slot_codes >= 0
    target_user = jnp.where(is_live, slot_codes // pos_count, 0)
    user_match = (
        (target_user[:, None] == jnp.arange(groups, dtype=jnp.int32)[None, :]) & is_live[:, None]
    ).astype(jnp.int32)
    earlier = jnp.cumsum(user_match, axis=0) - user_match
    slot_rank = jnp.sum(earlier * user_match, axis=1)
    dump_slot = groups * CAP
    slot_dest = jnp.where(is_live, target_user * CAP + slot_rank, dump_slot)
    block_place = (slot_codes - target_user * pos_count).astype(jnp.float32)
    outgoing = jnp.zeros((dump_slot + 1, BLK, BLK), jnp.bfloat16).at[slot_dest].set(blocks[0])
    outgoing_pos = (
        jnp.full((dump_slot + 1,), -1.0, jnp.float32)
        .at[slot_dest]
        .set(block_place)
        .astype(jnp.bfloat16)
    )
    arrived, arrived_pos = (
        lax.all_to_all(
            outgoing[:dump_slot].reshape(groups, CAP, BLK, BLK),
            "wt",
            split_axis=0,
            concat_axis=0,
            tiled=True,
        ),
        lax.all_to_all(
            outgoing_pos[:dump_slot].reshape(groups, CAP),
            "wt",
            split_axis=0,
            concat_axis=0,
            tiled=True,
        ),
    )
    arrival = arrived_pos.reshape(-1).astype(jnp.int32)
    arrival = jnp.where(arrival < 0, pos_count, arrival)
    weight_table = (
        jnp.zeros((pos_count + 1, BLK, BLK), jnp.bfloat16)
        .at[arrival]
        .set(arrived.reshape(-1, BLK, BLK))
    )
    w_query = weight_table[:row_blocks].reshape(D, HD)
    w_pair = weight_table[row_blocks:pos_count].reshape(D, HD)
    query_proj = jnp.dot(normed, w_query, preferred_element_type=jnp.float32)
    pair_proj = jnp.dot(normed, w_pair, preferred_element_type=jnp.float32)
    cos_table, sin_table = rope_tables(positions, HD)
    query_rot = (rotate(query_proj, cos_table, sin_table) * query_scale).astype(jnp.bfloat16)
    own_pair = jnp.where(is_even, rotate(pair_proj, cos_table, sin_table), pair_proj).astype(
        jnp.bfloat16
    )
    partner = from_partner(own_pair, "wt", 0)
    key_rows = jnp.where(is_even, own_pair, partner)
    value_rows = jnp.where(is_even, partner, own_pair)
    reach_slabs = lax.axis_size("seq") // 2
    window = reach_slabs * tok_rows
    key_list = [key_rows]
    value_list = [value_rows]
    for offset in range(1, reach_slabs + 1):
        prev_key, prev_value = shifted((key_rows, value_rows), "seq", offset)
        key_list.append(prev_key)
        value_list.append(prev_value)
    key_all = jnp.concatenate(key_list, axis=0)
    value_all = jnp.concatenate(value_list, axis=0)
    local_index = jnp.arange(tok_rows, dtype=jnp.int32)
    query_index = slab_index * tok_rows + local_index
    key_index = jnp.concatenate(
        [(slab_index - offset) * tok_rows + local_index for offset in range(reach_slabs + 1)]
    )
    doc_begin = query_index - positions
    distance = query_index[:, None] - key_index[None, :]
    visible = (distance >= 0) & (distance < window) & (key_index[None, :] >= doc_begin[:, None])
    scores = contract(query_rot, key_all)
    capped = soft_cap * jnp.tanh(scores / soft_cap)
    exp_scores = jnp.where(visible, jnp.exp(capped), 0.0)
    row_total = jnp.sum(exp_scores, axis=1)
    attn_rows = (
        jnp.dot(exp_scores.astype(jnp.bfloat16), value_all, preferred_element_type=jnp.float32)
        / row_total[:, None]
    ).astype(jnp.bfloat16)
    row_delta = jnp.sum(out_grad.astype(jnp.float32) * attn_rows.astype(jnp.float32), axis=1)
    soft_probs = exp_scores / row_total[:, None]
    prob_grad = contract(out_grad, value_all)
    score_grad = soft_probs * (prob_grad - row_delta[:, None]) * (1.0 - (capped / soft_cap) ** 2)
    score_low = score_grad.astype(jnp.bfloat16)
    probs_low = soft_probs.astype(jnp.bfloat16)
    rot_grad = jnp.dot(score_low, key_all, preferred_element_type=jnp.float32)
    query_grad = (rotate(rot_grad, cos_table, -sin_table) * query_scale).astype(jnp.bfloat16)
    key_grads = contract_rows(score_low, query_rot)
    value_grads = contract_rows(probs_low, out_grad)
    key_total = key_grads[:tok_rows]
    value_total = value_grads[:tok_rows]
    for offset in range(1, reach_slabs + 1):
        recv_key, recv_value = (
            shifted(
                key_grads[offset * tok_rows : (offset + 1) * tok_rows].astype(jnp.bfloat16),
                "seq",
                -offset,
            ).astype(jnp.float32),
            shifted(
                value_grads[offset * tok_rows : (offset + 1) * tok_rows].astype(jnp.bfloat16),
                "seq",
                -offset,
            ).astype(jnp.float32),
        )
        key_total = key_total + recv_key
        value_total = value_total + recv_value
    outbound = jnp.where(is_even, value_total, key_total)
    partner_grad = from_partner(outbound.astype(jnp.bfloat16), "wt", 0).astype(outbound.dtype)
    pair_total = jnp.where(is_even, key_total, value_total) + partner_grad
    pair_grad = jnp.where(is_even, rotate(pair_total, cos_table, -sin_table), pair_total).astype(
        jnp.bfloat16
    )
    normed_grad = (
        lax.psum_scatter(
            (contract(w_query, query_grad) + contract(w_pair, pair_grad)).astype(jnp.bfloat16),
            "wt",
            scatter_dimension=0,
            tiled=True,
        )
        .astype(jnp.float32)
        .T
    )
    scaled_grad = normed_grad * norm_gain[None, :]
    row_dots = lax.psum(jnp.sum(scaled_grad * scaled, axis=1), "wt")
    tokens_grad = (inv_rms[:, None] * (scaled_grad - scaled * (row_dots / D)[:, None])).astype(
        jnp.bfloat16
    )
    gain_part = jnp.sum(normed_grad * scaled, axis=0)
    grad_query = contract_rows(normed, query_grad)
    grad_pair = contract_rows(normed, pair_grad)
    grad_table = jnp.concatenate(
        [
            grad_query.reshape(row_blocks, BLK, BLK),
            grad_pair.reshape(row_blocks, BLK, BLK),
            jnp.zeros((1, BLK, BLK), jnp.float32),
        ],
        axis=0,
    )
    slot_grads = grad_table[arrival].reshape(groups, CAP, BLK, BLK)
    empty_block = jnp.zeros((1, BLK, BLK), jnp.bfloat16)
    returned = lax.all_to_all(
        slot_grads.astype(jnp.bfloat16), "wt", split_axis=0, concat_axis=0, tiled=True
    )
    owned_grads = jnp.concatenate([returned.reshape(-1, BLK, BLK), empty_block], axis=0)[slot_dest]
    summed = (
        lax.psum(owned_grads.astype(jnp.float32).astype(jnp.bfloat16), "seq").astype(jnp.float32),
        lax.psum(gain_part.astype(jnp.bfloat16), "seq").astype(jnp.float32),
    )
    block_grads = summed[0].astype(jnp.bfloat16)
    gain_total = summed[1]
    return (attn_rows, tokens_grad, gain_total, block_grads[None])


def solution(mesh):
    placed = (
        P("seq", "wt"),
        P("wt"),
        P("seq"),
        P("wt", None, None, None),
        P("wt", None),
        P("seq", "wt"),
    )
    return jax.shard_map(
        body,
        mesh=mesh,
        in_specs=placed,
        out_specs=(P("seq", "wt"), P("seq", "wt"), P("wt"), P("wt", None, None, None)),
        check_vma=False,
    )
```

profile of v0, /device:TPU:6, one launch (start us, length us, event | category | flops | bytes accessed | tf_op | source)
XLA Modules:
  0.0 624.8 jit_solution(6291189816856732794)
XLA Ops:
  11.1 10.2 %all-to-all-start = ((bf16[32,1,2]{2,1,0:T(2,128)(2,1)}), bf16[32,1,2]{2,1,0:T(2,128)(2,1)S(1)}, u32[]{:S(2)}, u32[]{:S(2)}) async-start(bf16[32,1,2]{2,1,0:T(2,128)(2,1)} %all_to_all.16), calls=%async_computation | async-start | bytes 32768 | tf_op jit(solution)/shard_map/all_to_all | solution.py:104
  22.2 63.7 %psum.28 = f32[224]{0:T(256)S(1)} all-reduce(f32[224]{0:T(256)S(1)} %fusion.39), channel_id=1, replica_groups=mesh['seq'=16,'wt'=32] {'wt'}, use_global_device_ids=true, to_apply=%region_1.2 | all-reduce | flops 224 | bytes 1792 | tf_op jit(solution)/shard_map/psum | solution.py:71
  86.5 6.7 %scatter_fusion = bf16[65,128,128]{2,1,0:T(8,128)(2,1)S(1)} fusion(bf16[65,128,128]{2,1,0:T(8,128)(2,1)S(1)} %broadcast_in_dim.23, s32[64]{0:T(128)S(1)} %fusion.70, bf16[64,128,128]{2,1,0:T(8,128)(2,1)} %bitcast.109), kind=kCustom, calls=%fused_computation.3 | custom fusion | bytes 6291712 | tf_op jit(solution)/shard_map/scatter | solution.py:89
  93.2 1.5 slice.140
  94.7 16.1 %all-to-all-start.1 = ((bf16[32,2,128,128]{3,2,1,0:T(8,128)(2,1)}), bf16[32,2,128,128]{3,2,1,0:T(8,128)(2,1)S(1)}, u32[]{:S(2)}, u32[]{:S(2)}) async-start(bf16[32,2,128,128]{3,2,1,0:T(8,128)(2,1)} %bitcast.107), calls=%async_computation.1 | async-start | bytes 4194304 | tf_op jit(solution)/shard_map/all_to_all | solution.py:97
  112.1 51.3 %all-to-all-done.1 = bf16[32,2,128,128]{3,2,1,0:T(8,128)(2,1)S(1)} async-done(((bf16[32,2,128,128]{3,2,1,0:T(8,128)(2,1)}), bf16[32,2,128,128]{3,2,1,0:T(8,128)(2,1)S(1)}, u32[]{:S(2)}, u32[]{:S(2)}) %all-to-all-start.1) | async-done | bytes 2097184 | tf_op jit(solution)/shard_map/all_to_all | solution.py:97
  163.3 1.3 copy-done.3
  165.2 6.7 %scatter_fusion.1 = bf16[73,128,128]{2,1,0:T(8,128)(2,1)S(1)} fusion(bf16[73,128,128]{2,1,0:T(8,128)(2,1)S(1)} %broadcast_in_dim.20, s32[64]{0:T(128)S(1)} %fusion.71, bf16[64,128,128]{2,1,0:T(8,128)(2,1)} %bitcast.106), kind=kCustom, calls=%fused_computation.4 | custom fusion | bytes 6291712 | tf_op jit(solution)/shard_map/scatter | solution.py:117
  171.9 1.6 fusion.81
  173.5 18.5 %all-gather.2.cloned.1.call-done = bf16[224,4608]{0,1:T(8,128)(2,1)} async-done(((bf16[224,144]{0,1:T(8,128)(2,1)}), bf16[224,4608]{0,1:T(8,128)(2,1)}) %all-gather.2.cloned.1.call-update) | async-done | bytes 2064400 | tf_op jit(solution)/shard_map/all_gather | solution.py:75
  192.0 2.9 fusion.87
  195.5 2.1 collective-permute-start
  199.1 3.8 collective-permute-start.1
  203.0 8.0 %collective-permute-start.8 = (bf16[224,128]{1,0:T(8,128)(2,1)S(1)}, bf16[224,128]{1,0:T(8,128)(2,1)S(1)}, u32[]{:S(2)}, u32[]{:S(2)}) collective-permute-start(bf16[224,128]{1,0:T(8,128)(2,1)S(1)} %get-tuple-element.10), channel_id=1, source_target_pairs={{0,256},{32,288},{64,320},{96,352},{128,384},{160,416},{192,448},{... | collective-permute-start | bytes 172040 | tf_op jit(solution)/shard_map/ppermute | solution.py:30
  211.0 1.8 collective-permute-start.7
  212.8 2.5 collective-permute-start.6
  215.3 2.0 collective-permute-start.5
  217.3 3.3 collective-permute-start.2
  220.6 1.8 collective-permute-done.2
  222.4 5.7 collective-permute-start.3
  228.1 1.8 collective-permute-done.3
  229.9 6.5 %collective-permute-start.4 = (bf16[224,128]{1,0:T(8,128)(2,1)S(1)}, bf16[224,128]{1,0:T(8,128)(2,1)S(1)}, u32[]{:S(2)}, u32[]{:S(2)}) collective-permute-start(bf16[224,128]{1,0:T(8,128)(2,1)S(1)} %get-tuple-element.10), channel_id=1, source_target_pairs={{0,128},{32,160},{64,192},{96,224},{128,256},{160,288},{192,320},{... | collective-permute-start | bytes 172040 | tf_op jit(solution)/shard_map/ppermute | solution.py:30
  236.5 1.8 collective-permute-done.4
  238.3 7.2 %collective-permute-start.15 = (bf16[224,128]{1,0:T(8,128)(2,1)S(1)}, bf16[224,128]{1,0:T(8,128)(2,1)S(1)}, u32[]{:S(2)}, u32[]{:S(2)}) collective-permute-start(bf16[224,128]{1,0:T(8,128)(2,1)S(1)} %get-tuple-element.42), channel_id=1, source_target_pairs={{0,224},{32,256},{64,288},{96,320},{128,352},{160,384},{192,416},{... | collective-permute-start | bytes 172040 | tf_op jit(solution)/shard_map/ppermute | solution.py:30
  245.5 2.6 collective-permute-start.14
  248.1 4.9 collective-permute-start.13
  253.1 1.3 collective-permute-start.12
  254.4 3.1 collective-permute-start.9
  259.7 4.0 collective-permute-start.10
  263.7 1.8 collective-permute-done.10
  265.4 4.9 collective-permute-start.11
  270.3 1.8 collective-permute-done.11
  272.1 10.4 %collective-permute-start.16 = (bf16[224,128]{1,0:T(8,128)(2,1)S(1)}, bf16[224,128]{1,0:T(8,128)(2,1)S(1)}, u32[]{:S(2)}, u32[]{:S(2)}) collective-permute-start(bf16[224,128]{1,0:T(8,128)(2,1)S(1)} %get-tuple-element.42), channel_id=1, source_target_pairs={{0,256},{32,288},{64,320},{96,352},{128,384},{160,416},{192,448},{... | collective-permute-start | bytes 172040 | tf_op jit(solution)/shard_map/ppermute | solution.py:30
  282.6 1.5 collective-permute-done.16
  284.1 1.4 multiply_reduce_fusion
  286.7 1.3 collective-permute-start.25
  288.9 1.3 collective-permute-start.32
  290.2 1.3 collective-permute-start.31
  291.5 1.3 collective-permute-start.30
  292.8 1.3 collective-permute-start.29
  294.2 1.3 collective-permute-start.28
  295.5 3.8 collective-permute-done.32
  300.6 1.3 collective-permute-start.26
  304.1 1.3 collective-permute-start.24
  305.4 1.3 collective-permute-start.23
  308.5 1.7 collective-permute-done.26
  313.7 6.4 %collective-permute-done.24 = bf16[224,128]{1,0:T(8,128)(2,1)S(1)} collective-permute-done((bf16[224,128]{1,0:T(8,128)(2,1)S(1)}, bf16[224,128]{1,0:T(8,128)(2,1)S(1)}, u32[]{:S(2)}, u32[]{:S(2)}) %collective-permute-start.24) | collective-permute-done | bytes 57376 | tf_op jit(solution)/shard_map/ppermute | solution.py:30
  322.8 1.8 collective-permute-done.20
  324.6 2.7 collective-permute-done.19
  327.3 1.6 collective-permute-done.18
  329.1 1.9 collective-permute-start.33
  333.6 1.7 maximum_maximum_fusion
  335.3 3.8 gather_fusion
  339.1 7.3 %all-to-all-start.2 = ((bf16[32,2,128,128]{3,2,1,0:T(8,128)(2,1)}), bf16[32,2,128,128]{3,2,1,0:T(8,128)(2,1)}, u32[]{:S(2)}, u32[]{:S(2)}) async-start(bf16[32,2,128,128]{3,2,1,0:T(8,128)(2,1)} %bitcast.16), calls=%async_computation.3 | async-start | bytes 4194304 | tf_op jit(solution)/shard_map/all_to_all | solution.py:218
  347.7 2.2 fusion
  350.0 38.6 %all-to-all-done.2 = bf16[32,2,128,128]{3,2,1,0:T(8,128)(2,1)} async-done(((bf16[32,2,128,128]{3,2,1,0:T(8,128)(2,1)}), bf16[32,2,128,128]{3,2,1,0:T(8,128)(2,1)}, u32[]{:S(2)}, u32[]{:S(2)}) %all-to-all-start.2) | async-done | bytes 2097184 | tf_op jit(solution)/shard_map/all_to_all | solution.py:218
  388.6 1.8 concatenate.35
  390.4 2.1 gather_fusion.1
  392.5 61.7 %reduce-scatter.2.cloned.1.call-done = bf16[144,224]{1,0:T(8,128)(2,1)} async-done(((bf16[4608,224]{1,0:T(8,128)(2,1)}), bf16[144,224]{1,0:T(8,128)(2,1)}) %reduce-scatter.2.cloned.1.call-update) | async-done | bytes 64528 | tf_op jit(solution)/shard_map/reduce_scatter | solution.py:191
  455.2 34.9 %psum.30 = bf16[144]{0:T(256)(128)(2,1)S(1)} all-reduce(bf16[144]{0:T(256)(128)(2,1)S(1)} %get-tuple-element.4), channel_id=1, replica_groups=mesh['seq'=16,'wt'=32] {'seq'}, use_global_device_ids=true, to_apply=%region_13.14 | all-reduce | flops 144 | bytes 576 | tf_op jit(solution)/shard_map/psum | solution.py:224
  490.7 60.5 %psum.29 = f32[224]{0:T(256)S(1)} all-reduce(f32[224]{0:T(256)S(1)} %get-tuple-element.5), channel_id=1, replica_groups=mesh['seq'=16,'wt'=32] {'wt'}, use_global_device_ids=true, to_apply=%region_11.12 | all-reduce | flops 224 | bytes 1792 | tf_op jit(solution)/shard_map/psum | solution.py:201
  551.3 1.6 fusion.37
  552.9 62.3 %all-reduce.3.cloned.1.call-done = bf16[1,64,128,128]{3,2,1,0:T(8,128)(2,1)} async-done(((bf16[1,64,128,128]{3,2,1,0:T(8,128)(2,1)}), bf16[1,64,128,128]{3,2,1,0:T(8,128)(2,1)}) %all-reduce.3.cloned.1.call-update) | async-done | bytes 2097168 | tf_op jit(solution)/shard_map/psum | solution.py:223
  615.1 3.2 copy.30
  (120 shorter events, 30.6 us)
Async XLA Ops:
  11.1 83.6 %all-to-all-start = ((bf16[32,1,2]{2,1,0:T(2,128)(2,1)}), bf16[32,1,2]{2,1,0:T(2,128)(2,1)S(1)}, u32[]{:S(2)}, u32[]{:S(2)}) async-start(bf16[32,1,2]{2,1,0:T(2,128)(2,1)} %all_to_all.16), calls=%async_computation | async-start | bytes 32768 | tf_op jit(solution)/shard_map/all_to_all | solution.py:104
  94.6 16.2 %copy-start.4 = (bf16[224,144]{0,1:T(8,128)(2,1)S(1)}, bf16[224,144]{0,1:T(8,128)(2,1)}, u32[]{:S(2)}) copy-start(bf16[224,144]{0,1:T(8,128)(2,1)} %param.6) | copy-start | bytes 193540
  94.6 16.2 %copy-start.5 = (f32[144]{0:T(256)S(1)}, f32[144]{0:T(256)}, u32[]{:S(2)}) copy-start(f32[144]{0:T(256)} %param.7) | copy-start | bytes 1732
  94.6 17.2 %copy-start.6 = (s32[224]{0:T(256)S(1)}, s32[224]{0:T(256)}, u32[]{:S(2)}) copy-start(s32[224]{0:T(256)} %param.8) | copy-start | bytes 2692
  94.7 68.7 %all-to-all-start.1 = ((bf16[32,2,128,128]{3,2,1,0:T(8,128)(2,1)}), bf16[32,2,128,128]{3,2,1,0:T(8,128)(2,1)S(1)}, u32[]{:S(2)}, u32[]{:S(2)}) async-start(bf16[32,2,128,128]{3,2,1,0:T(8,128)(2,1)} %bitcast.107), calls=%async_computation.1 | async-start | bytes 4194304 | tf_op jit(solution)/shard_map/all_to_all | solution.py:97
  110.7 81.2 %all-gather.2.cloned.1.call-start = ((), (), s32[]{:S(2)}) async-start(), calls=%async_computation.4 | async-start | bytes 2433024 | tf_op jit(solution)/shard_map/all_gather | solution.py:75
  163.3 1.3 copy-start.3
  191.9 5.7 copy-start
  191.9 5.7 copy-start.1
  195.5 3.5 collective-permute-start
  199.1 18.2 %collective-permute-start.1 = (bf16[224,128]{1,0:T(8,128)(2,1)S(1)}, bf16[224,128]{1,0:T(8,128)(2,1)S(1)}, u32[]{:S(2)}, u32[]{:S(2)}) collective-permute-start(bf16[224,128]{1,0:T(8,128)(2,1)S(1)} %get-tuple-element.10), channel_id=1, source_target_pairs={{0,32},{32,64},{64,96},{96,128},{128,160},{160,192},{192,224},{224... | collective-permute-start | bytes 172040 | tf_op jit(solution)/shard_map/ppermute | solution.py:30
  203.0 51.4 %collective-permute-start.8 = (bf16[224,128]{1,0:T(8,128)(2,1)S(1)}, bf16[224,128]{1,0:T(8,128)(2,1)S(1)}, u32[]{:S(2)}, u32[]{:S(2)}) collective-permute-start(bf16[224,128]{1,0:T(8,128)(2,1)S(1)} %get-tuple-element.10), channel_id=1, source_target_pairs={{0,256},{32,288},{64,320},{96,352},{128,384},{160,416},{192,448},{... | collective-permute-start | bytes 172040 | tf_op jit(solution)/shard_map/ppermute | solution.py:30
  211.0 42.1 %collective-permute-start.7 = (bf16[224,128]{1,0:T(8,128)(2,1)S(1)}, bf16[224,128]{1,0:T(8,128)(2,1)S(1)}, u32[]{:S(2)}, u32[]{:S(2)}) collective-permute-start(bf16[224,128]{1,0:T(8,128)(2,1)S(1)} %get-tuple-element.10), channel_id=1, source_target_pairs={{0,224},{32,256},{64,288},{96,320},{128,352},{160,384},{192,416},{... | collective-permute-start | bytes 172040 | tf_op jit(solution)/shard_map/ppermute | solution.py:30
  212.8 35.3 %collective-permute-start.6 = (bf16[224,128]{1,0:T(8,128)(2,1)S(1)}, bf16[224,128]{1,0:T(8,128)(2,1)S(1)}, u32[]{:S(2)}, u32[]{:S(2)}) collective-permute-start(bf16[224,128]{1,0:T(8,128)(2,1)S(1)} %get-tuple-element.10), channel_id=1, source_target_pairs={{0,192},{32,224},{64,256},{96,288},{128,320},{160,352},{192,384},{... | collective-permute-start | bytes 172040 | tf_op jit(solution)/shard_map/ppermute | solution.py:30
  215.3 30.2 %collective-permute-start.5 = (bf16[224,128]{1,0:T(8,128)(2,1)S(1)}, bf16[224,128]{1,0:T(8,128)(2,1)S(1)}, u32[]{:S(2)}, u32[]{:S(2)}) collective-permute-start(bf16[224,128]{1,0:T(8,128)(2,1)S(1)} %get-tuple-element.10), channel_id=1, source_target_pairs={{0,160},{32,192},{64,224},{96,256},{128,288},{160,320},{192,352},{... | collective-permute-start | bytes 172040 | tf_op jit(solution)/shard_map/ppermute | solution.py:30
  217.3 5.1 collective-permute-start.2
  222.4 7.5 %collective-permute-start.3 = (bf16[224,128]{1,0:T(8,128)(2,1)S(1)}, bf16[224,128]{1,0:T(8,128)(2,1)S(1)}, u32[]{:S(2)}, u32[]{:S(2)}) collective-permute-start(bf16[224,128]{1,0:T(8,128)(2,1)S(1)} %get-tuple-element.10), channel_id=1, source_target_pairs={{0,96},{32,128},{64,160},{96,192},{128,224},{160,256},{192,288},{2... | collective-permute-start | bytes 172040 | tf_op jit(solution)/shard_map/ppermute | solution.py:30
  229.9 8.3 %collective-permute-start.4 = (bf16[224,128]{1,0:T(8,128)(2,1)S(1)}, bf16[224,128]{1,0:T(8,128)(2,1)S(1)}, u32[]{:S(2)}, u32[]{:S(2)}) collective-permute-start(bf16[224,128]{1,0:T(8,128)(2,1)S(1)} %get-tuple-element.10), channel_id=1, source_target_pairs={{0,128},{32,160},{64,192},{96,224},{128,256},{160,288},{192,320},{... | collective-permute-start | bytes 172040 | tf_op jit(solution)/shard_map/ppermute | solution.py:30
  238.3 44.4 %collective-permute-start.15 = (bf16[224,128]{1,0:T(8,128)(2,1)S(1)}, bf16[224,128]{1,0:T(8,128)(2,1)S(1)}, u32[]{:S(2)}, u32[]{:S(2)}) collective-permute-start(bf16[224,128]{1,0:T(8,128)(2,1)S(1)} %get-tuple-element.42), channel_id=1, source_target_pairs={{0,224},{32,256},{64,288},{96,320},{128,352},{160,384},{192,416},{... | collective-permute-start | bytes 172040 | tf_op jit(solution)/shard_map/ppermute | solution.py:30
  245.5 37.1 %collective-permute-start.14 = (bf16[224,128]{1,0:T(8,128)(2,1)S(1)}, bf16[224,128]{1,0:T(8,128)(2,1)S(1)}, u32[]{:S(2)}, u32[]{:S(2)}) collective-permute-start(bf16[224,128]{1,0:T(8,128)(2,1)S(1)} %get-tuple-element.42), channel_id=1, source_target_pairs={{0,192},{32,224},{64,256},{96,288},{128,320},{160,352},{192,384},{... | collective-permute-start | bytes 172040 | tf_op jit(solution)/shard_map/ppermute | solution.py:30
  248.1 34.4 %collective-permute-start.13 = (bf16[224,128]{1,0:T(8,128)(2,1)S(1)}, bf16[224,128]{1,0:T(8,128)(2,1)S(1)}, u32[]{:S(2)}, u32[]{:S(2)}) collective-permute-start(bf16[224,128]{1,0:T(8,128)(2,1)S(1)} %get-tuple-element.42), channel_id=1, source_target_pairs={{0,160},{32,192},{64,224},{96,256},{128,288},{160,320},{192,352},{... | collective-permute-start | bytes 172040 | tf_op jit(solution)/shard_map/ppermute | solution.py:30
  253.1 29.5 %collective-permute-start.12 = (bf16[224,128]{1,0:T(8,128)(2,1)S(1)}, bf16[224,128]{1,0:T(8,128)(2,1)S(1)}, u32[]{:S(2)}, u32[]{:S(2)}) collective-permute-start(bf16[224,128]{1,0:T(8,128)(2,1)S(1)} %get-tuple-element.42), channel_id=1, source_target_pairs={{0,128},{32,160},{64,192},{96,224},{128,256},{160,288},{192,320},{... | collective-permute-start | bytes 172040 | tf_op jit(solution)/shard_map/ppermute | solution.py:30
  254.4 5.3 collective-permute-start.9
  257.5 1.1 copy-start.7
  259.7 5.8 collective-permute-start.10
  265.4 6.7 %collective-permute-start.11 = (bf16[224,128]{1,0:T(8,128)(2,1)S(1)}, bf16[224,128]{1,0:T(8,128)(2,1)S(1)}, u32[]{:S(2)}, u32[]{:S(2)}) collective-permute-start(bf16[224,128]{1,0:T(8,128)(2,1)S(1)} %get-tuple-element.42), channel_id=1, source_target_pairs={{0,96},{32,128},{64,160},{96,192},{128,224},{160,256},{192,288},{2... | collective-permute-start | bytes 172040 | tf_op jit(solution)/shard_map/ppermute | solution.py:30
  272.1 12.0 %collective-permute-start.16 = (bf16[224,128]{1,0:T(8,128)(2,1)S(1)}, bf16[224,128]{1,0:T(8,128)(2,1)S(1)}, u32[]{:S(2)}, u32[]{:S(2)}) collective-permute-start(bf16[224,128]{1,0:T(8,128)(2,1)S(1)} %get-tuple-element.42), channel_id=1, source_target_pairs={{0,256},{32,288},{64,320},{96,352},{128,384},{160,416},{192,448},{... | collective-permute-start | bytes 172040 | tf_op jit(solution)/shard_map/ppermute | solution.py:30
  286.7 7.4 %collective-permute-start.25 = (bf16[224,128]{1,0:T(8,128)(2,1)S(1)}, bf16[224,128]{1,0:T(8,128)(2,1)S(1)}, u32[]{:S(2)}, u32[]{:S(2)}) collective-permute-start(bf16[224,128]{1,0:T(8,128)(2,1)S(1)} %get-tuple-element.17), channel_id=1, source_target_pairs={{32,0},{64,32},{96,64},{128,96},{160,128},{192,160},{224,192},{256... | collective-permute-start | bytes 172040 | tf_op jit(solution)/shard_map/ppermute | solution.py:30
  288.9 10.3 %collective-permute-start.32 = (bf16[224,128]{1,0:T(8,128)(2,1)S(1)}, bf16[224,128]{1,0:T(8,128)(2,1)S(1)}, u32[]{:S(2)}, u32[]{:S(2)}) collective-permute-start(bf16[224,128]{1,0:T(8,128)(2,1)S(1)} %get-tuple-element.18), channel_id=1, source_target_pairs={{256,0},{288,32},{320,64},{352,96},{384,128},{416,160},{448,192},{... | collective-permute-start | bytes 172040 | tf_op jit(solution)/shard_map/ppermute | solution.py:30
  290.2 10.3 %collective-permute-start.31 = (bf16[224,128]{1,0:T(8,128)(2,1)S(1)}, bf16[224,128]{1,0:T(8,128)(2,1)S(1)}, u32[]{:S(2)}, u32[]{:S(2)}) collective-permute-start(bf16[224,128]{1,0:T(8,128)(2,1)S(1)} %get-tuple-element.19), channel_id=1, source_target_pairs={{224,0},{256,32},{288,64},{320,96},{352,128},{384,160},{416,192},{... | collective-permute-start | bytes 172040 | tf_op jit(solution)/shard_map/ppermute | solution.py:30
  291.5 11.2 %collective-permute-start.30 = (bf16[224,128]{1,0:T(8,128)(2,1)S(1)}, bf16[224,128]{1,0:T(8,128)(2,1)S(1)}, u32[]{:S(2)}, u32[]{:S(2)}) collective-permute-start(bf16[224,128]{1,0:T(8,128)(2,1)S(1)} %get-tuple-element.20), channel_id=1, source_target_pairs={{192,0},{224,32},{256,64},{288,96},{320,128},{352,160},{384,192},{... | collective-permute-start | bytes 172040 | tf_op jit(solution)/shard_map/ppermute | solution.py:30
  292.8 11.2 %collective-permute-start.29 = (bf16[224,128]{1,0:T(8,128)(2,1)S(1)}, bf16[224,128]{1,0:T(8,128)(2,1)S(1)}, u32[]{:S(2)}, u32[]{:S(2)}) collective-permute-start(bf16[224,128]{1,0:T(8,128)(2,1)S(1)} %get-tuple-element.21), channel_id=1, source_target_pairs={{160,0},{192,32},{224,64},{256,96},{288,128},{320,160},{352,192},{... | collective-permute-start | bytes 172040 | tf_op jit(solution)/shard_map/ppermute | solution.py:30
  294.2 11.2 %collective-permute-start.28 = (bf16[224,128]{1,0:T(8,128)(2,1)S(1)}, bf16[224,128]{1,0:T(8,128)(2,1)S(1)}, u32[]{:S(2)}, u32[]{:S(2)}) collective-permute-start(bf16[224,128]{1,0:T(8,128)(2,1)S(1)} %get-tuple-element.22), channel_id=1, source_target_pairs={{128,0},{160,32},{192,64},{224,96},{256,128},{288,160},{320,192},{... | collective-permute-start | bytes 172040 | tf_op jit(solution)/shard_map/ppermute | solution.py:30
  299.3 7.9 %collective-permute-start.27 = (bf16[224,128]{1,0:T(8,128)(2,1)S(1)}, bf16[224,128]{1,0:T(8,128)(2,1)S(1)}, u32[]{:S(2)}, u32[]{:S(2)}) collective-permute-start(bf16[224,128]{1,0:T(8,128)(2,1)S(1)} %get-tuple-element.23), channel_id=1, source_target_pairs={{96,0},{128,32},{160,64},{192,96},{224,128},{256,160},{288,192},{3... | collective-permute-start | bytes 172040 | tf_op jit(solution)/shard_map/ppermute | solution.py:30
  300.6 9.7 %collective-permute-start.26 = (bf16[224,128]{1,0:T(8,128)(2,1)S(1)}, bf16[224,128]{1,0:T(8,128)(2,1)S(1)}, u32[]{:S(2)}, u32[]{:S(2)}) collective-permute-start(bf16[224,128]{1,0:T(8,128)(2,1)S(1)} %get-tuple-element.24), channel_id=1, source_target_pairs={{64,0},{96,32},{128,64},{160,96},{192,128},{224,160},{256,192},{28... | collective-permute-start | bytes 172040 | tf_op jit(solution)/shard_map/ppermute | solution.py:30
  302.8 9.6 %collective-permute-start.17 = (bf16[224,128]{1,0:T(8,128)(2,1)S(1)}, bf16[224,128]{1,0:T(8,128)(2,1)S(1)}, u32[]{:S(2)}, u32[]{:S(2)}) collective-permute-start(bf16[224,128]{1,0:T(8,128)(2,1)S(1)} %get-tuple-element.25), channel_id=1, source_target_pairs={{32,0},{64,32},{96,64},{128,96},{160,128},{192,160},{224,192},{256... | collective-permute-start | bytes 172040 | tf_op jit(solution)/shard_map/ppermute | solution.py:30
  304.1 16.0 %collective-permute-start.24 = (bf16[224,128]{1,0:T(8,128)(2,1)S(1)}, bf16[224,128]{1,0:T(8,128)(2,1)S(1)}, u32[]{:S(2)}, u32[]{:S(2)}) collective-permute-start(bf16[224,128]{1,0:T(8,128)(2,1)S(1)} %get-tuple-element.26), channel_id=1, source_target_pairs={{256,0},{288,32},{320,64},{352,96},{384,128},{416,160},{448,192},{... | collective-permute-start | bytes 172040 | tf_op jit(solution)/shard_map/ppermute | solution.py:30
  305.4 16.0 %collective-permute-start.23 = (bf16[224,128]{1,0:T(8,128)(2,1)S(1)}, bf16[224,128]{1,0:T(8,128)(2,1)S(1)}, u32[]{:S(2)}, u32[]{:S(2)}) collective-permute-start(bf16[224,128]{1,0:T(8,128)(2,1)S(1)} %get-tuple-element.27), channel_id=1, source_target_pairs={{224,0},{256,32},{288,64},{320,96},{352,128},{384,160},{416,192},{... | collective-permute-start | bytes 172040 | tf_op jit(solution)/shard_map/ppermute | solution.py:30
  307.2 15.6 %collective-permute-start.22 = (bf16[224,128]{1,0:T(8,128)(2,1)S(1)}, bf16[224,128]{1,0:T(8,128)(2,1)S(1)}, u32[]{:S(2)}, u32[]{:S(2)}) collective-permute-start(bf16[224,128]{1,0:T(8,128)(2,1)S(1)} %get-tuple-element.28), channel_id=1, source_target_pairs={{192,0},{224,32},{256,64},{288,96},{320,128},{352,160},{384,192},{... | collective-permute-start | bytes 172040 | tf_op jit(solution)/shard_map/ppermute | solution.py:30
  310.2 12.6 %collective-permute-start.21 = (bf16[224,128]{1,0:T(8,128)(2,1)S(1)}, bf16[224,128]{1,0:T(8,128)(2,1)S(1)}, u32[]{:S(2)}, u32[]{:S(2)}) collective-permute-start(bf16[224,128]{1,0:T(8,128)(2,1)S(1)} %get-tuple-element.29), channel_id=1, source_target_pairs={{160,0},{192,32},{224,64},{256,96},{288,128},{320,160},{352,192},{... | collective-permute-start | bytes 172040 | tf_op jit(solution)/shard_map/ppermute | solution.py:30
  312.4 12.3 %collective-permute-start.20 = (bf16[224,128]{1,0:T(8,128)(2,1)S(1)}, bf16[224,128]{1,0:T(8,128)(2,1)S(1)}, u32[]{:S(2)}, u32[]{:S(2)}) collective-permute-start(bf16[224,128]{1,0:T(8,128)(2,1)S(1)} %get-tuple-element.30), channel_id=1, source_target_pairs={{128,0},{160,32},{192,64},{224,96},{256,128},{288,160},{320,192},{... | collective-permute-start | bytes 172040 | tf_op jit(solution)/shard_map/ppermute | solution.py:30
  320.1 7.2 %collective-permute-start.19 = (bf16[224,128]{1,0:T(8,128)(2,1)S(1)}, bf16[224,128]{1,0:T(8,128)(2,1)S(1)}, u32[]{:S(2)}, u32[]{:S(2)}) collective-permute-start(bf16[224,128]{1,0:T(8,128)(2,1)S(1)} %get-tuple-element.31), channel_id=1, source_target_pairs={{96,0},{128,32},{160,64},{192,96},{224,128},{256,160},{288,192},{3... | collective-permute-start | bytes 172040 | tf_op jit(solution)/shard_map/ppermute | solution.py:30
  321.4 7.6 %collective-permute-start.18 = (bf16[224,128]{1,0:T(8,128)(2,1)S(1)}, bf16[224,128]{1,0:T(8,128)(2,1)S(1)}, u32[]{:S(2)}, u32[]{:S(2)}) collective-permute-start(bf16[224,128]{1,0:T(8,128)(2,1)S(1)} %get-tuple-element.32), channel_id=1, source_target_pairs={{64,0},{96,32},{128,64},{160,96},{192,128},{224,160},{256,192},{28... | collective-permute-start | bytes 172040 | tf_op jit(solution)/shard_map/ppermute | solution.py:30
  329.1 3.1 collective-permute-start.33
  339.1 49.5 %all-to-all-start.2 = ((bf16[32,2,128,128]{3,2,1,0:T(8,128)(2,1)}), bf16[32,2,128,128]{3,2,1,0:T(8,128)(2,1)}, u32[]{:S(2)}, u32[]{:S(2)}) async-start(bf16[32,2,128,128]{3,2,1,0:T(8,128)(2,1)} %bitcast.16), calls=%async_computation.3 | async-start | bytes 4194304 | tf_op jit(solution)/shard_map/all_to_all | solution.py:218
  346.4 1.3 copy-start.2
  346.4 107.8 %reduce-scatter.2.cloned.1.call-start = ((), (), s32[]{:S(2)}) async-start(), calls=%async_computation.5 | async-start | bytes 2433024 | tf_op jit(solution)/shard_map/reduce_scatter | solution.py:191
  349.9 265.2 %all-reduce.3.cloned.1.call-start = ((), (), s32[]{:S(2)}) async-start(), calls=%async_computation.6 | async-start | bytes 4194304 | tf_op jit(solution)/shard_map/psum | solution.py:223
Sparse Core Ops, SparseCore 0:
  115.3 76.6 all-gather.1
  351.7 102.4 reduce-scatter.1
  457.7 157.3 all-reduce.2
where the time goes:
time: 627 us; the launch traced here: 625 us
  waiting for transfers between devices  263 us (42%)
  blocking collectives  159 us (25%)
  starting transfers between devices  130 us (21%)
  local copies, waits for them, and re-layouts  32.1 us (5%)
  between operations  14.7 us (2%)
  matrix products  13.9 us (2%)
  other arithmetic  11.7 us (2%)
    ppermute x32, starting transfers between devices, shifted(): lax.ppermute(value, axis, [(source, source + steps) for source in range(i...  92.5 us
    psum x1, blocking collectives, body(): squares = lax.psum(jnp.sum(tokens_f32 * tokens_f32, axis=1), 'wt')  63.7 us
    psum x1, waiting for transfers between devices, body(): lax.psum(owned_grads.astype(jnp.float32).astype(jnp.bfloat16), 'seq')  62.3 us
    reduce_scatter x1, waiting for transfers between devices, body(): lax.psum_scatter((contract(w_query, query_grad) + contract(w_pair, pair_g...  61.7 us
    psum x1, blocking collectives, body(): row_dots = lax.psum(jnp.sum(scaled_grad * scaled, axis=1), 'wt')  60.5 us
    all_to_all x1, waiting for transfers between devices, body(): lax.all_to_all(outgoing[:dump_slot].reshape(groups, CAP, BLK, BLK), 'wt',...  51.3 us
    all_to_all x1, waiting for transfers between devices, body(): lax.all_to_all(slot_grads.astype(jnp.bfloat16), 'wt', split_axis=0, conca...  38.6 us
    psum x1, blocking collectives, body(): lax.psum(gain_part.astype(jnp.bfloat16), 'seq').astype(jnp.float32)  34.9 us
  transfers between devices with their start and end apart: 40, of which 20 were waited for; matrix products, arithmetic and copies ran while one was open for 6% of the time, Pallas kernels for 0%

commit v1 on v0

--- a/solution.py
+++ b/solution.py
@@ -64,15 +64,10 @@
 
 def body(tokens_in, norm_gain, positions, blocks, slot_code, out_grad):
     tok_rows = tokens_in.shape[0]
+    feat = tokens_in.shape[1]
     groups = lax.axis_size("wt")
     slab_index = lax.axis_index("seq")
     is_even = lax.axis_index("wt") % 2 == 0
-    tokens_f32 = tokens_in.astype(jnp.float32)
-    squares = lax.psum(jnp.sum(tokens_f32 * tokens_f32, axis=1), "wt")
-    inv_rms = lax.rsqrt(squares / D + norm_eps)
-    scaled = tokens_f32 * inv_rms[:, None]
-    normed_part = (scaled * norm_gain[None, :]).astype(jnp.bfloat16)
-    normed = lax.all_gather(normed_part, "wt", axis=1, tiled=True)
     pos_count = 2 * (D // BLK)
     row_blocks = pos_count // 2
     slot_codes = slot_code[0]
@@ -109,6 +104,30 @@
             tiled=True,
         ),
     )
+    gain_hi = lax.reduce_precision(norm_gain, exponent_bits=8, mantissa_bits=7)
+    gain_rest = norm_gain - gain_hi
+    gain_mid = lax.reduce_precision(gain_rest, exponent_bits=8, mantissa_bits=7)
+    gain_lo = gain_rest - gain_mid
+    gain_rows = jnp.stack([gain_hi, gain_mid, gain_lo]).astype(jnp.bfloat16)
+    side_rows = 8
+    gathered = lax.all_gather(
+        jnp.concatenate(
+            [tokens_in, gain_rows, jnp.zeros((side_rows - 3, feat), jnp.bfloat16)], axis=0
+        ),
+        "wt",
+        axis=1,
+        tiled=True,
+    )
+    tokens_full = gathered[:tok_rows]
+    gain_parts = gathered[tok_rows : tok_rows + 3].astype(jnp.float32)
+    gain_full = (gain_parts[0] + gain_parts[1]) + gain_parts[2]
+    full_f32 = tokens_full.astype(jnp.float32)
+    squares = jnp.sum(full_f32 * full_f32, axis=1)
+    inv_rms = lax.rsqrt(squares / D + norm_eps)
+    scaled_full = full_f32 * inv_rms[:, None]
+    gained_full = scaled_full * gain_full[None, :]
+    normed = gained_full.astype(jnp.bfloat16)
+    scaled = tokens_in.astype(jnp.float32) * inv_rms[:, None]
     arrival = arrived_pos.reshape(-1).astype(jnp.int32)
     arrival = jnp.where(arrival < 0, pos_count, arrival)
     weight_table = (
@@ -130,12 +149,13 @@
     value_rows = jnp.where(is_even, partner, own_pair)
     reach_slabs = lax.axis_size("seq") // 2
     window = reach_slabs * tok_rows
+    key_value = jnp.concatenate([key_rows, value_rows], axis=1)
     key_list = [key_rows]
     value_list = [value_rows]
     for offset in range(1, reach_slabs + 1):
-        prev_key, prev_value = shifted((key_rows, value_rows), "seq", offset)
-        key_list.append(prev_key)
-        value_list.append(prev_value)
+        prev = shifted(key_value, "seq", offset)
+        key_list.append(prev[:, :HD])
+        value_list.append(prev[:, HD:])
     key_all = jnp.concatenate(key_list, axis=0)
     value_all = jnp.concatenate(value_list, axis=0)
     local_index = jnp.arange(tok_rows, dtype=jnp.int32)
@@ -167,38 +187,42 @@
     key_total = key_grads[:tok_rows]
     value_total = value_grads[:tok_rows]
     for offset in range(1, reach_slabs + 1):
-        recv_key, recv_value = (
-            shifted(
+        piece = jnp.concatenate(
+            [
                 key_grads[offset * tok_rows : (offset + 1) * tok_rows].astype(jnp.bfloat16),
-                "seq",
-                -offset,
-            ).astype(jnp.float32),
-            shifted(
                 value_grads[offset * tok_rows : (offset + 1) * tok_rows].astype(jnp.bfloat16),
-                "seq",
-                -offset,
-            ).astype(jnp.float32),
+            ],
+            axis=1,
         )
-        key_total = key_total + recv_key
-        value_total = value_total + recv_value
+        recv = shifted(piece, "seq", -offset).astype(jnp.float32)
+        key_total = key_total + recv[:, :HD]
+        value_total = value_total + recv[:, HD:]
     outbound = jnp.where(is_even, value_total, key_total)
     partner_grad = from_partner(outbound.astype(jnp.bfloat16), "wt", 0).astype(outbound.dtype)
     pair_total = jnp.where(is_even, key_total, value_total) + partner_grad
     pair_grad = jnp.where(is_even, rotate(pair_total, cos_table, -sin_table), pair_total).astype(
         jnp.bfloat16
     )
-    normed_grad = (
-        lax.psum_scatter(
-            (contract(w_query, query_grad) + contract(w_pair, pair_grad)).astype(jnp.bfloat16),
-            "wt",
-            scatter_dimension=0,
-            tiled=True,
-        )
-        .astype(jnp.float32)
-        .T
-    )
+    contribution = contract(w_query, query_grad) + contract(w_pair, pair_grad)
+    row_part = jnp.sum(contribution * gained_full.T, axis=0)
+    row_top = lax.reduce_precision(row_part, exponent_bits=8, mantissa_bits=7)
+    row_hi = row_top.astype(jnp.bfloat16)
+    row_lo = (row_part - row_top).astype(jnp.bfloat16)
+    pad_rows = 16
+    extra_rows = jnp.concatenate(
+        [row_hi[None], row_lo[None], jnp.zeros((pad_rows - 2, tok_rows), jnp.bfloat16)], axis=0
+    )
+    packed = jnp.concatenate(
+        [
+            contribution.astype(jnp.bfloat16).reshape(groups, feat, tok_rows),
+            jnp.broadcast_to(extra_rows[None], (groups, pad_rows, tok_rows)),
+        ],
+        axis=1,
+    ).reshape(groups * (feat + pad_rows), tok_rows)
+    scattered = lax.psum_scatter(packed, "wt", scatter_dimension=0, tiled=True)
+    normed_grad = scattered[:feat].astype(jnp.float32).T
+    row_dots = scattered[feat].astype(jnp.float32) + scattered[feat + 1].astype(jnp.float32)
     scaled_grad = normed_grad * norm_gain[None, :]
-    row_dots = lax.psum(jnp.sum(scaled_grad * scaled, axis=1), "wt")
     tokens_grad = (inv_rms[:, None] * (scaled_grad - scaled * (row_dots / D)[:, None])).astype(
         jnp.bfloat16
     )
@@ -219,12 +243,10 @@
         slot_grads.astype(jnp.bfloat16), "wt", split_axis=0, concat_axis=0, tiled=True
     )
     owned_grads = jnp.concatenate([returned.reshape(-1, BLK, BLK), empty_block], axis=0)[slot_dest]
-    summed = (
-        lax.psum(owned_grads.astype(jnp.float32).astype(jnp.bfloat16), "seq").astype(jnp.float32),
-        lax.psum(gain_part.astype(jnp.bfloat16), "seq").astype(jnp.float32),
-    )
-    block_grads = summed[0].astype(jnp.bfloat16)
-    gain_total = summed[1]
+    gain_block = jnp.pad(gain_part.astype(jnp.bfloat16), (0, BLK * BLK - feat)).reshape(1, BLK, BLK)
+    summed = lax.psum(jnp.concatenate([owned_grads, gain_block], axis=0), "seq")
+    block_grads = summed[:-1]
+    gain_total = summed[-1].reshape(-1)[:feat].astype(jnp.float32)
     return (attn_rows, tokens_grad, gain_total, block_grads[None])
 
 

time: 627 us -> 539 us (0.86)
  blocking collectives: 159 us -> 0 us
  waiting for transfers between devices: 263 us -> 379 us
  starting transfers between devices: 130 us -> 68.9 us
  other arithmetic: 11.7 us -> 19.7 us
  local copies, waits for them, and re-layouts: 32.1 us -> 39.1 us
    psum x3 -> x0, blocking collectives: 159 us -> none  [the longest x1 63.7 us: body(): squares = lax.psum(jnp.sum(tokens_f32 * tokens_f32, axis=1), 'wt')]
    psum x1, waiting for transfers between devices: 62.3 us -> 158 us  [body(): summed = lax.psum(jnp.concatenate([owned_grads, gain_block], axis=0), 'seq')]
    ppermute x32 -> x16, starting transfers between devices: 92.5 us -> 36.8 us  [shifted(): lax.ppermute(value, axis, [(source, source + steps) for source in range(i...]
    reduce_scatter x1, waiting for transfers between devices: 61.7 us -> 109 us  [body(): scattered = lax.psum_scatter(packed, 'wt', scatter_dimension=0, tiled=True)]
    all_to_all x1, waiting for transfers between devices: 38.6 us -> 0.01 us  [body(): lax.all_to_all(slot_grads.astype(jnp.bfloat16), 'wt', split_axis=0, conca...]
    ppermute x32 -> x16, waiting for transfers between devices: 30.3 us -> 44.5 us  [shifted(): lax.ppermute(value, axis, [(source, source + steps) for source in range(i...]
  transfers between devices with their start and end apart: 40 -> 24, of which waited for: 20 -> 13; matrix products, arithmetic and copies ran while one was open for 6% -> 7% of each run, Pallas kernels for 0% -> 0%
where the time goes in v1:
time: 539 us; the launch traced here: 537 us
  waiting for transfers between devices  379 us (70%)
  starting transfers between devices  68.9 us (13%)
  local copies, waits for them, and re-layouts  39.1 us (7%)
  other arithmetic  19.7 us (4%)
  matrix products  16.3 us (3%)
  between operations  14.6 us (3%)
    psum x1, waiting for transfers between devices, body(): summed = lax.psum(jnp.concatenate([owned_grads, gain_block], axis=0), 'seq')  158 us
    reduce_scatter x1, waiting for transfers between devices, body(): scattered = lax.psum_scatter(packed, 'wt', scatter_dimension=0, tiled=True)  109 us
    all_to_all x1, waiting for transfers between devices, body(): lax.all_to_all(outgoing[:dump_slot].reshape(groups, CAP, BLK, BLK), 'wt',...  50.9 us
    ppermute x16, waiting for transfers between devices, shifted(): lax.ppermute(value, axis, [(source, source + steps) for source in range(i...  44.5 us
    ppermute x16, starting transfers between devices, shifted(): lax.ppermute(value, axis, [(source, source + steps) for source in range(i...  36.8 us
    all_gather x1, waiting for transfers between devices, body(): lax.all_gather(jnp.concatenate([tokens_in, gain_rows, jnp.zeros((side_row...  15.7 us
  transfers between devices with their start and end apart: 24, of which 13 were waited for; matrix products, arithmetic and copies ran while one was open for 7% of the time, Pallas kernels for 0%

profile of v1, /device:TPU:6, one launch (start us, length us, event | category | flops | bytes accessed | tf_op | source)
XLA Modules:
  0.0 537.5 jit_solution(3917345095816928907)
XLA Ops:
  9.5 0.8 scatter_custom_fusion
  10.3 0.7 all_to_all.16
  11.1 10.2 %all-to-all-start = ((bf16[32,1,2]{2,1,0:T(2,128)(2,1)}), bf16[32,1,2]{2,1,0:T(2,128)(2,1)S(1)}, u32[]{:S(2)}, u32[]{:S(2)}) async-start(bf16[32,1,2]{2,1,0:T(2,128)(2,1)} %all_to_all.16), calls=%async_computation | async-start | bytes 32768 | tf_op jit(solution)/shard_map/all_to_all | solution.py:99
  21.8 6.6 %scatter_fusion = bf16[65,128,128]{2,1,0:T(8,128)(2,1)S(1)} fusion(bf16[65,128,128]{2,1,0:T(8,128)(2,1)S(1)} %broadcast_in_dim.31, s32[64]{0:T(128)S(1)} %fusion.59, bf16[64,128,128]{2,1,0:T(8,128)(2,1)} %bitcast.123), kind=kCustom, calls=%fused_computation.3 | custom fusion | bytes 6291712 | tf_op jit(solution)/shard_map/scatter | solution.py:84
  28.5 1.5 slice.317
  30.0 9.9 %all-to-all-start.1 = ((bf16[32,2,128,128]{3,2,1,0:T(8,128)(2,1)}), bf16[32,2,128,128]{3,2,1,0:T(8,128)(2,1)S(1)}, u32[]{:S(2)}, u32[]{:S(2)}) async-start(bf16[32,2,128,128]{3,2,1,0:T(8,128)(2,1)} %bitcast.118), calls=%async_computation.1 | async-start | bytes 4194304 | tf_op jit(solution)/shard_map/all_to_all | solution.py:92
  40.3 0.8 concatenate.68
  41.6 50.9 %all-to-all-done.1 = bf16[32,2,128,128]{3,2,1,0:T(8,128)(2,1)S(1)} async-done(((bf16[32,2,128,128]{3,2,1,0:T(8,128)(2,1)}), bf16[32,2,128,128]{3,2,1,0:T(8,128)(2,1)S(1)}, u32[]{:S(2)}, u32[]{:S(2)}) %all-to-all-start.1) | async-done | bytes 2097184 | tf_op jit(solution)/shard_map/all_to_all | solution.py:92
  92.5 1.3 copy-done.1
  94.4 6.7 %scatter_fusion.1 = bf16[73,128,128]{2,1,0:T(8,128)(2,1)S(1)} fusion(bf16[73,128,128]{2,1,0:T(8,128)(2,1)S(1)} %broadcast_in_dim.28, s32[64]{0:T(128)S(1)} %fusion.60, bf16[64,128,128]{2,1,0:T(8,128)(2,1)} %bitcast.117), kind=kCustom, calls=%fused_computation.4 | custom fusion | bytes 6291712 | tf_op jit(solution)/shard_map/scatter | solution.py:136
  101.1 1.6 fusion.77
  102.7 15.7 %all-gather.2.cloned.1.call-done = bf16[232,4608]{0,1:T(8,128)(2,1)} async-done(((bf16[232,144]{0,1:T(8,128)(2,1)}), bf16[232,4608]{0,1:T(8,128)(2,1)}) %all-gather.2.cloned.1.call-update) | async-done | bytes 2138128 | tf_op jit(solution)/shard_map/all_gather | solution.py:113
  118.4 2.8 copy.23
  121.7 1.6 slice_convert_fusion
  123.4 2.2 fusion.11
  125.6 0.8 fusion.70
  127.0 2.1 collective-permute-start
  129.1 0.8 fusion.72
  130.2 3.8 collective-permute-start.1
  134.6 3.6 collective-permute-start.2
  138.1 4.2 collective-permute-start.3
  142.4 4.9 collective-permute-start.4
  147.3 4.1 collective-permute-start.5
  151.5 1.3 collective-permute-start.6
  152.8 1.8 collective-permute-start.7
  154.7 2.8 collective-permute-start.8
  157.5 5.8 %collective-permute-done.4 = bf16[224,256]{1,0:T(8,128)(2,1)S(1)} collective-permute-done((bf16[224,256]{1,0:T(8,128)(2,1)S(1)}, bf16[224,256]{1,0:T(8,128)(2,1)S(1)}, u32[]{:S(2)}, u32[]{:S(2)}) %collective-permute-start.4) | collective-permute-done | bytes 114720 | tf_op jit(solution)/shard_map/ppermute | solution.py:30
  163.4 2.4 collective-permute-done.6
  165.9 2.0 collective-permute-done.8
  167.8 1.1 fusion.74
  168.9 1.0 fusion.80
  170.0 1.4 multiply_reduce_fusion
  171.4 1.1 fusion.10
  173.5 1.3 collective-permute-start.9
  174.9 1.3 collective-permute-start.10
  176.2 1.3 collective-permute-start.11
  177.5 1.3 collective-permute-start.12
  178.8 1.3 collective-permute-start.13
  180.8 1.3 collective-permute-start.14
  182.1 5.0 collective-permute-done.10
  187.1 1.3 collective-permute-start.15
  188.4 1.8 collective-permute-done.11
  190.3 1.3 collective-permute-start.16
  191.5 2.6 fusion.83
  194.2 16.6 %collective-permute-done.12 = bf16[224,256]{1,0:T(8,128)(2,1)S(1)} collective-permute-done((bf16[224,256]{1,0:T(8,128)(2,1)S(1)}, bf16[224,256]{1,0:T(8,128)(2,1)S(1)}, u32[]{:S(2)}, u32[]{:S(2)}) %collective-permute-start.12) | collective-permute-done | bytes 114720 | tf_op jit(solution)/shard_map/ppermute | solution.py:30
  210.9 10.8 %collective-permute-done.14 = bf16[224,256]{1,0:T(8,128)(2,1)S(1)} collective-permute-done((bf16[224,256]{1,0:T(8,128)(2,1)S(1)}, bf16[224,256]{1,0:T(8,128)(2,1)S(1)}, u32[]{:S(2)}, u32[]{:S(2)}) %collective-permute-start.14) | collective-permute-done | bytes 114720 | tf_op jit(solution)/shard_map/ppermute | solution.py:30
  221.9 1.9 collective-permute-start.17
  223.9 0.9 fusion.68
  225.7 0.9 fusion.66
  226.6 1.7 maximum_maximum_fusion
  228.4 3.8 gather_fusion
  232.2 7.5 %all-to-all-start.2 = ((bf16[32,2,128,128]{3,2,1,0:T(8,128)(2,1)}), bf16[32,2,128,128]{3,2,1,0:T(8,128)(2,1)}, u32[]{:S(2)}, u32[]{:S(2)}) async-start(bf16[32,2,128,128]{3,2,1,0:T(8,128)(2,1)} %bitcast.119), calls=%async_computation.3 | async-start | bytes 4194304 | tf_op jit(solution)/shard_map/all_to_all | solution.py:242
  240.0 4.7 fusion.76
  244.6 2.8 copy.22
  247.5 2.0 pad_maximum_fusion
  249.6 109.4 %reduce-scatter.2.cloned.1.call-done = bf16[160,224]{1,0:T(8,128)(2,1)} async-done(((bf16[5120,224]{1,0:T(8,128)(2,1)}), bf16[160,224]{1,0:T(8,128)(2,1)}) %reduce-scatter.2.cloned.1.call-update) | async-done | bytes 71696 | tf_op jit(solution)/shard_map/reduce_scatter | solution.py:222
  359.0 0.8 fusion.56
  359.8 1.7 fusion.38
  361.5 1.8 concatenate.87
  363.3 2.1 gather_fusion.1
  365.4 3.1 pad_maximum_fusion.1
  368.5 157.9 %all-reduce.4.cloned.1.call-done = bf16[65,128,128]{2,1,0:T(8,128)(2,1)} async-done(((bf16[65,128,128]{2,1,0:T(8,128)(2,1)}), bf16[65,128,128]{2,1,0:T(8,128)(2,1)}) %all-reduce.4.cloned.1.call-update) | async-done | bytes 2129936 | tf_op jit(solution)/shard_map/psum | solution.py:247
  526.5 0.8 slice_bitcast_fusion.1
  527.8 3.2 slice_bitcast_fusion
  (109 shorter events, 10.3 us)
Async XLA Ops:
  11.1 18.9 %all-to-all-start = ((bf16[32,1,2]{2,1,0:T(2,128)(2,1)}), bf16[32,1,2]{2,1,0:T(2,128)(2,1)S(1)}, u32[]{:S(2)}, u32[]{:S(2)}) async-start(bf16[32,1,2]{2,1,0:T(2,128)(2,1)} %all_to_all.16), calls=%async_computation | async-start | bytes 32768 | tf_op jit(solution)/shard_map/all_to_all | solution.py:99
  29.9 10.0 %copy-start.4 = (f32[144]{0:T(256)S(1)}, f32[144]{0:T(256)}, u32[]{:S(2)}) copy-start(f32[144]{0:T(256)} %param.7) | copy-start | bytes 1732
  29.9 10.3 %copy-start.3 = (bf16[224,144]{0,1:T(8,128)(2,1)S(1)}, bf16[224,144]{0,1:T(8,128)(2,1)}, u32[]{:S(2)}) copy-start(bf16[224,144]{0,1:T(8,128)(2,1)} %param.6) | copy-start | bytes 193540
  29.9 11.4 %copy-start.5 = (s32[224]{0:T(256)S(1)}, s32[224]{0:T(256)}, u32[]{:S(2)}) copy-start(s32[224]{0:T(256)} %param.8) | copy-start | bytes 2692
  30.0 62.6 %all-to-all-start.1 = ((bf16[32,2,128,128]{3,2,1,0:T(8,128)(2,1)}), bf16[32,2,128,128]{3,2,1,0:T(8,128)(2,1)S(1)}, u32[]{:S(2)}, u32[]{:S(2)}) async-start(bf16[32,2,128,128]{3,2,1,0:T(8,128)(2,1)} %bitcast.118), calls=%async_computation.1 | async-start | bytes 4194304 | tf_op jit(solution)/shard_map/all_to_all | solution.py:92
  39.9 78.5 %all-gather.2.cloned.1.call-start = ((), (), s32[]{:S(2)}) async-start(), calls=%async_computation.4 | async-start | bytes 2433024 | tf_op jit(solution)/shard_map/all_gather | solution.py:113
  92.5 1.3 copy-start.1
  123.4 2.2 copy-start.2
  125.6 3.6 copy-start
  127.0 3.1 collective-permute-start
  130.2 21.3 %collective-permute-start.1 = (bf16[224,256]{1,0:T(8,128)(2,1)S(1)}, bf16[224,256]{1,0:T(8,128)(2,1)S(1)}, u32[]{:S(2)}, u32[]{:S(2)}) collective-permute-start(bf16[224,256]{1,0:T(8,128)(2,1)S(1)} %pad_maximum_fusion.2), channel_id=1, source_target_pairs={{0,32},{32,64},{64,96},{96,128},{128,160},{160,192},{192,224},{224... | collective-permute-start | bytes 344072 | tf_op jit(solution)/shard_map/ppermute | solution.py:30
  134.6 18.2 %collective-permute-start.2 = (bf16[224,256]{1,0:T(8,128)(2,1)S(1)}, bf16[224,256]{1,0:T(8,128)(2,1)S(1)}, u32[]{:S(2)}, u32[]{:S(2)}) collective-permute-start(bf16[224,256]{1,0:T(8,128)(2,1)S(1)} %pad_maximum_fusion.2), channel_id=1, source_target_pairs={{0,64},{32,96},{64,128},{96,160},{128,192},{160,224},{192,256},{22... | collective-permute-start | bytes 344072 | tf_op jit(solution)/shard_map/ppermute | solution.py:30
  138.1 16.5 %collective-permute-start.3 = (bf16[224,256]{1,0:T(8,128)(2,1)S(1)}, bf16[224,256]{1,0:T(8,128)(2,1)S(1)}, u32[]{:S(2)}, u32[]{:S(2)}) collective-permute-start(bf16[224,256]{1,0:T(8,128)(2,1)S(1)} %pad_maximum_fusion.2), channel_id=1, source_target_pairs={{0,96},{32,128},{64,160},{96,192},{128,224},{160,256},{192,288},{2... | collective-permute-start | bytes 344072 | tf_op jit(solution)/shard_map/ppermute | solution.py:30
  142.4 20.9 %collective-permute-start.4 = (bf16[224,256]{1,0:T(8,128)(2,1)S(1)}, bf16[224,256]{1,0:T(8,128)(2,1)S(1)}, u32[]{:S(2)}, u32[]{:S(2)}) collective-permute-start(bf16[224,256]{1,0:T(8,128)(2,1)S(1)} %pad_maximum_fusion.2), channel_id=1, source_target_pairs={{0,128},{32,160},{64,192},{96,224},{128,256},{160,288},{192,320},{... | collective-permute-start | bytes 344072 | tf_op jit(solution)/shard_map/ppermute | solution.py:30
  147.3 16.0 %collective-permute-start.5 = (bf16[224,256]{1,0:T(8,128)(2,1)S(1)}, bf16[224,256]{1,0:T(8,128)(2,1)S(1)}, u32[]{:S(2)}, u32[]{:S(2)}) collective-permute-start(bf16[224,256]{1,0:T(8,128)(2,1)S(1)} %pad_maximum_fusion.2), channel_id=1, source_target_pairs={{0,160},{32,192},{64,224},{96,256},{128,288},{160,320},{192,352},{... | collective-permute-start | bytes 344072 | tf_op jit(solution)/shard_map/ppermute | solution.py:30
  151.5 14.3 %collective-permute-start.6 = (bf16[224,256]{1,0:T(8,128)(2,1)S(1)}, bf16[224,256]{1,0:T(8,128)(2,1)S(1)}, u32[]{:S(2)}, u32[]{:S(2)}) collective-permute-start(bf16[224,256]{1,0:T(8,128)(2,1)S(1)} %pad_maximum_fusion.2), channel_id=1, source_target_pairs={{0,192},{32,224},{64,256},{96,288},{128,320},{160,352},{192,384},{... | collective-permute-start | bytes 344072 | tf_op jit(solution)/shard_map/ppermute | solution.py:30
  152.8 13.0 %collective-permute-start.7 = (bf16[224,256]{1,0:T(8,128)(2,1)S(1)}, bf16[224,256]{1,0:T(8,128)(2,1)S(1)}, u32[]{:S(2)}, u32[]{:S(2)}) collective-permute-start(bf16[224,256]{1,0:T(8,128)(2,1)S(1)} %pad_maximum_fusion.2), channel_id=1, source_target_pairs={{0,224},{32,256},{64,288},{96,320},{128,352},{160,384},{192,416},{... | collective-permute-start | bytes 344072 | tf_op jit(solution)/shard_map/ppermute | solution.py:30
  154.7 13.1 %collective-permute-start.8 = (bf16[224,256]{1,0:T(8,128)(2,1)S(1)}, bf16[224,256]{1,0:T(8,128)(2,1)S(1)}, u32[]{:S(2)}, u32[]{:S(2)}) collective-permute-start(bf16[224,256]{1,0:T(8,128)(2,1)S(1)} %pad_maximum_fusion.2), channel_id=1, source_target_pairs={{0,256},{32,288},{64,320},{96,352},{128,384},{160,416},{192,448},{... | collective-permute-start | bytes 344072 | tf_op jit(solution)/shard_map/ppermute | solution.py:30
  167.8 1.1 copy-start.6
  173.5 7.3 %collective-permute-start.9 = (bf16[224,256]{1,0:T(8,128)(2,1)S(1)}, bf16[224,256]{1,0:T(8,128)(2,1)S(1)}, u32[]{:S(2)}, u32[]{:S(2)}) collective-permute-start(bf16[224,256]{1,0:T(8,128)(2,1)S(1)} %pad_maximum_fusion.3), channel_id=1, source_target_pairs={{32,0},{64,32},{96,64},{128,96},{160,128},{192,160},{224,192},{256... | collective-permute-start | bytes 344072 | tf_op jit(solution)/shard_map/ppermute | solution.py:30
  174.9 12.3 %collective-permute-start.10 = (bf16[224,256]{1,0:T(8,128)(2,1)S(1)}, bf16[224,256]{1,0:T(8,128)(2,1)S(1)}, u32[]{:S(2)}, u32[]{:S(2)}) collective-permute-start(bf16[224,256]{1,0:T(8,128)(2,1)S(1)} %pad_maximum_fusion.4), channel_id=1, source_target_pairs={{64,0},{96,32},{128,64},{160,96},{192,128},{224,160},{256,192},{28... | collective-permute-start | bytes 344072 | tf_op jit(solution)/shard_map/ppermute | solution.py:30
  176.2 14.1 %collective-permute-start.11 = (bf16[224,256]{1,0:T(8,128)(2,1)S(1)}, bf16[224,256]{1,0:T(8,128)(2,1)S(1)}, u32[]{:S(2)}, u32[]{:S(2)}) collective-permute-start(bf16[224,256]{1,0:T(8,128)(2,1)S(1)} %pad_maximum_fusion.5), channel_id=1, source_target_pairs={{96,0},{128,32},{160,64},{192,96},{224,128},{256,160},{288,192},{3... | collective-permute-start | bytes 344072 | tf_op jit(solution)/shard_map/ppermute | solution.py:30
  177.5 33.4 %collective-permute-start.12 = (bf16[224,256]{1,0:T(8,128)(2,1)S(1)}, bf16[224,256]{1,0:T(8,128)(2,1)S(1)}, u32[]{:S(2)}, u32[]{:S(2)}) collective-permute-start(bf16[224,256]{1,0:T(8,128)(2,1)S(1)} %pad_maximum_fusion.6), channel_id=1, source_target_pairs={{128,0},{160,32},{192,64},{224,96},{256,128},{288,160},{320,192},{... | collective-permute-start | bytes 344072 | tf_op jit(solution)/shard_map/ppermute | solution.py:30
  178.8 32.1 %collective-permute-start.13 = (bf16[224,256]{1,0:T(8,128)(2,1)S(1)}, bf16[224,256]{1,0:T(8,128)(2,1)S(1)}, u32[]{:S(2)}, u32[]{:S(2)}) collective-permute-start(bf16[224,256]{1,0:T(8,128)(2,1)S(1)} %pad_maximum_fusion.7), channel_id=1, source_target_pairs={{160,0},{192,32},{224,64},{256,96},{288,128},{320,160},{352,192},{... | collective-permute-start | bytes 344072 | tf_op jit(solution)/shard_map/ppermute | solution.py:30
  180.8 40.9 %collective-permute-start.14 = (bf16[224,256]{1,0:T(8,128)(2,1)S(1)}, bf16[224,256]{1,0:T(8,128)(2,1)S(1)}, u32[]{:S(2)}, u32[]{:S(2)}) collective-permute-start(bf16[224,256]{1,0:T(8,128)(2,1)S(1)} %pad_maximum_fusion.8), channel_id=1, source_target_pairs={{192,0},{224,32},{256,64},{288,96},{320,128},{352,160},{384,192},{... | collective-permute-start | bytes 344072 | tf_op jit(solution)/shard_map/ppermute | solution.py:30
  187.1 34.6 %collective-permute-start.15 = (bf16[224,256]{1,0:T(8,128)(2,1)S(1)}, bf16[224,256]{1,0:T(8,128)(2,1)S(1)}, u32[]{:S(2)}, u32[]{:S(2)}) collective-permute-start(bf16[224,256]{1,0:T(8,128)(2,1)S(1)} %pad_maximum_fusion.9), channel_id=1, source_target_pairs={{224,0},{256,32},{288,64},{320,96},{352,128},{384,160},{416,192},{... | collective-permute-start | bytes 344072 | tf_op jit(solution)/shard_map/ppermute | solution.py:30
  190.3 31.5 %collective-permute-start.16 = (bf16[224,256]{1,0:T(8,128)(2,1)S(1)}, bf16[224,256]{1,0:T(8,128)(2,1)S(1)}, u32[]{:S(2)}, u32[]{:S(2)}) collective-permute-start(bf16[224,256]{1,0:T(8,128)(2,1)S(1)} %pad_maximum_fusion.10), channel_id=1, source_target_pairs={{256,0},{288,32},{320,64},{352,96},{384,128},{416,160},{448,192},{... | collective-permute-start | bytes 344072 | tf_op jit(solution)/shard_map/ppermute | solution.py:30
  221.9 3.1 collective-permute-start.17
  232.2 129.3 %all-to-all-start.2 = ((bf16[32,2,128,128]{3,2,1,0:T(8,128)(2,1)}), bf16[32,2,128,128]{3,2,1,0:T(8,128)(2,1)}, u32[]{:S(2)}, u32[]{:S(2)}) async-start(bf16[32,2,128,128]{3,2,1,0:T(8,128)(2,1)} %bitcast.119), calls=%async_computation.3 | async-start | bytes 4194304 | tf_op jit(solution)/shard_map/all_to_all | solution.py:242
  239.7 119.4 %reduce-scatter.2.cloned.1.call-start = ((), (), s32[]{:S(2)}) async-start(), calls=%async_computation.5 | async-start | bytes 2703360 | tf_op jit(solution)/shard_map/reduce_scatter | solution.py:222
  249.5 276.9 %all-reduce.4.cloned.1.call-start = ((), (), s32[]{:S(2)}) async-start(), calls=%async_computation.6 | async-start | bytes 4259840 | tf_op jit(solution)/shard_map/psum | solution.py:247
Sparse Core Ops, SparseCore 0:
  44.4 73.9 all-gather.1
  249.7 109.3 reduce-scatter.1
  368.6 157.7 all-reduce.3

commit v2 on v1

--- a/solution.py
+++ b/solution.py
@@ -219,7 +219,16 @@
         ],
         axis=1,
     ).reshape(groups * (feat + pad_rows), tok_rows)
-    scattered = lax.psum_scatter(packed, "wt", scatter_dimension=0, tiled=True)
+    scattered = jnp.sum(
+        lax.all_to_all(
+            packed.reshape(groups, feat + pad_rows, tok_rows),
+            "wt",
+            split_axis=0,
+            concat_axis=0,
+            tiled=True,
+        ).astype(jnp.float32),
+        axis=0,
+    )
     normed_grad = scattered[:feat].astype(jnp.float32).T
     row_dots = scattered[feat].astype(jnp.float32) + scattered[feat + 1].astype(jnp.float32)
     scaled_grad = normed_grad * norm_gain[None, :]
@@ -243,10 +252,31 @@
         slot_grads.astype(jnp.bfloat16), "wt", split_axis=0, concat_axis=0, tiled=True
     )
     owned_grads = jnp.concatenate([returned.reshape(-1, BLK, BLK), empty_block], axis=0)[slot_dest]
-    gain_block = jnp.pad(gain_part.astype(jnp.bfloat16), (0, BLK * BLK - feat)).reshape(1, BLK, BLK)
-    summed = lax.psum(jnp.concatenate([owned_grads, gain_block], axis=0), "seq")
-    block_grads = summed[:-1]
-    gain_total = summed[-1].reshape(-1)[:feat].astype(jnp.float32)
+    n_seq = lax.axis_size("seq")
+    slots = owned_grads.shape[0]
+    chunk = slots * BLK * BLK // n_seq
+    gain_width = -(-feat // 128) * 128
+    gain_row = jnp.pad(gain_part.astype(jnp.bfloat16), (0, gain_width - feat))
+    to_reduce = jnp.concatenate(
+        [
+            owned_grads.reshape(n_seq, chunk),
+            jnp.broadcast_to(gain_row[None], (n_seq, gain_width)),
+        ],
+        axis=1,
+    )
+    reduced = jnp.sum(
+        lax.all_to_all(to_reduce, "seq", split_axis=0, concat_axis=0, tiled=True).astype(
+            jnp.float32
+        ),
+        axis=0,
+    )
+    block_grads = lax.all_gather(
+        reduced[:chunk].astype(jnp.bfloat16).reshape(slots // n_seq, BLK, BLK),
+        "seq",
+        axis=0,
+        tiled=True,
+    )
+    gain_total = reduced[chunk : chunk + feat]
     return (attn_rows, tokens_grad, gain_total, block_grads[None])
 
 

time: 539 us -> 537 us (level)
  waiting for transfers between devices: 379 us -> 280 us
  blocking collectives: 0 us -> 66.6 us
  local copies, waits for them, and re-layouts: 39.1 us -> 58 us
  other arithmetic: 19.7 us -> 27.6 us
  starting transfers between devices: 68.9 us -> 75.2 us
    psum x1 -> x0, waiting for transfers between devices: 158 us -> none  [body(): summed = lax.psum(jnp.concatenate([owned_grads, gain_block], axis=0), 'seq')]
    reduce_scatter x1 -> x0, waiting for transfers between devices: 109 us -> none  [body(): scattered = lax.psum_scatter(packed, 'wt', scatter_dimension=0, tiled=True)]
    all_gather x0 -> x1, waiting for transfers between devices: none -> 75.9 us  [body(): lax.all_gather(reduced[:chunk].astype(jnp.bfloat16).reshape(slots // n_se...]
    all_to_all x0 -> x1, blocking collectives: none -> 66.6 us  [body(): lax.all_to_all(to_reduce, 'seq', split_axis=0, concat_axis=0, tiled=True)]
    all_to_all x0 -> x1, waiting for transfers between devices: none -> 50.4 us  [body(): lax.all_to_all(packed.reshape(groups, feat + pad_rows, tok_rows), 'wt', s...]
    all_to_all x1, waiting for transfers between devices: 0.01 us -> 39.8 us  [body(): lax.all_to_all(slot_grads.astype(jnp.bfloat16), 'wt', split_axis=0, conca...]
    unnamed x22 -> x29, local copies, waits for them, and re-layouts: 4.29 us -> 19.3 us
    reduce_sum x0 -> x2, other arithmetic: none -> 7.57 us  [the longest x1 7.13 us: body(): jnp.sum(lax.all_to_all(to_reduce, 'seq', split_axis=0, concat_axis=0, til...]
  transfers between devices with their start and end apart: 24 -> 24, of which waited for: 13 -> 14; matrix products, arithmetic and copies ran while one was open for 7% -> 8% of each run, Pallas kernels for 0% -> 0%
where the time goes in v2:
time: 537 us; the launch traced here: 535 us
  waiting for transfers between devices  280 us (52%)
  starting transfers between devices  75.2 us (14%)
  blocking collectives  66.6 us (12%)
  local copies, waits for them, and re-layouts  58 us (11%)
  other arithmetic  27.6 us (5%)
  between operations  14.9 us (3%)
  matrix products  12.2 us (2%)
    all_gather x1, waiting for transfers between devices, body(): lax.all_gather(reduced[:chunk].astype(jnp.bfloat16).reshape(slots // n_se...  75.9 us
    all_to_all x1, blocking collectives, body(): lax.all_to_all(to_reduce, 'seq', split_axis=0, concat_axis=0, tiled=True)  66.6 us
    all_to_all x1, waiting for transfers between devices, body(): lax.all_to_all(outgoing[:dump_slot].reshape(groups, CAP, BLK, BLK), 'wt',...  51 us
    all_to_all x1, waiting for transfers between devices, body(): lax.all_to_all(packed.reshape(groups, feat + pad_rows, tok_rows), 'wt', s...  50.4 us
    ppermute x16, waiting for transfers between devices, shifted(): lax.ppermute(value, axis, [(source, source + steps) for source in range(i...  47.1 us
    all_to_all x1, waiting for transfers between devices, body(): lax.all_to_all(slot_grads.astype(jnp.bfloat16), 'wt', split_axis=0, conca...  39.8 us
    ppermute x16, starting transfers between devices, shifted(): lax.ppermute(value, axis, [(source, source + steps) for source in range(i...  36.8 us
    unnamed x29, local copies, waits for them, and re-layouts  19.3 us
  transfers between devices with their start and end apart: 24, of which 14 were waited for; matrix products, arithmetic and copies ran while one was open for 8% of the time, Pallas kernels for 0%

profile of v2, /device:TPU:6, one launch (start us, length us, event | category | flops | bytes accessed | tf_op | source)
XLA Modules:
  0.0 535.0 jit_solution(13940885404350819155)
XLA Ops:
  11.1 10.2 %all-to-all-start = ((bf16[32,1,2]{2,1,0:T(2,128)(2,1)}), bf16[32,1,2]{2,1,0:T(2,128)(2,1)S(1)}, u32[]{:S(2)}, u32[]{:S(2)}) async-start(bf16[32,1,2]{2,1,0:T(2,128)(2,1)} %all_to_all.28), calls=%async_computation | async-start | bytes 32768 | tf_op jit(solution)/shard_map/all_to_all | solution.py:99
  21.8 6.6 %scatter_fusion = bf16[65,128,128]{2,1,0:T(8,128)(2,1)S(1)} fusion(bf16[65,128,128]{2,1,0:T(8,128)(2,1)S(1)} %broadcast_in_dim.33, s32[64]{0:T(128)S(1)} %fusion.55, bf16[64,128,128]{2,1,0:T(8,128)(2,1)} %bitcast.114), kind=kCustom, calls=%fused_computation.3 | custom fusion | bytes 6291712 | tf_op jit(solution)/shard_map/scatter | solution.py:84
  28.5 1.5 slice.314
  29.9 9.9 %all-to-all-start.1 = ((bf16[32,2,128,128]{3,2,1,0:T(8,128)(2,1)}), bf16[32,2,128,128]{3,2,1,0:T(8,128)(2,1)S(1)}, u32[]{:S(2)}, u32[]{:S(2)}) async-start(bf16[32,2,128,128]{3,2,1,0:T(8,128)(2,1)} %bitcast.109), calls=%async_computation.1 | async-start | bytes 4194304 | tf_op jit(solution)/shard_map/all_to_all | solution.py:92
  41.5 51.0 %all-to-all-done.1 = bf16[32,2,128,128]{3,2,1,0:T(8,128)(2,1)S(1)} async-done(((bf16[32,2,128,128]{3,2,1,0:T(8,128)(2,1)}), bf16[32,2,128,128]{3,2,1,0:T(8,128)(2,1)S(1)}, u32[]{:S(2)}, u32[]{:S(2)}) %all-to-all-start.1) | async-done | bytes 2097184 | tf_op jit(solution)/shard_map/all_to_all | solution.py:92
  92.5 1.3 copy-done.1
  94.4 6.6 %scatter_fusion.1 = bf16[73,128,128]{2,1,0:T(8,128)(2,1)S(1)} fusion(bf16[73,128,128]{2,1,0:T(8,128)(2,1)S(1)} %broadcast_in_dim.30, s32[64]{0:T(128)S(1)} %fusion.56, bf16[64,128,128]{2,1,0:T(8,128)(2,1)} %bitcast.108), kind=kCustom, calls=%fused_computation.4 | custom fusion | bytes 6291712 | tf_op jit(solution)/shard_map/scatter | solution.py:136
  101.1 1.6 fusion.73
  102.7 15.7 %all-gather.3.cloned.1.call-done = bf16[232,4608]{0,1:T(8,128)(2,1)} async-done(((bf16[232,144]{0,1:T(8,128)(2,1)}), bf16[232,4608]{0,1:T(8,128)(2,1)}) %all-gather.3.cloned.1.call-update) | async-done | bytes 2138128 | tf_op jit(solution)/shard_map/all_gather | solution.py:113
  118.4 2.8 copy.23
  121.7 1.6 slice_convert_fusion
  123.4 2.2 fusion.11
  125.6 0.8 fusion.66
  127.0 2.1 collective-permute-start
  130.2 3.8 collective-permute-start.1
  134.6 3.6 collective-permute-start.2
  138.2 4.2 collective-permute-start.3
  142.4 5.0 collective-permute-start.4
  147.4 4.1 collective-permute-start.5
  151.5 1.3 collective-permute-start.6
  152.8 1.8 collective-permute-start.7
  154.7 2.8 collective-permute-start.8
  157.5 5.8 %collective-permute-done.4 = bf16[224,256]{1,0:T(8,128)(2,1)S(1)} collective-permute-done((bf16[224,256]{1,0:T(8,128)(2,1)S(1)}, bf16[224,256]{1,0:T(8,128)(2,1)S(1)}, u32[]{:S(2)}, u32[]{:S(2)}) %collective-permute-start.4) | collective-permute-done | bytes 114720 | tf_op jit(solution)/shard_map/ppermute | solution.py:30
  163.4 2.4 collective-permute-done.6
  165.9 2.0 collective-permute-done.8
  167.9 1.1 fusion.70
  168.9 1.0 fusion.76
  169.9 1.4 multiply_reduce_fusion.1
  171.4 1.1 fusion.10
  173.5 1.3 collective-permute-start.9
  174.8 1.3 collective-permute-start.10
  176.1 1.3 collective-permute-start.11
  177.5 1.3 collective-permute-start.12
  178.8 1.3 collective-permute-start.13
  180.2 1.3 collective-permute-start.14
  181.5 5.6 %collective-permute-done.10 = bf16[224,256]{1,0:T(8,128)(2,1)S(1)} collective-permute-done((bf16[224,256]{1,0:T(8,128)(2,1)S(1)}, bf16[224,256]{1,0:T(8,128)(2,1)S(1)}, u32[]{:S(2)}, u32[]{:S(2)}) %collective-permute-start.10) | collective-permute-done | bytes 114720 | tf_op jit(solution)/shard_map/ppermute | solution.py:30
  187.1 1.3 collective-permute-start.15
  188.4 1.8 collective-permute-done.11
  190.2 1.3 collective-permute-start.16
  192.2 18.7 %collective-permute-done.12 = bf16[224,256]{1,0:T(8,128)(2,1)S(1)} collective-permute-done((bf16[224,256]{1,0:T(8,128)(2,1)S(1)}, bf16[224,256]{1,0:T(8,128)(2,1)S(1)}, u32[]{:S(2)}, u32[]{:S(2)}) %collective-permute-start.12) | collective-permute-done | bytes 114720 | tf_op jit(solution)/shard_map/ppermute | solution.py:30
  210.9 10.7 %collective-permute-done.14 = bf16[224,256]{1,0:T(8,128)(2,1)S(1)} collective-permute-done((bf16[224,256]{1,0:T(8,128)(2,1)S(1)}, bf16[224,256]{1,0:T(8,128)(2,1)S(1)}, u32[]{:S(2)}, u32[]{:S(2)}) %collective-permute-start.14) | collective-permute-done | bytes 114720 | tf_op jit(solution)/shard_map/ppermute | solution.py:30
  221.9 1.9 collective-permute-start.17
  223.8 0.9 fusion.64
  225.6 0.9 fusion.62
  226.6 1.7 maximum_maximum_fusion
  228.3 3.8 gather_fusion
  232.1 7.5 %all-to-all-start.3 = ((bf16[32,2,128,128]{3,2,1,0:T(8,128)(2,1)}), bf16[32,2,128,128]{3,2,1,0:T(8,128)(2,1)}, u32[]{:S(2)}, u32[]{:S(2)}) async-start(bf16[32,2,128,128]{3,2,1,0:T(8,128)(2,1)} %bitcast.110), calls=%async_computation.3 | async-start | bytes 4194304 | tf_op jit(solution)/shard_map/all_to_all | solution.py:251
  241.0 2.5 fusion.72
  243.5 2.8 copy.21
  246.4 2.0 pad_maximum_fusion
  248.4 39.8 %all-to-all-done.3 = bf16[32,2,128,128]{3,2,1,0:T(8,128)(2,1)} async-done(((bf16[32,2,128,128]{3,2,1,0:T(8,128)(2,1)}), bf16[32,2,128,128]{3,2,1,0:T(8,128)(2,1)}, u32[]{:S(2)}, u32[]{:S(2)}) %all-to-all-start.3) | async-done | bytes 2097184 | tf_op jit(solution)/shard_map/all_to_all | solution.py:251
  288.2 6.6 %all-to-all-start.2 = ((bf16[32,160,224]{2,1,0:T(8,128)(2,1)}), bf16[32,160,224]{2,1,0:T(8,128)(2,1)S(1)}, u32[]{:S(2)}, u32[]{:S(2)}) async-start(bf16[32,160,224]{2,1,0:T(8,128)(2,1)} %pad_maximum_fusion), calls=%async_computation.2 | async-start | bytes 5242880 | tf_op jit(solution)/shard_map/all_to_all | solution.py:223
  294.8 3.2 concatenate.87
  298.1 3.7 gather_fusion.1
  301.8 3.1 reshape.240
  304.9 50.4 %all-to-all-done.2 = bf16[32,160,224]{2,1,0:T(8,128)(2,1)S(1)} async-done(((bf16[32,160,224]{2,1,0:T(8,128)(2,1)}), bf16[32,160,224]{2,1,0:T(8,128)(2,1)S(1)}, u32[]{:S(2)}, u32[]{:S(2)}) %all-to-all-start.2) | async-done | bytes 2293792 | tf_op jit(solution)/shard_map/all_to_all | solution.py:223
  357.0 1.8 maximum_bitcast_fusion
  359.3 3.9 reduce.7
  363.1 1.7 reshape.294
  364.8 66.6 %all_to_all.34 = bf16[16,2,32896]{2,1,0:T(2,128)(2,1)S(1)} all-to-all(bf16[16,2,32896]{2,1,0:T(2,128)(2,1)} %reshape.294), channel_id=1, replica_groups=mesh['seq'=16,'wt'=32] {'seq'}, dimensions={0} | all-to-all | bytes 4210688 | tf_op jit(solution)/shard_map/all_to_all | solution.py:268
  431.4 9.2 %reshape.295 = bf16[16,1,65792]{2,1,0:T(2,128)(2,1)} reshape(bf16[16,2,32896]{2,1,0:T(2,128)(2,1)S(1)} %all_to_all.34) | data formatting | bytes 4210688
  440.7 7.1 %convert_reduce_fusion.1 = f32[65792]{0:T(1024)S(1)} fusion(bf16[16,1,65792]{2,1,0:T(2,128)(2,1)} %reshape.295), kind=kLoop, calls=%fused_computation.10 | loop fusion | flops 2039552 | bytes 2368512 | tf_op jit(solution)/shard_map/reduce_sum | solution.py:267
  449.1 75.9 %all-gather.5.cloned.1.call-done = bf16[64,128,128]{2,1,0:T(8,128)(2,1)} async-done(((bf16[4,128,128]{2,1,0:T(8,128)(2,1)}), bf16[64,128,128]{2,1,0:T(8,128)(2,1)}) %all-gather.5.cloned.1.call-update) | async-done | bytes 2097168 | tf_op jit(solution)/shard_map/all_gather | solution.py:273
  525.0 3.2 copy.44
  (120 shorter events, 17.1 us)
Async XLA Ops:
  11.1 18.9 %all-to-all-start = ((bf16[32,1,2]{2,1,0:T(2,128)(2,1)}), bf16[32,1,2]{2,1,0:T(2,128)(2,1)S(1)}, u32[]{:S(2)}, u32[]{:S(2)}) async-start(bf16[32,1,2]{2,1,0:T(2,128)(2,1)} %all_to_all.28), calls=%async_computation | async-start | bytes 32768 | tf_op jit(solution)/shard_map/all_to_all | solution.py:99
  29.9 10.0 %copy-start.6 = (f32[144]{0:T(256)S(1)}, f32[144]{0:T(256)}, u32[]{:S(2)}) copy-start(f32[144]{0:T(256)} %param.7) | copy-start | bytes 1732
  29.9 10.3 %copy-start.5 = (bf16[224,144]{0,1:T(8,128)(2,1)S(1)}, bf16[224,144]{0,1:T(8,128)(2,1)}, u32[]{:S(2)}) copy-start(bf16[224,144]{0,1:T(8,128)(2,1)} %param.6) | copy-start | bytes 193540
  29.9 11.4 %copy-start.7 = (s32[224]{0:T(256)S(1)}, s32[224]{0:T(256)}, u32[]{:S(2)}) copy-start(s32[224]{0:T(256)} %param.8) | copy-start | bytes 2692
  29.9 62.6 %all-to-all-start.1 = ((bf16[32,2,128,128]{3,2,1,0:T(8,128)(2,1)}), bf16[32,2,128,128]{3,2,1,0:T(8,128)(2,1)S(1)}, u32[]{:S(2)}, u32[]{:S(2)}) async-start(bf16[32,2,128,128]{3,2,1,0:T(8,128)(2,1)} %bitcast.109), calls=%async_computation.1 | async-start | bytes 4194304 | tf_op jit(solution)/shard_map/all_to_all | solution.py:92
  39.9 78.5 %all-gather.3.cloned.1.call-start = ((), (), s32[]{:S(2)}) async-start(), calls=%async_computation.5 | async-start | bytes 2433024 | tf_op jit(solution)/shard_map/all_gather | solution.py:113
  92.5 1.3 copy-start.1
  123.4 2.2 copy-start.3
  125.6 3.6 copy-start
  127.0 3.1 collective-permute-start
  130.2 21.3 %collective-permute-start.1 = (bf16[224,256]{1,0:T(8,128)(2,1)S(1)}, bf16[224,256]{1,0:T(8,128)(2,1)S(1)}, u32[]{:S(2)}, u32[]{:S(2)}) collective-permute-start(bf16[224,256]{1,0:T(8,128)(2,1)S(1)} %pad_maximum_fusion.1), channel_id=1, source_target_pairs={{0,32},{32,64},{64,96},{96,128},{128,160},{160,192},{192,224},{224... | collective-permute-start | bytes 344072 | tf_op jit(solution)/shard_map/ppermute | solution.py:30
  134.6 18.3 %collective-permute-start.2 = (bf16[224,256]{1,0:T(8,128)(2,1)S(1)}, bf16[224,256]{1,0:T(8,128)(2,1)S(1)}, u32[]{:S(2)}, u32[]{:S(2)}) collective-permute-start(bf16[224,256]{1,0:T(8,128)(2,1)S(1)} %pad_maximum_fusion.1), channel_id=1, source_target_pairs={{0,64},{32,96},{64,128},{96,160},{128,192},{160,224},{192,256},{22... | collective-permute-start | bytes 344072 | tf_op jit(solution)/shard_map/ppermute | solution.py:30
  138.2 16.5 %collective-permute-start.3 = (bf16[224,256]{1,0:T(8,128)(2,1)S(1)}, bf16[224,256]{1,0:T(8,128)(2,1)S(1)}, u32[]{:S(2)}, u32[]{:S(2)}) collective-permute-start(bf16[224,256]{1,0:T(8,128)(2,1)S(1)} %pad_maximum_fusion.1), channel_id=1, source_target_pairs={{0,96},{32,128},{64,160},{96,192},{128,224},{160,256},{192,288},{2... | collective-permute-start | bytes 344072 | tf_op jit(solution)/shard_map/ppermute | solution.py:30
  142.4 20.9 %collective-permute-start.4 = (bf16[224,256]{1,0:T(8,128)(2,1)S(1)}, bf16[224,256]{1,0:T(8,128)(2,1)S(1)}, u32[]{:S(2)}, u32[]{:S(2)}) collective-permute-start(bf16[224,256]{1,0:T(8,128)(2,1)S(1)} %pad_maximum_fusion.1), channel_id=1, source_target_pairs={{0,128},{32,160},{64,192},{96,224},{128,256},{160,288},{192,320},{... | collective-permute-start | bytes 344072 | tf_op jit(solution)/shard_map/ppermute | solution.py:30
  147.4 16.0 %collective-permute-start.5 = (bf16[224,256]{1,0:T(8,128)(2,1)S(1)}, bf16[224,256]{1,0:T(8,128)(2,1)S(1)}, u32[]{:S(2)}, u32[]{:S(2)}) collective-permute-start(bf16[224,256]{1,0:T(8,128)(2,1)S(1)} %pad_maximum_fusion.1), channel_id=1, source_target_pairs={{0,160},{32,192},{64,224},{96,256},{128,288},{160,320},{192,352},{... | collective-permute-start | bytes 344072 | tf_op jit(solution)/shard_map/ppermute | solution.py:30
  151.5 14.3 %collective-permute-start.6 = (bf16[224,256]{1,0:T(8,128)(2,1)S(1)}, bf16[224,256]{1,0:T(8,128)(2,1)S(1)}, u32[]{:S(2)}, u32[]{:S(2)}) collective-permute-start(bf16[224,256]{1,0:T(8,128)(2,1)S(1)} %pad_maximum_fusion.1), channel_id=1, source_target_pairs={{0,192},{32,224},{64,256},{96,288},{128,320},{160,352},{192,384},{... | collective-permute-start | bytes 344072 | tf_op jit(solution)/shard_map/ppermute | solution.py:30
  152.8 13.0 %collective-permute-start.7 = (bf16[224,256]{1,0:T(8,128)(2,1)S(1)}, bf16[224,256]{1,0:T(8,128)(2,1)S(1)}, u32[]{:S(2)}, u32[]{:S(2)}) collective-permute-start(bf16[224,256]{1,0:T(8,128)(2,1)S(1)} %pad_maximum_fusion.1), channel_id=1, source_target_pairs={{0,224},{32,256},{64,288},{96,320},{128,352},{160,384},{192,416},{... | collective-permute-start | bytes 344072 | tf_op jit(solution)/shard_map/ppermute | solution.py:30
  154.7 13.1 %collective-permute-start.8 = (bf16[224,256]{1,0:T(8,128)(2,1)S(1)}, bf16[224,256]{1,0:T(8,128)(2,1)S(1)}, u32[]{:S(2)}, u32[]{:S(2)}) collective-permute-start(bf16[224,256]{1,0:T(8,128)(2,1)S(1)} %pad_maximum_fusion.1), channel_id=1, source_target_pairs={{0,256},{32,288},{64,320},{96,352},{128,384},{160,416},{192,448},{... | collective-permute-start | bytes 344072 | tf_op jit(solution)/shard_map/ppermute | solution.py:30
  167.8 1.1 copy-start.8
  173.5 6.7 %collective-permute-start.9 = (bf16[224,256]{1,0:T(8,128)(2,1)S(1)}, bf16[224,256]{1,0:T(8,128)(2,1)S(1)}, u32[]{:S(2)}, u32[]{:S(2)}) collective-permute-start(bf16[224,256]{1,0:T(8,128)(2,1)S(1)} %pad_maximum_fusion.2), channel_id=1, source_target_pairs={{32,0},{64,32},{96,64},{128,96},{160,128},{192,160},{224,192},{256... | collective-permute-start | bytes 344072 | tf_op jit(solution)/shard_map/ppermute | solution.py:30
  174.8 12.3 %collective-permute-start.10 = (bf16[224,256]{1,0:T(8,128)(2,1)S(1)}, bf16[224,256]{1,0:T(8,128)(2,1)S(1)}, u32[]{:S(2)}, u32[]{:S(2)}) collective-permute-start(bf16[224,256]{1,0:T(8,128)(2,1)S(1)} %pad_maximum_fusion.3), channel_id=1, source_target_pairs={{64,0},{96,32},{128,64},{160,96},{192,128},{224,160},{256,192},{28... | collective-permute-start | bytes 344072 | tf_op jit(solution)/shard_map/ppermute | solution.py:30
  176.1 14.1 %collective-permute-start.11 = (bf16[224,256]{1,0:T(8,128)(2,1)S(1)}, bf16[224,256]{1,0:T(8,128)(2,1)S(1)}, u32[]{:S(2)}, u32[]{:S(2)}) collective-permute-start(bf16[224,256]{1,0:T(8,128)(2,1)S(1)} %pad_maximum_fusion.4), channel_id=1, source_target_pairs={{96,0},{128,32},{160,64},{192,96},{224,128},{256,160},{288,192},{3... | collective-permute-start | bytes 344072 | tf_op jit(solution)/shard_map/ppermute | solution.py:30
  177.5 33.4 %collective-permute-start.12 = (bf16[224,256]{1,0:T(8,128)(2,1)S(1)}, bf16[224,256]{1,0:T(8,128)(2,1)S(1)}, u32[]{:S(2)}, u32[]{:S(2)}) collective-permute-start(bf16[224,256]{1,0:T(8,128)(2,1)S(1)} %pad_maximum_fusion.5), channel_id=1, source_target_pairs={{128,0},{160,32},{192,64},{224,96},{256,128},{288,160},{320,192},{... | collective-permute-start | bytes 344072 | tf_op jit(solution)/shard_map/ppermute | solution.py:30
  178.8 32.1 %collective-permute-start.13 = (bf16[224,256]{1,0:T(8,128)(2,1)S(1)}, bf16[224,256]{1,0:T(8,128)(2,1)S(1)}, u32[]{:S(2)}, u32[]{:S(2)}) collective-permute-start(bf16[224,256]{1,0:T(8,128)(2,1)S(1)} %pad_maximum_fusion.6), channel_id=1, source_target_pairs={{160,0},{192,32},{224,64},{256,96},{288,128},{320,160},{352,192},{... | collective-permute-start | bytes 344072 | tf_op jit(solution)/shard_map/ppermute | solution.py:30
  180.2 41.5 %collective-permute-start.14 = (bf16[224,256]{1,0:T(8,128)(2,1)S(1)}, bf16[224,256]{1,0:T(8,128)(2,1)S(1)}, u32[]{:S(2)}, u32[]{:S(2)}) collective-permute-start(bf16[224,256]{1,0:T(8,128)(2,1)S(1)} %pad_maximum_fusion.7), channel_id=1, source_target_pairs={{192,0},{224,32},{256,64},{288,96},{320,128},{352,160},{384,192},{... | collective-permute-start | bytes 344072 | tf_op jit(solution)/shard_map/ppermute | solution.py:30
  187.1 34.6 %collective-permute-start.15 = (bf16[224,256]{1,0:T(8,128)(2,1)S(1)}, bf16[224,256]{1,0:T(8,128)(2,1)S(1)}, u32[]{:S(2)}, u32[]{:S(2)}) collective-permute-start(bf16[224,256]{1,0:T(8,128)(2,1)S(1)} %pad_maximum_fusion.8), channel_id=1, source_target_pairs={{224,0},{256,32},{288,64},{320,96},{352,128},{384,160},{416,192},{... | collective-permute-start | bytes 344072 | tf_op jit(solution)/shard_map/ppermute | solution.py:30
  190.2 31.5 %collective-permute-start.16 = (bf16[224,256]{1,0:T(8,128)(2,1)S(1)}, bf16[224,256]{1,0:T(8,128)(2,1)S(1)}, u32[]{:S(2)}, u32[]{:S(2)}) collective-permute-start(bf16[224,256]{1,0:T(8,128)(2,1)S(1)} %pad_maximum_fusion.9), channel_id=1, source_target_pairs={{256,0},{288,32},{320,64},{352,96},{384,128},{416,160},{448,192},{... | collective-permute-start | bytes 344072 | tf_op jit(solution)/shard_map/ppermute | solution.py:30
  221.9 3.1 collective-permute-start.17
  232.1 56.1 %all-to-all-start.3 = ((bf16[32,2,128,128]{3,2,1,0:T(8,128)(2,1)}), bf16[32,2,128,128]{3,2,1,0:T(8,128)(2,1)}, u32[]{:S(2)}, u32[]{:S(2)}) async-start(bf16[32,2,128,128]{3,2,1,0:T(8,128)(2,1)} %bitcast.110), calls=%async_computation.3 | async-start | bytes 4194304 | tf_op jit(solution)/shard_map/all_to_all | solution.py:251
  239.7 1.3 copy-start.4
  288.2 67.2 %all-to-all-start.2 = ((bf16[32,160,224]{2,1,0:T(8,128)(2,1)}), bf16[32,160,224]{2,1,0:T(8,128)(2,1)S(1)}, u32[]{:S(2)}, u32[]{:S(2)}) async-start(bf16[32,160,224]{2,1,0:T(8,128)(2,1)} %pad_maximum_fusion), calls=%async_computation.2 | async-start | bytes 5242880 | tf_op jit(solution)/shard_map/all_to_all | solution.py:223
  294.8 230.2 %all-gather.5.cloned.1.call-start = ((), (), s32[]{:S(2)}) async-start(), calls=%async_computation.6 | async-start | bytes 2228224 | tf_op jit(solution)/shard_map/all_gather | solution.py:273
  355.4 1.6 copy-start.2
Sparse Core Ops, SparseCore 0:
  44.4 73.9 all-gather.2
  448.6 76.2 all-gather.4

commit v3 on v2

--- a/solution.py
+++ b/solution.py
@@ -256,27 +256,16 @@
     slots = owned_grads.shape[0]
     chunk = slots * BLK * BLK // n_seq
     gain_width = -(-feat // 128) * 128
+    reduced = lax.psum_scatter(owned_grads, "seq", scatter_dimension=0, tiled=True)
     gain_row = jnp.pad(gain_part.astype(jnp.bfloat16), (0, gain_width - feat))
-    to_reduce = jnp.concatenate(
-        [
-            owned_grads.reshape(n_seq, chunk),
-            jnp.broadcast_to(gain_row[None], (n_seq, gain_width)),
-        ],
-        axis=1,
-    )
-    reduced = jnp.sum(
-        lax.all_to_all(to_reduce, "seq", split_axis=0, concat_axis=0, tiled=True).astype(
-            jnp.float32
-        ),
-        axis=0,
-    )
-    block_grads = lax.all_gather(
-        reduced[:chunk].astype(jnp.bfloat16).reshape(slots // n_seq, BLK, BLK),
+    gathered_back = lax.all_gather(
+        jnp.concatenate([reduced.reshape(1, chunk), gain_row[None]], axis=1),
         "seq",
         axis=0,
         tiled=True,
     )
-    gain_total = reduced[chunk : chunk + feat]
+    block_grads = gathered_back[:, :chunk].reshape(slots, BLK, BLK)
+    gain_total = jnp.sum(gathered_back[:, chunk : chunk + feat].astype(jnp.float32), axis=0)
     return (attn_rows, tokens_grad, gain_total, block_grads[None])
 
 

time: 537 us -> 545 us (1.015)
  waiting for transfers between devices: 280 us -> 365 us
  blocking collectives: 66.6 us -> 0 us
  starting transfers between devices: 75.2 us -> 91.1 us
  local copies, waits for them, and re-layouts: 58 us -> 44.3 us
  other arithmetic: 27.6 us -> 16.3 us
    all_to_all x1 -> x0, blocking collectives: 66.6 us -> none  [body(): lax.all_to_all(to_reduce, 'seq', split_axis=0, concat_axis=0, tiled=True)]
    reduce_scatter x0 -> x1, waiting for transfers between devices: none -> 51.1 us  [body(): lax.psum_scatter(owned_grads, 'seq', scatter_dimension=0, tiled=True)]
    all_gather x1, waiting for transfers between devices: 75.9 us -> 104 us  [body(): lax.all_gather(jnp.concatenate([reduced.reshape(1, chunk), gain_row[None]...]
    all_to_all x1, waiting for transfers between devices: 50.4 us -> 64.9 us  [body(): lax.all_to_all(packed.reshape(groups, feat + pad_rows, tok_rows), 'wt', s...]
    ppermute x16, starting transfers between devices: 36.8 us -> 48.9 us  [shifted(): lax.ppermute(value, axis, [(source, source + steps) for source in range(i...]
    unnamed x29 -> x25, local copies, waits for them, and re-layouts: 19.3 us -> 7.28 us
    ppermute x16, waiting for transfers between devices: 47.1 us -> 39.6 us  [shifted(): lax.ppermute(value, axis, [(source, source + steps) for source in range(i...]
    reduce_sum x1, other arithmetic: 7.13 us -> 0.58 us  [body(): jnp.sum(gathered_back[:, chunk:chunk + feat].astype(jnp.float32), axis=0)]
  transfers between devices with their start and end apart: 24 -> 25, of which waited for: 14 -> 16; matrix products, arithmetic and copies ran while one was open for 8% -> 7% of each run, Pallas kernels for 0% -> 0%
where the time goes in v3:
time: 545 us; the launch traced here: 543 us
  waiting for transfers between devices  365 us (67%)
  starting transfers between devices  91.1 us (17%)
  local copies, waits for them, and re-layouts  44.3 us (8%)
  other arithmetic  16.3 us (3%)
  between operations  14.6 us (3%)
  matrix products  12.2 us (2%)
    all_gather x1, waiting for transfers between devices, body(): lax.all_gather(jnp.concatenate([reduced.reshape(1, chunk), gain_row[None]...  104 us
    all_to_all x1, waiting for transfers between devices, body(): lax.all_to_all(packed.reshape(groups, feat + pad_rows, tok_rows), 'wt', s...  64.9 us
    reduce_scatter x1, waiting for transfers between devices, body(): lax.psum_scatter(owned_grads, 'seq', scatter_dimension=0, tiled=True)  51.1 us
    all_to_all x1, waiting for transfers between devices, body(): lax.all_to_all(outgoing[:dump_slot].reshape(groups, CAP, BLK, BLK), 'wt',...  51 us
    ppermute x16, starting transfers between devices, shifted(): lax.ppermute(value, axis, [(source, source + steps) for source in range(i...  48.9 us
    ppermute x16, waiting for transfers between devices, shifted(): lax.ppermute(value, axis, [(source, source + steps) for source in range(i...  39.6 us
    all_to_all x1, waiting for transfers between devices, body(): lax.all_to_all(slot_grads.astype(jnp.bfloat16), 'wt', split_axis=0, conca...  37.7 us
    all_gather x1, waiting for transfers between devices, body(): lax.all_gather(jnp.concatenate([tokens_in, gain_rows, jnp.zeros((side_row...  15.7 us
  transfers between devices with their start and end apart: 25, of which 16 were waited for; matrix products, arithmetic and copies ran while one was open for 7% of the time, Pallas kernels for 0%

profile of v3, /device:TPU:6, one launch (start us, length us, event | category | flops | bytes accessed | tf_op | source)
XLA Modules:
  0.0 543.5 jit_solution(120040908919249098)
XLA Ops:
  9.5 0.8 scatter_custom_fusion
  11.1 10.2 %all-to-all-start = ((bf16[32,1,2]{2,1,0:T(2,128)(2,1)}), bf16[32,1,2]{2,1,0:T(2,128)(2,1)S(1)}, u32[]{:S(2)}, u32[]{:S(2)}) async-start(bf16[32,1,2]{2,1,0:T(2,128)(2,1)} %all_to_all.20), calls=%async_computation | async-start | bytes 32768 | tf_op jit(solution)/shard_map/all_to_all | solution.py:99
  21.8 6.7 %scatter_fusion = bf16[65,128,128]{2,1,0:T(8,128)(2,1)S(1)} fusion(bf16[65,128,128]{2,1,0:T(8,128)(2,1)S(1)} %broadcast_in_dim.31, s32[64]{0:T(128)S(1)} %fusion.54, bf16[64,128,128]{2,1,0:T(8,128)(2,1)} %bitcast.120), kind=kCustom, calls=%fused_computation.3 | custom fusion | bytes 6291712 | tf_op jit(solution)/shard_map/scatter | solution.py:84
  28.5 1.5 slice.313
  30.0 9.9 %all-to-all-start.1 = ((bf16[32,2,128,128]{3,2,1,0:T(8,128)(2,1)}), bf16[32,2,128,128]{3,2,1,0:T(8,128)(2,1)S(1)}, u32[]{:S(2)}, u32[]{:S(2)}) async-start(bf16[32,2,128,128]{3,2,1,0:T(8,128)(2,1)} %bitcast.115), calls=%async_computation.1 | async-start | bytes 4194304 | tf_op jit(solution)/shard_map/all_to_all | solution.py:92
  41.6 51.0 %all-to-all-done.1 = bf16[32,2,128,128]{3,2,1,0:T(8,128)(2,1)S(1)} async-done(((bf16[32,2,128,128]{3,2,1,0:T(8,128)(2,1)}), bf16[32,2,128,128]{3,2,1,0:T(8,128)(2,1)S(1)}, u32[]{:S(2)}, u32[]{:S(2)}) %all-to-all-start.1) | async-done | bytes 2097184 | tf_op jit(solution)/shard_map/all_to_all | solution.py:92
  92.6 1.3 copy-done.1
  94.5 6.7 %scatter_fusion.1 = bf16[73,128,128]{2,1,0:T(8,128)(2,1)S(1)} fusion(bf16[73,128,128]{2,1,0:T(8,128)(2,1)S(1)} %broadcast_in_dim.28, s32[64]{0:T(128)S(1)} %fusion.55, bf16[64,128,128]{2,1,0:T(8,128)(2,1)} %bitcast.114), kind=kCustom, calls=%fused_computation.4 | custom fusion | bytes 6291712 | tf_op jit(solution)/shard_map/scatter | solution.py:136
  101.2 1.6 fusion.72
  102.7 15.7 %all-gather.4.cloned.1.call-done = bf16[232,4608]{0,1:T(8,128)(2,1)} async-done(((bf16[232,144]{0,1:T(8,128)(2,1)}), bf16[232,4608]{0,1:T(8,128)(2,1)}) %all-gather.4.cloned.1.call-update) | async-done | bytes 2138128 | tf_op jit(solution)/shard_map/all_gather | solution.py:113
  118.4 2.8 copy.23
  121.7 1.6 slice_convert_fusion
  123.4 2.2 fusion.11
  125.6 0.8 fusion.65
  127.0 2.1 collective-permute-start
  129.2 0.8 fusion.67
  130.2 3.8 collective-permute-start.1
  134.6 8.0 %collective-permute-start.8 = (bf16[224,256]{1,0:T(8,128)(2,1)S(1)}, bf16[224,256]{1,0:T(8,128)(2,1)S(1)}, u32[]{:S(2)}, u32[]{:S(2)}) collective-permute-start(bf16[224,256]{1,0:T(8,128)(2,1)S(1)} %pad_maximum_fusion.1), channel_id=1, source_target_pairs={{0,256},{32,288},{64,320},{96,352},{128,384},{160,416},{192,448},{... | collective-permute-start | bytes 344072 | tf_op jit(solution)/shard_map/ppermute | solution.py:30
  142.7 1.8 collective-permute-start.7
  144.5 2.5 collective-permute-start.6
  147.0 2.1 collective-permute-start.5
  149.1 3.2 collective-permute-start.2
  152.3 12.5 %collective-permute-done.2 = bf16[224,256]{1,0:T(8,128)(2,1)S(1)} collective-permute-done((bf16[224,256]{1,0:T(8,128)(2,1)S(1)}, bf16[224,256]{1,0:T(8,128)(2,1)S(1)}, u32[]{:S(2)}, u32[]{:S(2)}) %collective-permute-start.2) | collective-permute-done | bytes 114720 | tf_op jit(solution)/shard_map/ppermute | solution.py:30
  164.8 7.2 %collective-permute-start.3 = (bf16[224,256]{1,0:T(8,128)(2,1)S(1)}, bf16[224,256]{1,0:T(8,128)(2,1)S(1)}, u32[]{:S(2)}, u32[]{:S(2)}) collective-permute-start(bf16[224,256]{1,0:T(8,128)(2,1)S(1)} %pad_maximum_fusion.1), channel_id=1, source_target_pairs={{0,96},{32,128},{64,160},{96,192},{128,224},{160,256},{192,288},{2... | collective-permute-start | bytes 344072 | tf_op jit(solution)/shard_map/ppermute | solution.py:30
  172.1 2.6 collective-permute-done.3
  174.7 10.0 %collective-permute-start.4 = (bf16[224,256]{1,0:T(8,128)(2,1)S(1)}, bf16[224,256]{1,0:T(8,128)(2,1)S(1)}, u32[]{:S(2)}, u32[]{:S(2)}) collective-permute-start(bf16[224,256]{1,0:T(8,128)(2,1)S(1)} %pad_maximum_fusion.1), channel_id=1, source_target_pairs={{0,128},{32,160},{64,192},{96,224},{128,256},{160,288},{192,320},{... | collective-permute-start | bytes 344072 | tf_op jit(solution)/shard_map/ppermute | solution.py:30
  184.7 2.1 collective-permute-done.4
  187.0 1.1 fusion.69
  188.1 1.0 fusion.75
  189.1 1.4 multiply_reduce_fusion.1
  190.5 1.1 fusion.10
  192.7 1.3 collective-permute-start.10
  194.0 1.3 collective-permute-start.11
  195.3 1.3 collective-permute-start.12
  196.6 1.3 collective-permute-start.13
  198.0 1.3 collective-permute-start.14
  200.0 1.3 collective-permute-start.15
  201.3 0.8 collective-permute-done.11
  202.0 1.3 collective-permute-start.16
  203.3 9.9 %collective-permute-done.12 = bf16[224,256]{1,0:T(8,128)(2,1)S(1)} collective-permute-done((bf16[224,256]{1,0:T(8,128)(2,1)S(1)}, bf16[224,256]{1,0:T(8,128)(2,1)S(1)}, u32[]{:S(2)}, u32[]{:S(2)}) %collective-permute-start.12) | collective-permute-done | bytes 114720 | tf_op jit(solution)/shard_map/ppermute | solution.py:30
  213.3 1.3 collective-permute-start.9
  215.3 6.1 %collective-permute-done.14 = bf16[224,256]{1,0:T(8,128)(2,1)S(1)} collective-permute-done((bf16[224,256]{1,0:T(8,128)(2,1)S(1)}, bf16[224,256]{1,0:T(8,128)(2,1)S(1)}, u32[]{:S(2)}, u32[]{:S(2)}) %collective-permute-start.14) | collective-permute-done | bytes 114720 | tf_op jit(solution)/shard_map/ppermute | solution.py:30
  221.4 4.9 collective-permute-done.15
  226.5 1.9 collective-permute-start.17
  228.4 0.9 fusion.63
  230.3 0.9 fusion.61
  231.2 1.7 maximum_maximum_fusion
  232.9 3.8 gather_fusion
  236.7 7.8 %all-to-all-start.3 = ((bf16[32,2,128,128]{3,2,1,0:T(8,128)(2,1)}), bf16[32,2,128,128]{3,2,1,0:T(8,128)(2,1)}, u32[]{:S(2)}, u32[]{:S(2)}) async-start(bf16[32,2,128,128]{3,2,1,0:T(8,128)(2,1)} %bitcast.116), calls=%async_computation.3 | async-start | bytes 4194304 | tf_op jit(solution)/shard_map/all_to_all | solution.py:251
  245.9 2.6 fusion.71
  248.4 2.8 copy.21
  251.3 2.0 pad_maximum_fusion
  253.3 37.7 %all-to-all-done.3 = bf16[32,2,128,128]{3,2,1,0:T(8,128)(2,1)} async-done(((bf16[32,2,128,128]{3,2,1,0:T(8,128)(2,1)}), bf16[32,2,128,128]{3,2,1,0:T(8,128)(2,1)}, u32[]{:S(2)}, u32[]{:S(2)}) %all-to-all-start.3) | async-done | bytes 2097184 | tf_op jit(solution)/shard_map/all_to_all | solution.py:251
  291.0 10.1 %all-to-all-start.2 = ((bf16[32,160,224]{2,1,0:T(8,128)(2,1)}), bf16[32,160,224]{2,1,0:T(8,128)(2,1)S(1)}, u32[]{:S(2)}, u32[]{:S(2)}) async-start(bf16[32,160,224]{2,1,0:T(8,128)(2,1)} %pad_maximum_fusion), calls=%async_computation.2 | async-start | bytes 5242880 | tf_op jit(solution)/shard_map/all_to_all | solution.py:223
  301.2 3.2 concatenate.87
  304.4 3.7 gather_fusion.1
  308.2 64.9 %all-to-all-done.2 = bf16[32,160,224]{2,1,0:T(8,128)(2,1)S(1)} async-done(((bf16[32,160,224]{2,1,0:T(8,128)(2,1)}), bf16[32,160,224]{2,1,0:T(8,128)(2,1)S(1)}, u32[]{:S(2)}, u32[]{:S(2)}) %all-to-all-start.2) | async-done | bytes 2293792 | tf_op jit(solution)/shard_map/all_to_all | solution.py:223
  373.6 0.8 multiply_reduce_fusion
  374.4 51.1 %reduce-scatter.2.cloned.1.call-done = bf16[4,128,128]{2,1,0:T(8,128)(2,1)} async-done(((bf16[64,128,128]{2,1,0:T(8,128)(2,1)}), bf16[4,128,128]{2,1,0:T(8,128)(2,1)}) %reduce-scatter.2.cloned.1.call-update) | async-done | bytes 131088 | tf_op jit(solution)/shard_map/reduce_scatter | solution.py:259
  425.5 1.0 reshape.233
  426.5 1.0 maximum_bitcast_fusion
  427.5 104.4 %all-gather.6.cloned.1.call-done = bf16[16,1,65792]{2,1,0:T(2,128)(2,1)} async-done(((bf16[1,1,65792]{2,1,0:T(2,128)(2,1)}), bf16[16,1,65792]{2,1,0:T(2,128)(2,1)}) %all-gather.6.cloned.1.call-update) | async-done | bytes 2105360 | tf_op jit(solution)/shard_map/all_gather | solution.py:261
  531.8 2.4 copy.25
  535.0 2.0 broadcast_in_dim_reshape.3
  (117 shorter events, 14.1 us)
Async XLA Ops:
  11.1 18.9 %all-to-all-start = ((bf16[32,1,2]{2,1,0:T(2,128)(2,1)}), bf16[32,1,2]{2,1,0:T(2,128)(2,1)S(1)}, u32[]{:S(2)}, u32[]{:S(2)}) async-start(bf16[32,1,2]{2,1,0:T(2,128)(2,1)} %all_to_all.20), calls=%async_computation | async-start | bytes 32768 | tf_op jit(solution)/shard_map/all_to_all | solution.py:99
  30.0 10.0 %copy-start.5 = (f32[144]{0:T(256)S(1)}, f32[144]{0:T(256)}, u32[]{:S(2)}) copy-start(f32[144]{0:T(256)} %param.7) | copy-start | bytes 1732
  30.0 10.3 %copy-start.4 = (bf16[224,144]{0,1:T(8,128)(2,1)S(1)}, bf16[224,144]{0,1:T(8,128)(2,1)}, u32[]{:S(2)}) copy-start(bf16[224,144]{0,1:T(8,128)(2,1)} %param.6) | copy-start | bytes 193540
  30.0 11.4 %copy-start.6 = (s32[224]{0:T(256)S(1)}, s32[224]{0:T(256)}, u32[]{:S(2)}) copy-start(s32[224]{0:T(256)} %param.8) | copy-start | bytes 2692
  30.0 62.6 %all-to-all-start.1 = ((bf16[32,2,128,128]{3,2,1,0:T(8,128)(2,1)}), bf16[32,2,128,128]{3,2,1,0:T(8,128)(2,1)S(1)}, u32[]{:S(2)}, u32[]{:S(2)}) async-start(bf16[32,2,128,128]{3,2,1,0:T(8,128)(2,1)} %bitcast.115), calls=%async_computation.1 | async-start | bytes 4194304 | tf_op jit(solution)/shard_map/all_to_all | solution.py:92
  39.9 78.5 %all-gather.4.cloned.1.call-start = ((), (), s32[]{:S(2)}) async-start(), calls=%async_computation.5 | async-start | bytes 2433024 | tf_op jit(solution)/shard_map/all_gather | solution.py:113
  92.6 1.3 copy-start.1
  123.4 2.2 copy-start.2
  125.6 3.6 copy-start
  127.0 3.1 collective-permute-start
  130.2 18.9 %collective-permute-start.1 = (bf16[224,256]{1,0:T(8,128)(2,1)S(1)}, bf16[224,256]{1,0:T(8,128)(2,1)S(1)}, u32[]{:S(2)}, u32[]{:S(2)}) collective-permute-start(bf16[224,256]{1,0:T(8,128)(2,1)S(1)} %pad_maximum_fusion.1), channel_id=1, source_target_pairs={{0,32},{32,64},{64,96},{96,128},{128,160},{160,192},{192,224},{224... | collective-permute-start | bytes 344072 | tf_op jit(solution)/shard_map/ppermute | solution.py:30
  134.6 52.4 %collective-permute-start.8 = (bf16[224,256]{1,0:T(8,128)(2,1)S(1)}, bf16[224,256]{1,0:T(8,128)(2,1)S(1)}, u32[]{:S(2)}, u32[]{:S(2)}) collective-permute-start(bf16[224,256]{1,0:T(8,128)(2,1)S(1)} %pad_maximum_fusion.1), channel_id=1, source_target_pairs={{0,256},{32,288},{64,320},{96,352},{128,384},{160,416},{192,448},{... | collective-permute-start | bytes 344072 | tf_op jit(solution)/shard_map/ppermute | solution.py:30
  142.7 44.3 %collective-permute-start.7 = (bf16[224,256]{1,0:T(8,128)(2,1)S(1)}, bf16[224,256]{1,0:T(8,128)(2,1)S(1)}, u32[]{:S(2)}, u32[]{:S(2)}) collective-permute-start(bf16[224,256]{1,0:T(8,128)(2,1)S(1)} %pad_maximum_fusion.1), channel_id=1, source_target_pairs={{0,224},{32,256},{64,288},{96,320},{128,352},{160,384},{192,416},{... | collective-permute-start | bytes 344072 | tf_op jit(solution)/shard_map/ppermute | solution.py:30
  144.5 42.4 %collective-permute-start.6 = (bf16[224,256]{1,0:T(8,128)(2,1)S(1)}, bf16[224,256]{1,0:T(8,128)(2,1)S(1)}, u32[]{:S(2)}, u32[]{:S(2)}) collective-permute-start(bf16[224,256]{1,0:T(8,128)(2,1)S(1)} %pad_maximum_fusion.1), channel_id=1, source_target_pairs={{0,192},{32,224},{64,256},{96,288},{128,320},{160,352},{192,384},{... | collective-permute-start | bytes 344072 | tf_op jit(solution)/shard_map/ppermute | solution.py:30
  147.0 39.9 %collective-permute-start.5 = (bf16[224,256]{1,0:T(8,128)(2,1)S(1)}, bf16[224,256]{1,0:T(8,128)(2,1)S(1)}, u32[]{:S(2)}, u32[]{:S(2)}) collective-permute-start(bf16[224,256]{1,0:T(8,128)(2,1)S(1)} %pad_maximum_fusion.1), channel_id=1, source_target_pairs={{0,160},{32,192},{64,224},{96,256},{128,288},{160,320},{192,352},{... | collective-permute-start | bytes 344072 | tf_op jit(solution)/shard_map/ppermute | solution.py:30
  149.1 15.7 %collective-permute-start.2 = (bf16[224,256]{1,0:T(8,128)(2,1)S(1)}, bf16[224,256]{1,0:T(8,128)(2,1)S(1)}, u32[]{:S(2)}, u32[]{:S(2)}) collective-permute-start(bf16[224,256]{1,0:T(8,128)(2,1)S(1)} %pad_maximum_fusion.1), channel_id=1, source_target_pairs={{0,64},{32,96},{64,128},{96,160},{128,192},{160,224},{192,256},{22... | collective-permute-start | bytes 344072 | tf_op jit(solution)/shard_map/ppermute | solution.py:30
  164.8 9.9 %collective-permute-start.3 = (bf16[224,256]{1,0:T(8,128)(2,1)S(1)}, bf16[224,256]{1,0:T(8,128)(2,1)S(1)}, u32[]{:S(2)}, u32[]{:S(2)}) collective-permute-start(bf16[224,256]{1,0:T(8,128)(2,1)S(1)} %pad_maximum_fusion.1), channel_id=1, source_target_pairs={{0,96},{32,128},{64,160},{96,192},{128,224},{160,256},{192,288},{2... | collective-permute-start | bytes 344072 | tf_op jit(solution)/shard_map/ppermute | solution.py:30
  174.7 12.2 %collective-permute-start.4 = (bf16[224,256]{1,0:T(8,128)(2,1)S(1)}, bf16[224,256]{1,0:T(8,128)(2,1)S(1)}, u32[]{:S(2)}, u32[]{:S(2)}) collective-permute-start(bf16[224,256]{1,0:T(8,128)(2,1)S(1)} %pad_maximum_fusion.1), channel_id=1, source_target_pairs={{0,128},{32,160},{64,192},{96,224},{128,256},{160,288},{192,320},{... | collective-permute-start | bytes 344072 | tf_op jit(solution)/shard_map/ppermute | solution.py:30
  187.0 1.1 copy-start.7
  192.7 7.3 %collective-permute-start.10 = (bf16[224,256]{1,0:T(8,128)(2,1)S(1)}, bf16[224,256]{1,0:T(8,128)(2,1)S(1)}, u32[]{:S(2)}, u32[]{:S(2)}) collective-permute-start(bf16[224,256]{1,0:T(8,128)(2,1)S(1)} %pad_maximum_fusion.3), channel_id=1, source_target_pairs={{64,0},{96,32},{128,64},{160,96},{192,128},{224,160},{256,192},{28... | collective-permute-start | bytes 344072 | tf_op jit(solution)/shard_map/ppermute | solution.py:30
  194.0 8.1 %collective-permute-start.11 = (bf16[224,256]{1,0:T(8,128)(2,1)S(1)}, bf16[224,256]{1,0:T(8,128)(2,1)S(1)}, u32[]{:S(2)}, u32[]{:S(2)}) collective-permute-start(bf16[224,256]{1,0:T(8,128)(2,1)S(1)} %pad_maximum_fusion.4), channel_id=1, source_target_pairs={{96,0},{128,32},{160,64},{192,96},{224,128},{256,160},{288,192},{3... | collective-permute-start | bytes 344072 | tf_op jit(solution)/shard_map/ppermute | solution.py:30
  195.3 17.9 %collective-permute-start.12 = (bf16[224,256]{1,0:T(8,128)(2,1)S(1)}, bf16[224,256]{1,0:T(8,128)(2,1)S(1)}, u32[]{:S(2)}, u32[]{:S(2)}) collective-permute-start(bf16[224,256]{1,0:T(8,128)(2,1)S(1)} %pad_maximum_fusion.5), channel_id=1, source_target_pairs={{128,0},{160,32},{192,64},{224,96},{256,128},{288,160},{320,192},{... | collective-permute-start | bytes 344072 | tf_op jit(solution)/shard_map/ppermute | solution.py:30
  196.6 18.6 %collective-permute-start.13 = (bf16[224,256]{1,0:T(8,128)(2,1)S(1)}, bf16[224,256]{1,0:T(8,128)(2,1)S(1)}, u32[]{:S(2)}, u32[]{:S(2)}) collective-permute-start(bf16[224,256]{1,0:T(8,128)(2,1)S(1)} %pad_maximum_fusion.6), channel_id=1, source_target_pairs={{160,0},{192,32},{224,64},{256,96},{288,128},{320,160},{352,192},{... | collective-permute-start | bytes 344072 | tf_op jit(solution)/shard_map/ppermute | solution.py:30
  198.0 23.5 %collective-permute-start.14 = (bf16[224,256]{1,0:T(8,128)(2,1)S(1)}, bf16[224,256]{1,0:T(8,128)(2,1)S(1)}, u32[]{:S(2)}, u32[]{:S(2)}) collective-permute-start(bf16[224,256]{1,0:T(8,128)(2,1)S(1)} %pad_maximum_fusion.7), channel_id=1, source_target_pairs={{192,0},{224,32},{256,64},{288,96},{320,128},{352,160},{384,192},{... | collective-permute-start | bytes 344072 | tf_op jit(solution)/shard_map/ppermute | solution.py:30
  200.0 26.3 %collective-permute-start.15 = (bf16[224,256]{1,0:T(8,128)(2,1)S(1)}, bf16[224,256]{1,0:T(8,128)(2,1)S(1)}, u32[]{:S(2)}, u32[]{:S(2)}) collective-permute-start(bf16[224,256]{1,0:T(8,128)(2,1)S(1)} %pad_maximum_fusion.8), channel_id=1, source_target_pairs={{224,0},{256,32},{288,64},{320,96},{352,128},{384,160},{416,192},{... | collective-permute-start | bytes 344072 | tf_op jit(solution)/shard_map/ppermute | solution.py:30
  202.0 24.3 %collective-permute-start.16 = (bf16[224,256]{1,0:T(8,128)(2,1)S(1)}, bf16[224,256]{1,0:T(8,128)(2,1)S(1)}, u32[]{:S(2)}, u32[]{:S(2)}) collective-permute-start(bf16[224,256]{1,0:T(8,128)(2,1)S(1)} %pad_maximum_fusion.9), channel_id=1, source_target_pairs={{256,0},{288,32},{320,64},{352,96},{384,128},{416,160},{448,192},{... | collective-permute-start | bytes 344072 | tf_op jit(solution)/shard_map/ppermute | solution.py:30
  213.3 13.1 %collective-permute-start.9 = (bf16[224,256]{1,0:T(8,128)(2,1)S(1)}, bf16[224,256]{1,0:T(8,128)(2,1)S(1)}, u32[]{:S(2)}, u32[]{:S(2)}) collective-permute-start(bf16[224,256]{1,0:T(8,128)(2,1)S(1)} %pad_maximum_fusion.2), channel_id=1, source_target_pairs={{32,0},{64,32},{96,64},{128,96},{160,128},{192,160},{224,192},{256... | collective-permute-start | bytes 344072 | tf_op jit(solution)/shard_map/ppermute | solution.py:30
  226.5 3.1 collective-permute-start.17
  236.7 54.3 %all-to-all-start.3 = ((bf16[32,2,128,128]{3,2,1,0:T(8,128)(2,1)}), bf16[32,2,128,128]{3,2,1,0:T(8,128)(2,1)}, u32[]{:S(2)}, u32[]{:S(2)}) async-start(bf16[32,2,128,128]{3,2,1,0:T(8,128)(2,1)} %bitcast.116), calls=%async_computation.3 | async-start | bytes 4194304 | tf_op jit(solution)/shard_map/all_to_all | solution.py:251
  244.6 1.3 copy-start.3
  291.0 82.1 %all-to-all-start.2 = ((bf16[32,160,224]{2,1,0:T(8,128)(2,1)}), bf16[32,160,224]{2,1,0:T(8,128)(2,1)S(1)}, u32[]{:S(2)}, u32[]{:S(2)}) async-start(bf16[32,160,224]{2,1,0:T(8,128)(2,1)} %pad_maximum_fusion), calls=%async_computation.2 | async-start | bytes 5242880 | tf_op jit(solution)/shard_map/all_to_all | solution.py:223
  301.1 124.4 %reduce-scatter.2.cloned.1.call-start = ((), (), s32[]{:S(2)}) async-start(), calls=%async_computation.6 | async-start | bytes 2228224 | tf_op jit(solution)/shard_map/reduce_scatter | solution.py:259
  308.2 223.7 %all-gather.6.cloned.1.call-start = ((), (), s32[]{:S(2)}) async-start(), calls=%async_computation.7 | async-start | bytes 4473856 | tf_op jit(solution)/shard_map/all_gather | solution.py:261
Sparse Core Ops, SparseCore 0:
  44.4 73.9 all-gather.3
  308.3 117.1 reduce-scatter.1
  428.2 103.6 all-gather.5

commit v4 on v3

--- a/solution.py
+++ b/solution.py
@@ -235,7 +235,6 @@
     tokens_grad = (inv_rms[:, None] * (scaled_grad - scaled * (row_dots / D)[:, None])).astype(
         jnp.bfloat16
     )
-    gain_part = jnp.sum(normed_grad * scaled, axis=0)
     grad_query = contract_rows(normed, query_grad)
     grad_pair = contract_rows(normed, pair_grad)
     grad_table = jnp.concatenate(
@@ -246,26 +245,83 @@
         ],
         axis=0,
     )
-    slot_grads = grad_table[arrival].reshape(groups, CAP, BLK, BLK)
-    empty_block = jnp.zeros((1, BLK, BLK), jnp.bfloat16)
-    returned = lax.all_to_all(
-        slot_grads.astype(jnp.bfloat16), "wt", split_axis=0, concat_axis=0, tiled=True
-    )
-    owned_grads = jnp.concatenate([returned.reshape(-1, BLK, BLK), empty_block], axis=0)[slot_dest]
     n_seq = lax.axis_size("seq")
-    slots = owned_grads.shape[0]
-    chunk = slots * BLK * BLK // n_seq
-    gain_width = -(-feat // 128) * 128
-    reduced = lax.psum_scatter(owned_grads, "seq", scatter_dimension=0, tiled=True)
-    gain_row = jnp.pad(gain_part.astype(jnp.bfloat16), (0, gain_width - feat))
-    gathered_back = lax.all_gather(
-        jnp.concatenate([reduced.reshape(1, chunk), gain_row[None]], axis=1),
+    band = BLK // n_seq
+    slots = slot_dest.shape[0]
+    band_len = CAP * band * BLK
+    block_len = groups * band_len
+    slot_grads = grad_table[arrival].astype(jnp.bfloat16).reshape(groups, CAP, n_seq, band, BLK)
+    block_send = jnp.transpose(slot_grads, (2, 0, 1, 3, 4)).reshape(n_seq, block_len)
+    gain_width = D // n_seq
+    per_chunk = gain_width // feat
+    head_gain = jnp.sum(contribution * scaled_full.T, axis=1)
+    head_top = lax.reduce_precision(head_gain, exponent_bits=8, mantissa_bits=7)
+    head_pair = jnp.stack([head_top, head_gain - head_top]).astype(jnp.bfloat16)
+    gain_send = jnp.transpose(head_pair.reshape(2, n_seq, gain_width), (1, 0, 2)).reshape(
+        n_seq, 2 * gain_width
+    )
+    gain_pad = -(-(2 * gain_width) // 128) * 128 - 2 * gain_width
+    seq_recv = lax.all_to_all(
+        jnp.concatenate(
+            [block_send, gain_send, jnp.zeros((n_seq, gain_pad), jnp.bfloat16)], axis=1
+        ),
         "seq",
+        split_axis=0,
+        concat_axis=0,
+        tiled=True,
+    )
+    seq_sum = jnp.sum(seq_recv.astype(jnp.float32), axis=0)
+    block_chunk = seq_sum[:block_len].astype(jnp.bfloat16).reshape(groups, band_len)
+    gain_chunk = (
+        seq_sum[block_len : block_len + gain_width]
+        + seq_sum[block_len + gain_width : block_len + 2 * gain_width]
+    )
+    chunk_top = lax.reduce_precision(gain_chunk, exponent_bits=8, mantissa_bits=7)
+    chunk_pair = jnp.stack([chunk_top, gain_chunk - chunk_top]).astype(jnp.bfloat16)
+    chunk_dest = jnp.transpose(chunk_pair.reshape(2, per_chunk, feat), (1, 0, 2)).reshape(
+        per_chunk, 2 * feat
+    )
+    gain_slots = lax.dynamic_update_slice(
+        jnp.zeros((groups, 2 * feat), jnp.bfloat16), chunk_dest, (slab_index * per_chunk, 0)
+    )
+    slot_pad = -(-(2 * feat) // 128) * 128 - 2 * feat
+    wt_recv = lax.all_to_all(
+        jnp.concatenate(
+            [block_chunk, gain_slots, jnp.zeros((groups, slot_pad), jnp.bfloat16)], axis=1
+        ),
+        "wt",
+        split_axis=0,
+        concat_axis=0,
+        tiled=True,
+    )
+    returned = wt_recv[:, :band_len].reshape(groups * CAP, band, BLK)
+    owned_band = jnp.concatenate([returned, jnp.zeros((1, band, BLK), jnp.bfloat16)], axis=0)[
+        slot_dest
+    ]
+    gain_recv = wt_recv[:, band_len : band_len + 2 * feat].astype(jnp.float32)
+    gain_mine = jnp.sum(gain_recv[:, :feat] + gain_recv[:, feat:], axis=0)
+    mine_top = lax.reduce_precision(gain_mine, exponent_bits=8, mantissa_bits=7)
+    mine_pair = jnp.stack([mine_top, gain_mine - mine_top]).astype(jnp.bfloat16).reshape(-1)
+    owned_len = slots * band * BLK
+    send_len = -(-(owned_len + 2 * feat) // 1024) * 1024
+    gather_send = jnp.concatenate(
+        [
+            owned_band.reshape(-1),
+            mine_pair,
+            jnp.zeros((send_len - owned_len - 2 * feat,), jnp.bfloat16),
+        ]
+    ).reshape(send_len // 128, 128)
+    gathered_back = lax.all_gather(gather_send, "seq", axis=0, tiled=True).reshape(
+        n_seq, send_len
+    )
+    block_grads = jnp.transpose(
+        gathered_back[:, :owned_len].reshape(n_seq, slots, band, BLK), (1, 0, 2, 3)
+    ).reshape(slots, BLK, BLK)
+    gain_total = jnp.sum(
+        gathered_back[:, owned_len : owned_len + feat].astype(jnp.float32)
+        + gathered_back[:, owned_len + feat : owned_len + 2 * feat].astype(jnp.float32),
         axis=0,
-        tiled=True,
-    )
-    block_grads = gathered_back[:, :chunk].reshape(slots, BLK, BLK)
-    gain_total = jnp.sum(gathered_back[:, chunk : chunk + feat].astype(jnp.float32), axis=0)
+    )
     return (attn_rows, tokens_grad, gain_total, block_grads[None])
 
 

time: 545 us -> 495 us (0.908); the launches traced: 543 us -> 485 us
  waiting for transfers between devices: 365 us -> 275 us
  local copies, waits for them, and re-layouts: 44.3 us -> 61.2 us
  other arithmetic: 16.3 us -> 27.6 us
    all_gather x1, waiting for transfers between devices: 104 us -> 27.9 us  [body(): lax.all_gather(gather_send, 'seq', axis=0, tiled=True)]
    reduce_scatter x1 -> x0, waiting for transfers between devices: 51.1 us -> none  [body(): lax.psum_scatter(owned_grads, 'seq', scatter_dimension=0, tiled=True)]
    all_to_all x1 -> x2, waiting for transfers between devices: 37.7 us -> 56.4 us  [the longest x1 49 us: body(): lax.all_to_all(jnp.concatenate([block_send, gain_send, jnp.zeros((n_seq,...]
    unnamed x25 -> x33, local copies, waits for them, and re-layouts: 7.28 us -> 25.1 us
    all_to_all x1 -> x2, starting transfers between devices: 7.76 us -> 23.4 us  [the longest x1 16 us: body(): lax.all_to_all(jnp.concatenate([block_send, gain_send, jnp.zeros((n_seq,...]
    all_to_all x1, waiting for transfers between devices: 64.9 us -> 78.1 us  [body(): lax.all_to_all(packed.reshape(groups, feat + pad_rows, tok_rows), 'wt', s...]
    ppermute x16, starting transfers between devices: 48.9 us -> 37.1 us  [shifted(): lax.ppermute(value, axis, [(source, source + steps) for source in range(i...]
    reduce_sum x2 -> x3, other arithmetic: 1.37 us -> 7.92 us  [the longest x1 7.17 us: body(): seq_sum = jnp.sum(seq_recv.astype(jnp.float32), axis=0)]
  transfers between devices with their start and end apart: 25 -> 25, of which waited for: 16 -> 14; matrix products, arithmetic and copies ran while one was open for 7% -> 7% of each run, Pallas kernels for 0% -> 0%
where the time goes in v4:
time: 495 us; the launch traced here: 485 us
  waiting for transfers between devices  275 us (56%)
  starting transfers between devices  91.3 us (18%)
  local copies, waits for them, and re-layouts  61.2 us (12%)
  other arithmetic  27.6 us (6%)
  between operations  15.3 us (3%)
  matrix products  14.6 us (3%)
    all_to_all x1, waiting for transfers between devices, body(): lax.all_to_all(packed.reshape(groups, feat + pad_rows, tok_rows), 'wt', s...  78.1 us
    all_to_all x1, waiting for transfers between devices, body(): lax.all_to_all(outgoing[:dump_slot].reshape(groups, CAP, BLK, BLK), 'wt',...  51 us
    all_to_all x1, waiting for transfers between devices, body(): lax.all_to_all(jnp.concatenate([block_send, gain_send, jnp.zeros((n_seq,...  49 us
    ppermute x16, waiting for transfers between devices, shifted(): lax.ppermute(value, axis, [(source, source + steps) for source in range(i...  46.1 us
    ppermute x16, starting transfers between devices, shifted(): lax.ppermute(value, axis, [(source, source + steps) for source in range(i...  37.1 us
    all_gather x1, waiting for transfers between devices, body(): lax.all_gather(gather_send, 'seq', axis=0, tiled=True)  27.9 us
    unnamed x33, local copies, waits for them, and re-layouts  25.1 us
    all_to_all x1, starting transfers between devices, body(): lax.all_to_all(jnp.concatenate([block_send, gain_send, jnp.zeros((n_seq,...  16 us
  transfers between devices with their start and end apart: 25, of which 14 were waited for; matrix products, arithmetic and copies ran while one was open for 7% of the time, Pallas kernels for 0%

profile of v4, /device:TPU:6, one launch (start us, length us, event | category | flops | bytes accessed | tf_op | source)
XLA Modules:
  0.0 485.4 jit_solution(15301146922401039207)
XLA Ops:
  11.1 10.2 %all-to-all-start = ((bf16[32,1,2]{2,1,0:T(2,128)(2,1)}), bf16[32,1,2]{2,1,0:T(2,128)(2,1)S(1)}, u32[]{:S(2)}, u32[]{:S(2)}) async-start(bf16[32,1,2]{2,1,0:T(2,128)(2,1)} %all_to_all.35), calls=%async_computation | async-start | bytes 32768 | tf_op jit(solution)/shard_map/all_to_all | solution.py:99
  21.8 6.6 %scatter_fusion = bf16[65,128,128]{2,1,0:T(8,128)(2,1)S(1)} fusion(bf16[65,128,128]{2,1,0:T(8,128)(2,1)S(1)} %broadcast_in_dim.37, s32[64]{0:T(128)S(1)} %fusion.65, bf16[64,128,128]{2,1,0:T(8,128)(2,1)} %bitcast.147), kind=kCustom, calls=%fused_computation.3 | custom fusion | bytes 6291712 | tf_op jit(solution)/shard_map/scatter | solution.py:84
  28.5 1.5 slice.346
  29.9 9.9 %all-to-all-start.1 = ((bf16[32,2,128,128]{3,2,1,0:T(8,128)(2,1)}), bf16[32,2,128,128]{3,2,1,0:T(8,128)(2,1)S(1)}, u32[]{:S(2)}, u32[]{:S(2)}) async-start(bf16[32,2,128,128]{3,2,1,0:T(8,128)(2,1)} %bitcast.140), calls=%async_computation.1 | async-start | bytes 4194304 | tf_op jit(solution)/shard_map/all_to_all | solution.py:92
  41.5 51.0 %all-to-all-done.1 = bf16[32,2,128,128]{3,2,1,0:T(8,128)(2,1)S(1)} async-done(((bf16[32,2,128,128]{3,2,1,0:T(8,128)(2,1)}), bf16[32,2,128,128]{3,2,1,0:T(8,128)(2,1)S(1)}, u32[]{:S(2)}, u32[]{:S(2)}) %all-to-all-start.1) | async-done | bytes 2097184 | tf_op jit(solution)/shard_map/all_to_all | solution.py:92
  92.5 1.3 copy-done.2
  94.4 6.7 %scatter_fusion.1 = bf16[73,128,128]{2,1,0:T(8,128)(2,1)S(1)} fusion(bf16[73,128,128]{2,1,0:T(8,128)(2,1)S(1)} %broadcast_in_dim.34, s32[64]{0:T(128)S(1)} %fusion.66, bf16[64,128,128]{2,1,0:T(8,128)(2,1)} %bitcast.139), kind=kCustom, calls=%fused_computation.4 | custom fusion | bytes 6291712 | tf_op jit(solution)/shard_map/scatter | solution.py:136
  101.1 1.6 fusion.82
  102.7 15.7 %all-gather.3.cloned.1.call-done = bf16[232,4608]{0,1:T(8,128)(2,1)} async-done(((bf16[232,144]{0,1:T(8,128)(2,1)}), bf16[232,4608]{0,1:T(8,128)(2,1)}) %all-gather.3.cloned.1.call-update) | async-done | bytes 2138128 | tf_op jit(solution)/shard_map/all_gather | solution.py:113
  118.4 2.8 copy.55
  121.7 1.6 slice_convert_fusion
  123.4 2.2 fusion.14
  127.0 2.1 collective-permute-start
  130.2 3.8 collective-permute-start.1
  134.6 3.6 collective-permute-start.2
  138.2 4.2 collective-permute-start.3
  142.4 4.9 %collective-permute-start.4 = (bf16[224,256]{1,0:T(8,128)(2,1)S(1)}, bf16[224,256]{1,0:T(8,128)(2,1)S(1)}, u32[]{:S(2)}, u32[]{:S(2)}) collective-permute-start(bf16[224,256]{1,0:T(8,128)(2,1)S(1)} %pad_maximum_fusion.1), channel_id=1, source_target_pairs={{0,128},{32,160},{64,192},{96,224},{128,256},{160,288},{192,320},{... | collective-permute-start | bytes 344072 | tf_op jit(solution)/shard_map/ppermute | solution.py:30
  147.4 4.1 collective-permute-start.5
  151.5 1.3 collective-permute-start.6
  152.9 1.8 collective-permute-start.7
  154.7 3.1 collective-permute-start.8
  157.8 5.5 %collective-permute-done.4 = bf16[224,256]{1,0:T(8,128)(2,1)S(1)} collective-permute-done((bf16[224,256]{1,0:T(8,128)(2,1)S(1)}, bf16[224,256]{1,0:T(8,128)(2,1)S(1)}, u32[]{:S(2)}, u32[]{:S(2)}) %collective-permute-start.4) | collective-permute-done | bytes 114720 | tf_op jit(solution)/shard_map/ppermute | solution.py:30
  163.4 2.4 collective-permute-done.6
  165.9 2.0 collective-permute-done.8
  167.9 1.1 fusion.80
  170.0 1.4 multiply_reduce_fusion
  171.4 1.1 fusion.13
  173.5 1.3 collective-permute-start.9
  174.9 1.3 collective-permute-start.10
  176.2 1.3 collective-permute-start.11
  177.5 1.3 collective-permute-start.12
  178.8 1.3 collective-permute-start.13
  180.8 1.3 collective-permute-start.14
  182.1 5.0 %collective-permute-done.10 = bf16[224,256]{1,0:T(8,128)(2,1)S(1)} collective-permute-done((bf16[224,256]{1,0:T(8,128)(2,1)S(1)}, bf16[224,256]{1,0:T(8,128)(2,1)S(1)}, u32[]{:S(2)}, u32[]{:S(2)}) %collective-permute-start.10) | collective-permute-done | bytes 114720 | tf_op jit(solution)/shard_map/ppermute | solution.py:30
  187.1 1.3 collective-permute-start.15
  188.4 1.8 collective-permute-done.11
  190.3 1.3 collective-permute-start.16
  192.3 18.6 %collective-permute-done.12 = bf16[224,256]{1,0:T(8,128)(2,1)S(1)} collective-permute-done((bf16[224,256]{1,0:T(8,128)(2,1)S(1)}, bf16[224,256]{1,0:T(8,128)(2,1)S(1)}, u32[]{:S(2)}, u32[]{:S(2)}) %collective-permute-start.12) | collective-permute-done | bytes 114720 | tf_op jit(solution)/shard_map/ppermute | solution.py:30
  211.0 10.7 %collective-permute-done.14 = bf16[224,256]{1,0:T(8,128)(2,1)S(1)} collective-permute-done((bf16[224,256]{1,0:T(8,128)(2,1)S(1)}, bf16[224,256]{1,0:T(8,128)(2,1)S(1)}, u32[]{:S(2)}, u32[]{:S(2)}) %collective-permute-start.14) | collective-permute-done | bytes 114720 | tf_op jit(solution)/shard_map/ppermute | solution.py:30
  222.0 2.1 collective-permute-start.17
  224.1 2.0 fusion.74
  226.7 1.9 fusion.72
  228.6 2.8 fusion.7
  231.7 1.9 maximum_maximum_fusion
  233.6 2.1 gather_fusion
  235.7 2.1 copy.49
  237.9 1.2 bitcast_dynamic-update-slice_fusion
  239.7 1.3 copy-done.1
  241.5 3.9 reduce.7
  245.4 3.2 reshape.389
  248.6 16.0 %all-to-all-start.3 = ((bf16[16,2,33088]{2,1,0:T(2,128)(2,1)}), bf16[16,2,33088]{2,1,0:T(2,128)(2,1)}, u32[]{:S(2)}, u32[]{:S(2)}) async-start(bf16[16,2,33088]{2,1,0:T(2,128)(2,1)} %reshape.389), calls=%async_computation.3 | async-start | bytes 4243456 | tf_op jit(solution)/shard_map/all_to_all | solution.py:264
  264.7 2.8 copy.48
  267.4 49.0 %all-to-all-done.3 = bf16[16,2,33088]{2,1,0:T(2,128)(2,1)} async-done(((bf16[16,2,33088]{2,1,0:T(2,128)(2,1)}), bf16[16,2,33088]{2,1,0:T(2,128)(2,1)}, u32[]{:S(2)}, u32[]{:S(2)}) %all-to-all-start.3) | async-done | bytes 2117664 | tf_op jit(solution)/shard_map/all_to_all | solution.py:264
  316.5 13.2 %reshape.390 = bf16[16,1,66176]{2,1,0:T(2,128)(2,1)} reshape(bf16[16,2,33088]{2,1,0:T(2,128)(2,1)} %all-to-all-done.3) | data formatting | bytes 4235264
  329.7 7.2 %convert_reduce_fusion.1 = f32[66176]{0:T(1024)S(1)} fusion(bf16[16,1,66176]{2,1,0:T(2,128)(2,1)} %reshape.390), kind=kLoop, calls=%fused_computation.14 | loop fusion | flops 2051456 | bytes 2382336 | tf_op jit(solution)/shard_map/reduce_sum | solution.py:273
  338.9 7.5 %all-to-all-start.4 = ((bf16[32,2,1216]{2,1,0:T(2,128)(2,1)}), bf16[32,2,1216]{2,1,0:T(2,128)(2,1)S(1)}, u32[]{:S(2)}, u32[]{:S(2)}) async-start(bf16[32,2,1216]{2,1,0:T(2,128)(2,1)} %reshape.391), calls=%async_computation.4 | async-start | bytes 327680 | tf_op jit(solution)/shard_map/all_to_all | solution.py:288
  346.5 2.0 pad_maximum_fusion
  348.5 7.3 %all-to-all-done.4 = bf16[32,2,1216]{2,1,0:T(2,128)(2,1)S(1)} async-done(((bf16[32,2,1216]{2,1,0:T(2,128)(2,1)}), bf16[32,2,1216]{2,1,0:T(2,128)(2,1)S(1)}, u32[]{:S(2)}, u32[]{:S(2)}) %all-to-all-start.4) | async-done | bytes 155680 | tf_op jit(solution)/shard_map/all_to_all | solution.py:288
  355.8 6.3 %all-to-all-start.2 = ((bf16[32,160,224]{2,1,0:T(8,128)(2,1)}), bf16[32,160,224]{2,1,0:T(8,128)(2,1)S(1)}, u32[]{:S(2)}, u32[]{:S(2)}) async-start(bf16[32,160,224]{2,1,0:T(8,128)(2,1)} %pad_maximum_fusion), calls=%async_computation.2 | async-start | bytes 5242880 | tf_op jit(solution)/shard_map/all_to_all | solution.py:223
  363.4 2.5 concatenate.100
  365.9 78.1 %all-to-all-done.2 = bf16[32,160,224]{2,1,0:T(8,128)(2,1)S(1)} async-done(((bf16[32,160,224]{2,1,0:T(8,128)(2,1)}), bf16[32,160,224]{2,1,0:T(8,128)(2,1)S(1)}, u32[]{:S(2)}, u32[]{:S(2)}) %all-to-all-start.2) | async-done | bytes 2293792 | tf_op jit(solution)/shard_map/all_to_all | solution.py:223
  445.2 27.9 %all-gather.5.cloned.1.call-done = bf16[8320,128]{1,0:T(8,128)(2,1)} async-done(((bf16[520,128]{1,0:T(8,128)(2,1)}), bf16[8320,128]{1,0:T(8,128)(2,1)}) %all-gather.5.cloned.1.call-update) | async-done | bytes 2129936 | tf_op jit(solution)/shard_map/all_gather | solution.py:314
  473.1 2.2 reshape.335
  476.4 1.9 copy.61
  (151 shorter events, 21.5 us)
Async XLA Ops:
  11.1 18.9 %all-to-all-start = ((bf16[32,1,2]{2,1,0:T(2,128)(2,1)}), bf16[32,1,2]{2,1,0:T(2,128)(2,1)S(1)}, u32[]{:S(2)}, u32[]{:S(2)}) async-start(bf16[32,1,2]{2,1,0:T(2,128)(2,1)} %all_to_all.35), calls=%async_computation | async-start | bytes 32768 | tf_op jit(solution)/shard_map/all_to_all | solution.py:99
  29.9 10.0 %copy-start.5 = (f32[144]{0:T(256)S(1)}, f32[144]{0:T(256)}, u32[]{:S(2)}) copy-start(f32[144]{0:T(256)} %param.7) | copy-start | bytes 1732
  29.9 10.3 %copy-start.4 = (bf16[224,144]{0,1:T(8,128)(2,1)S(1)}, bf16[224,144]{0,1:T(8,128)(2,1)}, u32[]{:S(2)}) copy-start(bf16[224,144]{0,1:T(8,128)(2,1)} %param.6) | copy-start | bytes 193540
  29.9 11.4 %copy-start.6 = (s32[224]{0:T(256)S(1)}, s32[224]{0:T(256)}, u32[]{:S(2)}) copy-start(s32[224]{0:T(256)} %param.8) | copy-start | bytes 2692
  29.9 62.6 %all-to-all-start.1 = ((bf16[32,2,128,128]{3,2,1,0:T(8,128)(2,1)}), bf16[32,2,128,128]{3,2,1,0:T(8,128)(2,1)S(1)}, u32[]{:S(2)}, u32[]{:S(2)}) async-start(bf16[32,2,128,128]{3,2,1,0:T(8,128)(2,1)} %bitcast.140), calls=%async_computation.1 | async-start | bytes 4194304 | tf_op jit(solution)/shard_map/all_to_all | solution.py:92
  39.9 78.5 %all-gather.3.cloned.1.call-start = ((), (), s32[]{:S(2)}) async-start(), calls=%async_computation.5 | async-start | bytes 2433024 | tf_op jit(solution)/shard_map/all_gather | solution.py:113
  92.5 1.3 copy-start.2
  123.4 2.2 copy-start.3
  125.6 3.6 copy-start
  127.0 3.1 collective-permute-start
  130.2 21.3 %collective-permute-start.1 = (bf16[224,256]{1,0:T(8,128)(2,1)S(1)}, bf16[224,256]{1,0:T(8,128)(2,1)S(1)}, u32[]{:S(2)}, u32[]{:S(2)}) collective-permute-start(bf16[224,256]{1,0:T(8,128)(2,1)S(1)} %pad_maximum_fusion.1), channel_id=1, source_target_pairs={{0,32},{32,64},{64,96},{96,128},{128,160},{160,192},{192,224},{224... | collective-permute-start | bytes 344072 | tf_op jit(solution)/shard_map/ppermute | solution.py:30
  134.6 18.3 %collective-permute-start.2 = (bf16[224,256]{1,0:T(8,128)(2,1)S(1)}, bf16[224,256]{1,0:T(8,128)(2,1)S(1)}, u32[]{:S(2)}, u32[]{:S(2)}) collective-permute-start(bf16[224,256]{1,0:T(8,128)(2,1)S(1)} %pad_maximum_fusion.1), channel_id=1, source_target_pairs={{0,64},{32,96},{64,128},{96,160},{128,192},{160,224},{192,256},{22... | collective-permute-start | bytes 344072 | tf_op jit(solution)/shard_map/ppermute | solution.py:30
  138.2 16.5 %collective-permute-start.3 = (bf16[224,256]{1,0:T(8,128)(2,1)S(1)}, bf16[224,256]{1,0:T(8,128)(2,1)S(1)}, u32[]{:S(2)}, u32[]{:S(2)}) collective-permute-start(bf16[224,256]{1,0:T(8,128)(2,1)S(1)} %pad_maximum_fusion.1), channel_id=1, source_target_pairs={{0,96},{32,128},{64,160},{96,192},{128,224},{160,256},{192,288},{2... | collective-permute-start | bytes 344072 | tf_op jit(solution)/shard_map/ppermute | solution.py:30
  142.4 20.9 %collective-permute-start.4 = (bf16[224,256]{1,0:T(8,128)(2,1)S(1)}, bf16[224,256]{1,0:T(8,128)(2,1)S(1)}, u32[]{:S(2)}, u32[]{:S(2)}) collective-permute-start(bf16[224,256]{1,0:T(8,128)(2,1)S(1)} %pad_maximum_fusion.1), channel_id=1, source_target_pairs={{0,128},{32,160},{64,192},{96,224},{128,256},{160,288},{192,320},{... | collective-permute-start | bytes 344072 | tf_op jit(solution)/shard_map/ppermute | solution.py:30
  147.4 16.0 %collective-permute-start.5 = (bf16[224,256]{1,0:T(8,128)(2,1)S(1)}, bf16[224,256]{1,0:T(8,128)(2,1)S(1)}, u32[]{:S(2)}, u32[]{:S(2)}) collective-permute-start(bf16[224,256]{1,0:T(8,128)(2,1)S(1)} %pad_maximum_fusion.1), channel_id=1, source_target_pairs={{0,160},{32,192},{64,224},{96,256},{128,288},{160,320},{192,352},{... | collective-permute-start | bytes 344072 | tf_op jit(solution)/shard_map/ppermute | solution.py:30
  151.5 14.3 %collective-permute-start.6 = (bf16[224,256]{1,0:T(8,128)(2,1)S(1)}, bf16[224,256]{1,0:T(8,128)(2,1)S(1)}, u32[]{:S(2)}, u32[]{:S(2)}) collective-permute-start(bf16[224,256]{1,0:T(8,128)(2,1)S(1)} %pad_maximum_fusion.1), channel_id=1, source_target_pairs={{0,192},{32,224},{64,256},{96,288},{128,320},{160,352},{192,384},{... | collective-permute-start | bytes 344072 | tf_op jit(solution)/shard_map/ppermute | solution.py:30
  152.9 13.0 %collective-permute-start.7 = (bf16[224,256]{1,0:T(8,128)(2,1)S(1)}, bf16[224,256]{1,0:T(8,128)(2,1)S(1)}, u32[]{:S(2)}, u32[]{:S(2)}) collective-permute-start(bf16[224,256]{1,0:T(8,128)(2,1)S(1)} %pad_maximum_fusion.1), channel_id=1, source_target_pairs={{0,224},{32,256},{64,288},{96,320},{128,352},{160,384},{192,416},{... | collective-permute-start | bytes 344072 | tf_op jit(solution)/shard_map/ppermute | solution.py:30
  154.7 13.1 %collective-permute-start.8 = (bf16[224,256]{1,0:T(8,128)(2,1)S(1)}, bf16[224,256]{1,0:T(8,128)(2,1)S(1)}, u32[]{:S(2)}, u32[]{:S(2)}) collective-permute-start(bf16[224,256]{1,0:T(8,128)(2,1)S(1)} %pad_maximum_fusion.1), channel_id=1, source_target_pairs={{0,256},{32,288},{64,320},{96,352},{128,384},{160,416},{192,448},{... | collective-permute-start | bytes 344072 | tf_op jit(solution)/shard_map/ppermute | solution.py:30
  167.9 1.1 copy-start.7
  173.5 7.3 %collective-permute-start.9 = (bf16[224,256]{1,0:T(8,128)(2,1)S(1)}, bf16[224,256]{1,0:T(8,128)(2,1)S(1)}, u32[]{:S(2)}, u32[]{:S(2)}) collective-permute-start(bf16[224,256]{1,0:T(8,128)(2,1)S(1)} %pad_maximum_fusion.2), channel_id=1, source_target_pairs={{32,0},{64,32},{96,64},{128,96},{160,128},{192,160},{224,192},{256... | collective-permute-start | bytes 344072 | tf_op jit(solution)/shard_map/ppermute | solution.py:30
  174.9 12.3 %collective-permute-start.10 = (bf16[224,256]{1,0:T(8,128)(2,1)S(1)}, bf16[224,256]{1,0:T(8,128)(2,1)S(1)}, u32[]{:S(2)}, u32[]{:S(2)}) collective-permute-start(bf16[224,256]{1,0:T(8,128)(2,1)S(1)} %pad_maximum_fusion.3), channel_id=1, source_target_pairs={{64,0},{96,32},{128,64},{160,96},{192,128},{224,160},{256,192},{28... | collective-permute-start | bytes 344072 | tf_op jit(solution)/shard_map/ppermute | solution.py:30
  176.2 14.1 %collective-permute-start.11 = (bf16[224,256]{1,0:T(8,128)(2,1)S(1)}, bf16[224,256]{1,0:T(8,128)(2,1)S(1)}, u32[]{:S(2)}, u32[]{:S(2)}) collective-permute-start(bf16[224,256]{1,0:T(8,128)(2,1)S(1)} %pad_maximum_fusion.4), channel_id=1, source_target_pairs={{96,0},{128,32},{160,64},{192,96},{224,128},{256,160},{288,192},{3... | collective-permute-start | bytes 344072 | tf_op jit(solution)/shard_map/ppermute | solution.py:30
  177.5 33.4 %collective-permute-start.12 = (bf16[224,256]{1,0:T(8,128)(2,1)S(1)}, bf16[224,256]{1,0:T(8,128)(2,1)S(1)}, u32[]{:S(2)}, u32[]{:S(2)}) collective-permute-start(bf16[224,256]{1,0:T(8,128)(2,1)S(1)} %pad_maximum_fusion.5), channel_id=1, source_target_pairs={{128,0},{160,32},{192,64},{224,96},{256,128},{288,160},{320,192},{... | collective-permute-start | bytes 344072 | tf_op jit(solution)/shard_map/ppermute | solution.py:30
  178.8 32.1 %collective-permute-start.13 = (bf16[224,256]{1,0:T(8,128)(2,1)S(1)}, bf16[224,256]{1,0:T(8,128)(2,1)S(1)}, u32[]{:S(2)}, u32[]{:S(2)}) collective-permute-start(bf16[224,256]{1,0:T(8,128)(2,1)S(1)} %pad_maximum_fusion.6), channel_id=1, source_target_pairs={{160,0},{192,32},{224,64},{256,96},{288,128},{320,160},{352,192},{... | collective-permute-start | bytes 344072 | tf_op jit(solution)/shard_map/ppermute | solution.py:30
  180.8 40.9 %collective-permute-start.14 = (bf16[224,256]{1,0:T(8,128)(2,1)S(1)}, bf16[224,256]{1,0:T(8,128)(2,1)S(1)}, u32[]{:S(2)}, u32[]{:S(2)}) collective-permute-start(bf16[224,256]{1,0:T(8,128)(2,1)S(1)} %pad_maximum_fusion.7), channel_id=1, source_target_pairs={{192,0},{224,32},{256,64},{288,96},{320,128},{352,160},{384,192},{... | collective-permute-start | bytes 344072 | tf_op jit(solution)/shard_map/ppermute | solution.py:30
  187.1 34.6 %collective-permute-start.15 = (bf16[224,256]{1,0:T(8,128)(2,1)S(1)}, bf16[224,256]{1,0:T(8,128)(2,1)S(1)}, u32[]{:S(2)}, u32[]{:S(2)}) collective-permute-start(bf16[224,256]{1,0:T(8,128)(2,1)S(1)} %pad_maximum_fusion.8), channel_id=1, source_target_pairs={{224,0},{256,32},{288,64},{320,96},{352,128},{384,160},{416,192},{... | collective-permute-start | bytes 344072 | tf_op jit(solution)/shard_map/ppermute | solution.py:30
  190.3 31.5 %collective-permute-start.16 = (bf16[224,256]{1,0:T(8,128)(2,1)S(1)}, bf16[224,256]{1,0:T(8,128)(2,1)S(1)}, u32[]{:S(2)}, u32[]{:S(2)}) collective-permute-start(bf16[224,256]{1,0:T(8,128)(2,1)S(1)} %pad_maximum_fusion.9), channel_id=1, source_target_pairs={{256,0},{288,32},{320,64},{352,96},{384,128},{416,160},{448,192},{... | collective-permute-start | bytes 344072 | tf_op jit(solution)/shard_map/ppermute | solution.py:30
  222.0 4.1 collective-permute-start.17
  239.7 1.3 copy-start.1
  248.6 67.9 %all-to-all-start.3 = ((bf16[16,2,33088]{2,1,0:T(2,128)(2,1)}), bf16[16,2,33088]{2,1,0:T(2,128)(2,1)}, u32[]{:S(2)}, u32[]{:S(2)}) async-start(bf16[16,2,33088]{2,1,0:T(2,128)(2,1)} %reshape.389), calls=%async_computation.3 | async-start | bytes 4243456 | tf_op jit(solution)/shard_map/all_to_all | solution.py:264
  338.9 16.9 %all-to-all-start.4 = ((bf16[32,2,1216]{2,1,0:T(2,128)(2,1)}), bf16[32,2,1216]{2,1,0:T(2,128)(2,1)S(1)}, u32[]{:S(2)}, u32[]{:S(2)}) async-start(bf16[32,2,1216]{2,1,0:T(2,128)(2,1)} %reshape.391), calls=%async_computation.4 | async-start | bytes 327680 | tf_op jit(solution)/shard_map/all_to_all | solution.py:288
  355.8 88.2 %all-to-all-start.2 = ((bf16[32,160,224]{2,1,0:T(8,128)(2,1)}), bf16[32,160,224]{2,1,0:T(8,128)(2,1)S(1)}, u32[]{:S(2)}, u32[]{:S(2)}) async-start(bf16[32,160,224]{2,1,0:T(8,128)(2,1)} %pad_maximum_fusion), calls=%async_computation.2 | async-start | bytes 5242880 | tf_op jit(solution)/shard_map/all_to_all | solution.py:223
  362.1 111.0 %all-gather.5.cloned.1.call-start = ((), (), s32[]{:S(2)}) async-start(), calls=%async_computation.6 | async-start | bytes 2263040 | tf_op jit(solution)/shard_map/all_gather | solution.py:314
Sparse Core Ops, SparseCore 0:
  44.4 73.9 all-gather.2
  366.0 106.9 all-gather.4

commit v5 on v4

--- a/solution.py
+++ b/solution.py
@@ -248,10 +248,12 @@
     n_seq = lax.axis_size("seq")
     band = BLK // n_seq
     slots = slot_dest.shape[0]
-    band_len = CAP * band * BLK
-    block_len = groups * band_len
-    slot_grads = grad_table[arrival].astype(jnp.bfloat16).reshape(groups, CAP, n_seq, band, BLK)
-    block_send = jnp.transpose(slot_grads, (2, 0, 1, 3, 4)).reshape(n_seq, block_len)
+    band_rows = CAP * band
+    block_rows = groups * band_rows
+    side = 16
+    block_send = jnp.transpose(
+        grad_table[arrival].reshape(groups, CAP, n_seq, band, BLK), (2, 0, 1, 3, 4)
+    ).reshape(n_seq, block_rows, BLK)
     gain_width = D // n_seq
     per_chunk = gain_width // feat
     head_gain = jnp.sum(contribution * scaled_full.T, axis=1)
@@ -260,68 +262,67 @@
     gain_send = jnp.transpose(head_pair.reshape(2, n_seq, gain_width), (1, 0, 2)).reshape(
         n_seq, 2 * gain_width
     )
-    gain_pad = -(-(2 * gain_width) // 128) * 128 - 2 * gain_width
+    gain_send = jnp.pad(gain_send, ((0, 0), (0, side * BLK - 2 * gain_width))).reshape(
+        n_seq, side, BLK
+    )
     seq_recv = lax.all_to_all(
-        jnp.concatenate(
-            [block_send, gain_send, jnp.zeros((n_seq, gain_pad), jnp.bfloat16)], axis=1
-        ),
+        jnp.concatenate([block_send.astype(jnp.bfloat16), gain_send], axis=1),
         "seq",
         split_axis=0,
         concat_axis=0,
         tiled=True,
     )
     seq_sum = jnp.sum(seq_recv.astype(jnp.float32), axis=0)
-    block_chunk = seq_sum[:block_len].astype(jnp.bfloat16).reshape(groups, band_len)
-    gain_chunk = (
-        seq_sum[block_len : block_len + gain_width]
-        + seq_sum[block_len + gain_width : block_len + 2 * gain_width]
-    )
+    block_chunk = seq_sum[:block_rows].astype(jnp.bfloat16).reshape(groups, band_rows, BLK)
+    gain_flat = seq_sum[block_rows:].reshape(-1)
+    gain_chunk = gain_flat[:gain_width] + gain_flat[gain_width : 2 * gain_width]
     chunk_top = lax.reduce_precision(gain_chunk, exponent_bits=8, mantissa_bits=7)
     chunk_pair = jnp.stack([chunk_top, gain_chunk - chunk_top]).astype(jnp.bfloat16)
     chunk_dest = jnp.transpose(chunk_pair.reshape(2, per_chunk, feat), (1, 0, 2)).reshape(
         per_chunk, 2 * feat
     )
     gain_slots = lax.dynamic_update_slice(
-        jnp.zeros((groups, 2 * feat), jnp.bfloat16), chunk_dest, (slab_index * per_chunk, 0)
-    )
-    slot_pad = -(-(2 * feat) // 128) * 128 - 2 * feat
+        jnp.zeros((groups, side * BLK), jnp.bfloat16), chunk_dest, (slab_index * per_chunk, 0)
+    ).reshape(groups, side, BLK)
     wt_recv = lax.all_to_all(
-        jnp.concatenate(
-            [block_chunk, gain_slots, jnp.zeros((groups, slot_pad), jnp.bfloat16)], axis=1
-        ),
+        jnp.concatenate([block_chunk, gain_slots], axis=1),
         "wt",
         split_axis=0,
         concat_axis=0,
         tiled=True,
     )
-    returned = wt_recv[:, :band_len].reshape(groups * CAP, band, BLK)
-    owned_band = jnp.concatenate([returned, jnp.zeros((1, band, BLK), jnp.bfloat16)], axis=0)[
+    returned = wt_recv[:, :band_rows].astype(jnp.float32).reshape(groups * CAP, band, BLK)
+    owned_band = jnp.concatenate([returned, jnp.zeros((1, band, BLK), jnp.float32)], axis=0)[
         slot_dest
     ]
-    gain_recv = wt_recv[:, band_len : band_len + 2 * feat].astype(jnp.float32)
+    gain_recv = wt_recv[:, band_rows:].reshape(groups, side * BLK)[:, : 2 * feat]
+    gain_recv = gain_recv.astype(jnp.float32)
     gain_mine = jnp.sum(gain_recv[:, :feat] + gain_recv[:, feat:], axis=0)
     mine_top = lax.reduce_precision(gain_mine, exponent_bits=8, mantissa_bits=7)
     mine_pair = jnp.stack([mine_top, gain_mine - mine_top]).astype(jnp.bfloat16).reshape(-1)
-    owned_len = slots * band * BLK
-    send_len = -(-(owned_len + 2 * feat) // 1024) * 1024
+    owned_rows = slots * band
     gather_send = jnp.concatenate(
         [
-            owned_band.reshape(-1),
-            mine_pair,
-            jnp.zeros((send_len - owned_len - 2 * feat,), jnp.bfloat16),
-        ]
-    ).reshape(send_len // 128, 128)
+            owned_band.reshape(owned_rows, BLK).astype(jnp.bfloat16),
+            jnp.pad(mine_pair, (0, side * BLK - 2 * feat)).reshape(side, BLK),
+        ],
+        axis=0,
+    )
     gathered_back = lax.all_gather(gather_send, "seq", axis=0, tiled=True).reshape(
-        n_seq, send_len
-    )
-    block_grads = jnp.transpose(
-        gathered_back[:, :owned_len].reshape(n_seq, slots, band, BLK), (1, 0, 2, 3)
-    ).reshape(slots, BLK, BLK)
-    gain_total = jnp.sum(
-        gathered_back[:, owned_len : owned_len + feat].astype(jnp.float32)
-        + gathered_back[:, owned_len + feat : owned_len + 2 * feat].astype(jnp.float32),
-        axis=0,
-    )
+        n_seq, owned_rows + side, BLK
+    )
+    block_grads = (
+        jnp.transpose(
+            gathered_back[:, :owned_rows]
+            .astype(jnp.float32)
+            .reshape(n_seq, slots, band, BLK),
+            (1, 0, 2, 3),
+        )
+        .reshape(slots, BLK, BLK)
+        .astype(jnp.bfloat16)
+    )
+    gain_back = gathered_back[:, owned_rows:].reshape(n_seq, side * BLK).astype(jnp.float32)
+    gain_total = jnp.sum(gain_back[:, :feat] + gain_back[:, feat : 2 * feat], axis=0)
     return (attn_rows, tokens_grad, gain_total, block_grads[None])
 
 

time: 495 us -> 463 us (0.935); the launches traced: 485 us -> 461 us
  local copies, waits for them, and re-layouts: 61.2 us -> 40.1 us
  other arithmetic: 27.6 us -> 21.3 us
    unnamed x33 -> x29, local copies, waits for them, and re-layouts: 25.1 us -> 4.42 us
    convert_element_type x1 -> x2, local copies, waits for them, and re-layouts: 0.06 us -> 7.14 us  [the longest x1 3.63 us: body(): block_send.astype(jnp.bfloat16)]
    reduce_sum x1, other arithmetic: 7.17 us -> 0.3 us  [body(): seq_sum = jnp.sum(seq_recv.astype(jnp.float32), axis=0)]
  transfers between devices with their start and end apart: 25 -> 25, of which waited for: 14 -> 15; matrix products, arithmetic and copies ran while one was open for 7% -> 7% of each run, Pallas kernels for 0% -> 0%
where the time goes in v5:
time: 463 us; the launch traced here: 461 us
  waiting for transfers between devices  279 us (60%)
  starting transfers between devices  90.6 us (20%)
  local copies, waits for them, and re-layouts  40.1 us (9%)
  other arithmetic  21.3 us (5%)
  between operations  15 us (3%)
  matrix products  14.5 us (3%)
    all_to_all x1, waiting for transfers between devices, body(): lax.all_to_all(packed.reshape(groups, feat + pad_rows, tok_rows), 'wt', s...  80.9 us
    all_to_all x1, waiting for transfers between devices, body(): lax.all_to_all(jnp.concatenate([block_send.astype(jnp.bfloat16), gain_sen...  52.5 us
    all_to_all x1, waiting for transfers between devices, body(): lax.all_to_all(outgoing[:dump_slot].reshape(groups, CAP, BLK, BLK), 'wt',...  51 us
    ppermute x16, waiting for transfers between devices, shifted(): lax.ppermute(value, axis, [(source, source + steps) for source in range(i...  44.4 us
    ppermute x16, starting transfers between devices, shifted(): lax.ppermute(value, axis, [(source, source + steps) for source in range(i...  36.8 us
    all_gather x1, waiting for transfers between devices, body(): lax.all_gather(gather_send, 'seq', axis=0, tiled=True)  28 us
    all_to_all x1, starting transfers between devices, body(): lax.all_to_all(jnp.concatenate([block_send.astype(jnp.bfloat16), gain_sen...  15.7 us
    all_gather x1, waiting for transfers between devices, body(): lax.all_gather(jnp.concatenate([tokens_in, gain_rows, jnp.zeros((side_row...  15.7 us
  transfers between devices with their start and end apart: 25, of which 15 were waited for; matrix products, arithmetic and copies ran while one was open for 7% of the time, Pallas kernels for 0%

profile of v5, /device:TPU:6, one launch (start us, length us, event | category | flops | bytes accessed | tf_op | source)
XLA Modules:
  0.0 460.9 jit_solution(897414447662246800)
XLA Ops:
  9.5 0.8 scatter_custom_fusion
  11.1 10.2 %all-to-all-start = ((bf16[32,1,2]{2,1,0:T(2,128)(2,1)}), bf16[32,1,2]{2,1,0:T(2,128)(2,1)S(1)}, u32[]{:S(2)}, u32[]{:S(2)}) async-start(bf16[32,1,2]{2,1,0:T(2,128)(2,1)} %all_to_all.24), calls=%async_computation | async-start | bytes 32768 | tf_op jit(solution)/shard_map/all_to_all | solution.py:99
  21.8 6.7 %scatter_fusion = bf16[65,128,128]{2,1,0:T(8,128)(2,1)S(1)} fusion(bf16[65,128,128]{2,1,0:T(8,128)(2,1)S(1)} %broadcast_in_dim.31, s32[64]{0:T(128)S(1)} %fusion.66, bf16[64,128,128]{2,1,0:T(8,128)(2,1)} %bitcast.158), kind=kCustom, calls=%fused_computation.3 | custom fusion | bytes 6291712 | tf_op jit(solution)/shard_map/scatter | solution.py:84
  28.5 1.5 slice.358
  30.0 9.9 %all-to-all-start.1 = ((bf16[32,2,128,128]{3,2,1,0:T(8,128)(2,1)}), bf16[32,2,128,128]{3,2,1,0:T(8,128)(2,1)S(1)}, u32[]{:S(2)}, u32[]{:S(2)}) async-start(bf16[32,2,128,128]{3,2,1,0:T(8,128)(2,1)} %bitcast.150), calls=%async_computation.1 | async-start | bytes 4194304 | tf_op jit(solution)/shard_map/all_to_all | solution.py:92
  40.3 0.8 concatenate.80
  41.5 51.0 %all-to-all-done.1 = bf16[32,2,128,128]{3,2,1,0:T(8,128)(2,1)S(1)} async-done(((bf16[32,2,128,128]{3,2,1,0:T(8,128)(2,1)}), bf16[32,2,128,128]{3,2,1,0:T(8,128)(2,1)S(1)}, u32[]{:S(2)}, u32[]{:S(2)}) %all-to-all-start.1) | async-done | bytes 2097184 | tf_op jit(solution)/shard_map/all_to_all | solution.py:92
  92.5 1.3 copy-done.2
  94.4 6.6 %scatter_fusion.1 = bf16[73,128,128]{2,1,0:T(8,128)(2,1)S(1)} fusion(bf16[73,128,128]{2,1,0:T(8,128)(2,1)S(1)} %broadcast_in_dim.27, s32[64]{0:T(128)S(1)} %fusion.67, bf16[64,128,128]{2,1,0:T(8,128)(2,1)} %bitcast.149), kind=kCustom, calls=%fused_computation.4 | custom fusion | bytes 6291712 | tf_op jit(solution)/shard_map/scatter | solution.py:136
  101.1 1.6 fusion.83
  102.7 15.7 %all-gather.3.cloned.1.call-done = bf16[232,4608]{0,1:T(8,128)(2,1)} async-done(((bf16[232,144]{0,1:T(8,128)(2,1)}), bf16[232,4608]{0,1:T(8,128)(2,1)}) %all-gather.3.cloned.1.call-update) | async-done | bytes 2138128 | tf_op jit(solution)/shard_map/all_gather | solution.py:113
  118.4 2.8 copy.55
  121.7 1.6 slice_convert_fusion
  123.4 2.2 fusion.14
  125.6 0.8 fusion.77
  127.0 2.1 collective-permute-start
  129.1 0.8 fusion.79
  130.2 3.8 collective-permute-start.1
  134.6 3.6 collective-permute-start.2
  138.1 4.2 collective-permute-start.3
  142.4 4.9 %collective-permute-start.4 = (bf16[224,256]{1,0:T(8,128)(2,1)S(1)}, bf16[224,256]{1,0:T(8,128)(2,1)S(1)}, u32[]{:S(2)}, u32[]{:S(2)}) collective-permute-start(bf16[224,256]{1,0:T(8,128)(2,1)S(1)} %pad_maximum_fusion.4), channel_id=1, source_target_pairs={{0,128},{32,160},{64,192},{96,224},{128,256},{160,288},{192,320},{... | collective-permute-start | bytes 344072 | tf_op jit(solution)/shard_map/ppermute | solution.py:30
  147.4 4.1 collective-permute-start.5
  151.5 1.3 collective-permute-start.6
  152.9 1.8 collective-permute-start.7
  154.7 2.8 collective-permute-start.8
  157.5 5.8 %collective-permute-done.4 = bf16[224,256]{1,0:T(8,128)(2,1)S(1)} collective-permute-done((bf16[224,256]{1,0:T(8,128)(2,1)S(1)}, bf16[224,256]{1,0:T(8,128)(2,1)S(1)}, u32[]{:S(2)}, u32[]{:S(2)}) %collective-permute-start.4) | collective-permute-done | bytes 114720 | tf_op jit(solution)/shard_map/ppermute | solution.py:30
  163.4 2.4 collective-permute-done.6
  165.9 2.0 collective-permute-done.8
  167.9 1.1 fusion.81
  169.0 1.0 fusion.87
  170.0 1.4 multiply_reduce_fusion
  171.4 1.1 fusion.13
  173.5 1.3 collective-permute-start.9
  174.9 1.3 collective-permute-start.10
  176.2 1.3 collective-permute-start.11
  177.5 1.3 collective-permute-start.12
  178.8 1.3 collective-permute-start.13
  180.8 1.3 collective-permute-start.14
  182.1 5.0 %collective-permute-done.10 = bf16[224,256]{1,0:T(8,128)(2,1)S(1)} collective-permute-done((bf16[224,256]{1,0:T(8,128)(2,1)S(1)}, bf16[224,256]{1,0:T(8,128)(2,1)S(1)}, u32[]{:S(2)}, u32[]{:S(2)}) %collective-permute-start.10) | collective-permute-done | bytes 114720 | tf_op jit(solution)/shard_map/ppermute | solution.py:30
  187.1 1.3 collective-permute-start.15
  188.4 1.8 collective-permute-done.11
  190.3 1.3 collective-permute-start.16
  191.5 2.6 fusion.90
  194.2 16.6 %collective-permute-done.12 = bf16[224,256]{1,0:T(8,128)(2,1)S(1)} collective-permute-done((bf16[224,256]{1,0:T(8,128)(2,1)S(1)}, bf16[224,256]{1,0:T(8,128)(2,1)S(1)}, u32[]{:S(2)}, u32[]{:S(2)}) %collective-permute-start.12) | collective-permute-done | bytes 114720 | tf_op jit(solution)/shard_map/ppermute | solution.py:30
  210.9 10.7 %collective-permute-done.14 = bf16[224,256]{1,0:T(8,128)(2,1)S(1)} collective-permute-done((bf16[224,256]{1,0:T(8,128)(2,1)S(1)}, bf16[224,256]{1,0:T(8,128)(2,1)S(1)}, u32[]{:S(2)}, u32[]{:S(2)}) %collective-permute-start.14) | collective-permute-done | bytes 114720 | tf_op jit(solution)/shard_map/ppermute | solution.py:30
  221.9 1.9 collective-permute-start.17
  223.8 0.9 fusion.75
  225.7 0.9 fusion.73
  226.6 1.7 maximum_maximum_fusion
  228.4 3.8 gather_fusion
  232.2 3.6 copy.52
  235.8 2.8 fusion.7
  238.9 3.1 pad_maximum_fusion.1
  242.0 15.7 %all-to-all-start.3 = ((bf16[16,528,128]{2,1,0:T(8,128)(2,1)}), bf16[16,528,128]{2,1,0:T(8,128)(2,1)S(1)}, u32[]{:S(2)}, u32[]{:S(2)}) async-start(bf16[16,528,128]{2,1,0:T(8,128)(2,1)} %pad_maximum_fusion.1), calls=%async_computation.3 | async-start | bytes 4325376 | tf_op jit(solution)/shard_map/all_to_all | solution.py:268
  257.9 52.5 %all-to-all-done.3 = bf16[16,528,128]{2,1,0:T(8,128)(2,1)S(1)} async-done(((bf16[16,528,128]{2,1,0:T(8,128)(2,1)}), bf16[16,528,128]{2,1,0:T(8,128)(2,1)S(1)}, u32[]{:S(2)}, u32[]{:S(2)}) %all-to-all-start.3) | async-done | bytes 2162720 | tf_op jit(solution)/shard_map/all_to_all | solution.py:268
  312.2 7.4 %all-to-all-start.4 = ((bf16[32,32,128]{2,1,0:T(8,128)(2,1)}), bf16[32,32,128]{2,1,0:T(8,128)(2,1)S(1)}, u32[]{:S(2)}, u32[]{:S(2)}) async-start(bf16[32,32,128]{2,1,0:T(8,128)(2,1)} %pad_maximum_fusion.2), calls=%async_computation.4 | async-start | bytes 524288 | tf_op jit(solution)/shard_map/all_to_all | solution.py:287
  319.6 2.8 copy.51
  322.5 2.0 pad_maximum_fusion
  324.5 6.4 %all-to-all-done.4 = bf16[32,32,128]{2,1,0:T(8,128)(2,1)S(1)} async-done(((bf16[32,32,128]{2,1,0:T(8,128)(2,1)}), bf16[32,32,128]{2,1,0:T(8,128)(2,1)S(1)}, u32[]{:S(2)}, u32[]{:S(2)}) %all-to-all-start.4) | async-done | bytes 262176 | tf_op jit(solution)/shard_map/all_to_all | solution.py:287
  330.9 6.3 %all-to-all-start.2 = ((bf16[32,160,224]{2,1,0:T(8,128)(2,1)}), bf16[32,160,224]{2,1,0:T(8,128)(2,1)S(1)}, u32[]{:S(2)}, u32[]{:S(2)}) async-start(bf16[32,160,224]{2,1,0:T(8,128)(2,1)} %pad_maximum_fusion), calls=%async_computation.2 | async-start | bytes 5242880 | tf_op jit(solution)/shard_map/all_to_all | solution.py:223
  338.9 80.9 %all-to-all-done.2 = bf16[32,160,224]{2,1,0:T(8,128)(2,1)S(1)} async-done(((bf16[32,160,224]{2,1,0:T(8,128)(2,1)}), bf16[32,160,224]{2,1,0:T(8,128)(2,1)S(1)}, u32[]{:S(2)}, u32[]{:S(2)}) %all-to-all-start.2) | async-done | bytes 2293792 | tf_op jit(solution)/shard_map/all_to_all | solution.py:223
  421.0 28.0 %all-gather.5.cloned.1.call-done = bf16[8448,128]{1,0:T(8,128)(2,1)} async-done(((bf16[528,128]{1,0:T(8,128)(2,1)}), bf16[8448,128]{1,0:T(8,128)(2,1)}) %all-gather.5.cloned.1.call-update) | async-done | bytes 2162704 | tf_op jit(solution)/shard_map/all_gather | solution.py:311
  449.0 3.5 copy_bitcast_fusion
  452.5 0.9 slice_convert_fusion.2
  (141 shorter events, 15.7 us)
Async XLA Ops:
  11.1 18.9 %all-to-all-start = ((bf16[32,1,2]{2,1,0:T(2,128)(2,1)}), bf16[32,1,2]{2,1,0:T(2,128)(2,1)S(1)}, u32[]{:S(2)}, u32[]{:S(2)}) async-start(bf16[32,1,2]{2,1,0:T(2,128)(2,1)} %all_to_all.24), calls=%async_computation | async-start | bytes 32768 | tf_op jit(solution)/shard_map/all_to_all | solution.py:99
  29.9 10.0 %copy-start.5 = (f32[144]{0:T(256)S(1)}, f32[144]{0:T(256)}, u32[]{:S(2)}) copy-start(f32[144]{0:T(256)} %param.7) | copy-start | bytes 1732
  29.9 10.3 %copy-start.4 = (bf16[224,144]{0,1:T(8,128)(2,1)S(1)}, bf16[224,144]{0,1:T(8,128)(2,1)}, u32[]{:S(2)}) copy-start(bf16[224,144]{0,1:T(8,128)(2,1)} %param.6) | copy-start | bytes 193540
  29.9 11.4 %copy-start.6 = (s32[224]{0:T(256)S(1)}, s32[224]{0:T(256)}, u32[]{:S(2)}) copy-start(s32[224]{0:T(256)} %param.8) | copy-start | bytes 2692
  30.0 62.6 %all-to-all-start.1 = ((bf16[32,2,128,128]{3,2,1,0:T(8,128)(2,1)}), bf16[32,2,128,128]{3,2,1,0:T(8,128)(2,1)S(1)}, u32[]{:S(2)}, u32[]{:S(2)}) async-start(bf16[32,2,128,128]{3,2,1,0:T(8,128)(2,1)} %bitcast.150), calls=%async_computation.1 | async-start | bytes 4194304 | tf_op jit(solution)/shard_map/all_to_all | solution.py:92
  39.9 78.5 %all-gather.3.cloned.1.call-start = ((), (), s32[]{:S(2)}) async-start(), calls=%async_computation.5 | async-start | bytes 2433024 | tf_op jit(solution)/shard_map/all_gather | solution.py:113
  92.5 1.3 copy-start.2
  123.4 2.2 copy-start.3
  125.6 3.6 copy-start.1
  127.0 3.1 collective-permute-start
  130.2 21.3 %collective-permute-start.1 = (bf16[224,256]{1,0:T(8,128)(2,1)S(1)}, bf16[224,256]{1,0:T(8,128)(2,1)S(1)}, u32[]{:S(2)}, u32[]{:S(2)}) collective-permute-start(bf16[224,256]{1,0:T(8,128)(2,1)S(1)} %pad_maximum_fusion.4), channel_id=1, source_target_pairs={{0,32},{32,64},{64,96},{96,128},{128,160},{160,192},{192,224},{224... | collective-permute-start | bytes 344072 | tf_op jit(solution)/shard_map/ppermute | solution.py:30
  134.6 18.3 %collective-permute-start.2 = (bf16[224,256]{1,0:T(8,128)(2,1)S(1)}, bf16[224,256]{1,0:T(8,128)(2,1)S(1)}, u32[]{:S(2)}, u32[]{:S(2)}) collective-permute-start(bf16[224,256]{1,0:T(8,128)(2,1)S(1)} %pad_maximum_fusion.4), channel_id=1, source_target_pairs={{0,64},{32,96},{64,128},{96,160},{128,192},{160,224},{192,256},{22... | collective-permute-start | bytes 344072 | tf_op jit(solution)/shard_map/ppermute | solution.py:30
  138.1 16.6 %collective-permute-start.3 = (bf16[224,256]{1,0:T(8,128)(2,1)S(1)}, bf16[224,256]{1,0:T(8,128)(2,1)S(1)}, u32[]{:S(2)}, u32[]{:S(2)}) collective-permute-start(bf16[224,256]{1,0:T(8,128)(2,1)S(1)} %pad_maximum_fusion.4), channel_id=1, source_target_pairs={{0,96},{32,128},{64,160},{96,192},{128,224},{160,256},{192,288},{2... | collective-permute-start | bytes 344072 | tf_op jit(solution)/shard_map/ppermute | solution.py:30
  142.4 20.9 %collective-permute-start.4 = (bf16[224,256]{1,0:T(8,128)(2,1)S(1)}, bf16[224,256]{1,0:T(8,128)(2,1)S(1)}, u32[]{:S(2)}, u32[]{:S(2)}) collective-permute-start(bf16[224,256]{1,0:T(8,128)(2,1)S(1)} %pad_maximum_fusion.4), channel_id=1, source_target_pairs={{0,128},{32,160},{64,192},{96,224},{128,256},{160,288},{192,320},{... | collective-permute-start | bytes 344072 | tf_op jit(solution)/shard_map/ppermute | solution.py:30
  147.4 16.0 %collective-permute-start.5 = (bf16[224,256]{1,0:T(8,128)(2,1)S(1)}, bf16[224,256]{1,0:T(8,128)(2,1)S(1)}, u32[]{:S(2)}, u32[]{:S(2)}) collective-permute-start(bf16[224,256]{1,0:T(8,128)(2,1)S(1)} %pad_maximum_fusion.4), channel_id=1, source_target_pairs={{0,160},{32,192},{64,224},{96,256},{128,288},{160,320},{192,352},{... | collective-permute-start | bytes 344072 | tf_op jit(solution)/shard_map/ppermute | solution.py:30
  151.5 14.3 %collective-permute-start.6 = (bf16[224,256]{1,0:T(8,128)(2,1)S(1)}, bf16[224,256]{1,0:T(8,128)(2,1)S(1)}, u32[]{:S(2)}, u32[]{:S(2)}) collective-permute-start(bf16[224,256]{1,0:T(8,128)(2,1)S(1)} %pad_maximum_fusion.4), channel_id=1, source_target_pairs={{0,192},{32,224},{64,256},{96,288},{128,320},{160,352},{192,384},{... | collective-permute-start | bytes 344072 | tf_op jit(solution)/shard_map/ppermute | solution.py:30
  152.9 13.0 %collective-permute-start.7 = (bf16[224,256]{1,0:T(8,128)(2,1)S(1)}, bf16[224,256]{1,0:T(8,128)(2,1)S(1)}, u32[]{:S(2)}, u32[]{:S(2)}) collective-permute-start(bf16[224,256]{1,0:T(8,128)(2,1)S(1)} %pad_maximum_fusion.4), channel_id=1, source_target_pairs={{0,224},{32,256},{64,288},{96,320},{128,352},{160,384},{192,416},{... | collective-permute-start | bytes 344072 | tf_op jit(solution)/shard_map/ppermute | solution.py:30
  154.7 13.1 %collective-permute-start.8 = (bf16[224,256]{1,0:T(8,128)(2,1)S(1)}, bf16[224,256]{1,0:T(8,128)(2,1)S(1)}, u32[]{:S(2)}, u32[]{:S(2)}) collective-permute-start(bf16[224,256]{1,0:T(8,128)(2,1)S(1)} %pad_maximum_fusion.4), channel_id=1, source_target_pairs={{0,256},{32,288},{64,320},{96,352},{128,384},{160,416},{192,448},{... | collective-permute-start | bytes 344072 | tf_op jit(solution)/shard_map/ppermute | solution.py:30
  167.8 1.1 copy-start.7
  173.5 7.3 %collective-permute-start.9 = (bf16[224,256]{1,0:T(8,128)(2,1)S(1)}, bf16[224,256]{1,0:T(8,128)(2,1)S(1)}, u32[]{:S(2)}, u32[]{:S(2)}) collective-permute-start(bf16[224,256]{1,0:T(8,128)(2,1)S(1)} %pad_maximum_fusion.5), channel_id=1, source_target_pairs={{32,0},{64,32},{96,64},{128,96},{160,128},{192,160},{224,192},{256... | collective-permute-start | bytes 344072 | tf_op jit(solution)/shard_map/ppermute | solution.py:30
  174.9 12.3 %collective-permute-start.10 = (bf16[224,256]{1,0:T(8,128)(2,1)S(1)}, bf16[224,256]{1,0:T(8,128)(2,1)S(1)}, u32[]{:S(2)}, u32[]{:S(2)}) collective-permute-start(bf16[224,256]{1,0:T(8,128)(2,1)S(1)} %pad_maximum_fusion.6), channel_id=1, source_target_pairs={{64,0},{96,32},{128,64},{160,96},{192,128},{224,160},{256,192},{28... | collective-permute-start | bytes 344072 | tf_op jit(solution)/shard_map/ppermute | solution.py:30
  176.2 14.1 %collective-permute-start.11 = (bf16[224,256]{1,0:T(8,128)(2,1)S(1)}, bf16[224,256]{1,0:T(8,128)(2,1)S(1)}, u32[]{:S(2)}, u32[]{:S(2)}) collective-permute-start(bf16[224,256]{1,0:T(8,128)(2,1)S(1)} %pad_maximum_fusion.7), channel_id=1, source_target_pairs={{96,0},{128,32},{160,64},{192,96},{224,128},{256,160},{288,192},{3... | collective-permute-start | bytes 344072 | tf_op jit(solution)/shard_map/ppermute | solution.py:30
  177.5 33.4 %collective-permute-start.12 = (bf16[224,256]{1,0:T(8,128)(2,1)S(1)}, bf16[224,256]{1,0:T(8,128)(2,1)S(1)}, u32[]{:S(2)}, u32[]{:S(2)}) collective-permute-start(bf16[224,256]{1,0:T(8,128)(2,1)S(1)} %pad_maximum_fusion.8), channel_id=1, source_target_pairs={{128,0},{160,32},{192,64},{224,96},{256,128},{288,160},{320,192},{... | collective-permute-start | bytes 344072 | tf_op jit(solution)/shard_map/ppermute | solution.py:30
  178.8 32.1 %collective-permute-start.13 = (bf16[224,256]{1,0:T(8,128)(2,1)S(1)}, bf16[224,256]{1,0:T(8,128)(2,1)S(1)}, u32[]{:S(2)}, u32[]{:S(2)}) collective-permute-start(bf16[224,256]{1,0:T(8,128)(2,1)S(1)} %pad_maximum_fusion.9), channel_id=1, source_target_pairs={{160,0},{192,32},{224,64},{256,96},{288,128},{320,160},{352,192},{... | collective-permute-start | bytes 344072 | tf_op jit(solution)/shard_map/ppermute | solution.py:30
  180.8 40.9 %collective-permute-start.14 = (bf16[224,256]{1,0:T(8,128)(2,1)S(1)}, bf16[224,256]{1,0:T(8,128)(2,1)S(1)}, u32[]{:S(2)}, u32[]{:S(2)}) collective-permute-start(bf16[224,256]{1,0:T(8,128)(2,1)S(1)} %pad_maximum_fusion.10), channel_id=1, source_target_pairs={{192,0},{224,32},{256,64},{288,96},{320,128},{352,160},{384,192},{... | collective-permute-start | bytes 344072 | tf_op jit(solution)/shard_map/ppermute | solution.py:30
  187.1 34.6 %collective-permute-start.15 = (bf16[224,256]{1,0:T(8,128)(2,1)S(1)}, bf16[224,256]{1,0:T(8,128)(2,1)S(1)}, u32[]{:S(2)}, u32[]{:S(2)}) collective-permute-start(bf16[224,256]{1,0:T(8,128)(2,1)S(1)} %pad_maximum_fusion.11), channel_id=1, source_target_pairs={{224,0},{256,32},{288,64},{320,96},{352,128},{384,160},{416,192},{... | collective-permute-start | bytes 344072 | tf_op jit(solution)/shard_map/ppermute | solution.py:30
  190.3 31.5 %collective-permute-start.16 = (bf16[224,256]{1,0:T(8,128)(2,1)S(1)}, bf16[224,256]{1,0:T(8,128)(2,1)S(1)}, u32[]{:S(2)}, u32[]{:S(2)}) collective-permute-start(bf16[224,256]{1,0:T(8,128)(2,1)S(1)} %pad_maximum_fusion.12), channel_id=1, source_target_pairs={{256,0},{288,32},{320,64},{352,96},{384,128},{416,160},{448,192},{... | collective-permute-start | bytes 344072 | tf_op jit(solution)/shard_map/ppermute | solution.py:30
  221.9 3.1 collective-permute-start.17
  232.2 3.6 copy-start
  242.0 68.3 %all-to-all-start.3 = ((bf16[16,528,128]{2,1,0:T(8,128)(2,1)}), bf16[16,528,128]{2,1,0:T(8,128)(2,1)S(1)}, u32[]{:S(2)}, u32[]{:S(2)}) async-start(bf16[16,528,128]{2,1,0:T(8,128)(2,1)} %pad_maximum_fusion.1), calls=%async_computation.3 | async-start | bytes 4325376 | tf_op jit(solution)/shard_map/all_to_all | solution.py:268
  312.2 18.7 %all-to-all-start.4 = ((bf16[32,32,128]{2,1,0:T(8,128)(2,1)}), bf16[32,32,128]{2,1,0:T(8,128)(2,1)S(1)}, u32[]{:S(2)}, u32[]{:S(2)}) async-start(bf16[32,32,128]{2,1,0:T(8,128)(2,1)} %pad_maximum_fusion.2), calls=%async_computation.4 | async-start | bytes 524288 | tf_op jit(solution)/shard_map/all_to_all | solution.py:287
  330.9 88.9 %all-to-all-start.2 = ((bf16[32,160,224]{2,1,0:T(8,128)(2,1)}), bf16[32,160,224]{2,1,0:T(8,128)(2,1)S(1)}, u32[]{:S(2)}, u32[]{:S(2)}) async-start(bf16[32,160,224]{2,1,0:T(8,128)(2,1)} %pad_maximum_fusion), calls=%async_computation.2 | async-start | bytes 5242880 | tf_op jit(solution)/shard_map/all_to_all | solution.py:223
  337.2 111.8 %all-gather.5.cloned.1.call-start = ((), (), s32[]{:S(2)}) async-start(), calls=%async_computation.6 | async-start | bytes 2297856 | tf_op jit(solution)/shard_map/all_gather | solution.py:311
Sparse Core Ops, SparseCore 0:
  44.4 73.9 all-gather.2
  340.7 108.2 all-gather.4

commit v6 on v5

--- a/solution.py
+++ b/solution.py
@@ -81,7 +81,12 @@
     dump_slot = groups * CAP
     slot_dest = jnp.where(is_live, target_user * CAP + slot_rank, dump_slot)
     block_place = (slot_codes - target_user * pos_count).astype(jnp.float32)
-    outgoing = jnp.zeros((dump_slot + 1, BLK, BLK), jnp.bfloat16).at[slot_dest].set(blocks[0])
+    dest_match = slot_dest[:, None] == jnp.arange(dump_slot, dtype=jnp.int32)[None, :]
+    dest_source = jnp.sum(
+        jnp.where(dest_match, jnp.arange(slot_dest.shape[0], dtype=jnp.int32)[:, None], 0), axis=0
+    )
+    dest_used = jnp.any(dest_match, axis=0)
+    outgoing = jnp.where(dest_used[:, None, None], blocks[0][dest_source], jnp.zeros((), jnp.bfloat16))
     outgoing_pos = (
         jnp.full((dump_slot + 1,), -1.0, jnp.float32)
         .at[slot_dest]
@@ -90,7 +95,7 @@
     )
     arrived, arrived_pos = (
         lax.all_to_all(
-            outgoing[:dump_slot].reshape(groups, CAP, BLK, BLK),
+            outgoing.reshape(groups, CAP, BLK, BLK),
             "wt",
             split_axis=0,
             concat_axis=0,
@@ -130,10 +135,15 @@
     scaled = tokens_in.astype(jnp.float32) * inv_rms[:, None]
     arrival = arrived_pos.reshape(-1).astype(jnp.int32)
     arrival = jnp.where(arrival < 0, pos_count, arrival)
-    weight_table = (
-        jnp.zeros((pos_count + 1, BLK, BLK), jnp.bfloat16)
-        .at[arrival]
-        .set(arrived.reshape(-1, BLK, BLK))
+    place_match = arrival[:, None] == jnp.arange(pos_count, dtype=jnp.int32)[None, :]
+    place_source = jnp.sum(
+        jnp.where(place_match, jnp.arange(arrival.shape[0], dtype=jnp.int32)[:, None], 0), axis=0
+    )
+    place_used = jnp.any(place_match, axis=0)
+    weight_table = jnp.where(
+        place_used[:, None, None],
+        arrived.reshape(-1, BLK, BLK)[place_source],
+        jnp.zeros((), jnp.bfloat16),
     )
     w_query = weight_table[:row_blocks].reshape(D, HD)
     w_pair = weight_table[row_blocks:pos_count].reshape(D, HD)
@@ -235,25 +245,25 @@
     tokens_grad = (inv_rms[:, None] * (scaled_grad - scaled * (row_dots / D)[:, None])).astype(
         jnp.bfloat16
     )
-    grad_query = contract_rows(normed, query_grad)
-    grad_pair = contract_rows(normed, pair_grad)
-    grad_table = jnp.concatenate(
-        [
-            grad_query.reshape(row_blocks, BLK, BLK),
-            grad_pair.reshape(row_blocks, BLK, BLK),
-            jnp.zeros((1, BLK, BLK), jnp.float32),
-        ],
-        axis=0,
-    )
     n_seq = lax.axis_size("seq")
     band = BLK // n_seq
     slots = slot_dest.shape[0]
     band_rows = CAP * band
     block_rows = groups * band_rows
+    matrix_rows = row_blocks * band
     side = 16
-    block_send = jnp.transpose(
-        grad_table[arrival].reshape(groups, CAP, n_seq, band, BLK), (2, 0, 1, 3, 4)
-    ).reshape(n_seq, block_rows, BLK)
+
+    def banded(matrix_grad):
+        return jnp.transpose(
+            matrix_grad.reshape(row_blocks, n_seq, band, BLK), (1, 0, 2, 3)
+        ).reshape(n_seq, matrix_rows, BLK)
+
+    grad_query = contract_rows(normed, query_grad)
+    query_recv = lax.all_to_all(
+        banded(grad_query).astype(jnp.bfloat16), "seq", split_axis=0, concat_axis=0, tiled=True
+    )
+    query_band = jnp.sum(query_recv.astype(jnp.float32), axis=0)
+    grad_pair = contract_rows(normed, pair_grad)
     gain_width = D // n_seq
     per_chunk = gain_width // feat
     head_gain = jnp.sum(contribution * scaled_full.T, axis=1)
@@ -265,16 +275,24 @@
     gain_send = jnp.pad(gain_send, ((0, 0), (0, side * BLK - 2 * gain_width))).reshape(
         n_seq, side, BLK
     )
-    seq_recv = lax.all_to_all(
-        jnp.concatenate([block_send.astype(jnp.bfloat16), gain_send], axis=1),
+    pair_recv = lax.all_to_all(
+        jnp.concatenate([banded(grad_pair).astype(jnp.bfloat16), gain_send], axis=1),
         "seq",
         split_axis=0,
         concat_axis=0,
         tiled=True,
     )
-    seq_sum = jnp.sum(seq_recv.astype(jnp.float32), axis=0)
-    block_chunk = seq_sum[:block_rows].astype(jnp.bfloat16).reshape(groups, band_rows, BLK)
-    gain_flat = seq_sum[block_rows:].reshape(-1)
+    pair_sum = jnp.sum(pair_recv.astype(jnp.float32), axis=0)
+    band_table = jnp.concatenate(
+        [
+            query_band.reshape(row_blocks, band, BLK),
+            pair_sum[:matrix_rows].reshape(row_blocks, band, BLK),
+            jnp.zeros((1, band, BLK), jnp.float32),
+        ],
+        axis=0,
+    )
+    block_chunk = band_table[arrival].astype(jnp.bfloat16).reshape(groups, band_rows, BLK)
+    gain_flat = pair_sum[matrix_rows:].reshape(-1)
     gain_chunk = gain_flat[:gain_width] + gain_flat[gain_width : 2 * gain_width]
     chunk_top = lax.reduce_precision(gain_chunk, exponent_bits=8, mantissa_bits=7)
     chunk_pair = jnp.stack([chunk_top, gain_chunk - chunk_top]).astype(jnp.bfloat16)

time: 463 us -> 468 us (1.011)
  waiting for transfers between devices: 279 us -> 242 us
  starting transfers between devices: 90.6 us -> 124 us
  other arithmetic: 21.3 us -> 40.7 us
  local copies, waits for them, and re-layouts: 40.1 us -> 28.2 us
    ppermute x16, waiting for transfers between devices: 44.4 us -> 25.5 us  [shifted(): lax.ppermute(value, axis, [(source, source + steps) for source in range(i...]
    all_to_all x2 -> x3, waiting for transfers between devices: 103 us -> 86 us  [the longest x1 50.9 us: body(): lax.all_to_all(outgoing.reshape(groups, CAP, BLK, BLK), 'wt', split_axis=...]
    all_to_all x2 -> x3, starting transfers between devices: 25.7 us -> 39.8 us  [the longest x1 27.2 us: body(): lax.all_to_all(banded(grad_query).astype(jnp.bfloat16), 'seq', split_axis...]
    scatter x2 -> x0, local copies, waits for them, and re-layouts: 13.3 us -> none  [the longest x1 6.65 us: body(): jnp.zeros((dump_slot + 1, BLK, BLK), jnp.bfloat16).at[slot_dest]]
    ppermute x16, starting transfers between devices: 36.8 us -> 48.9 us  [shifted(): lax.ppermute(value, axis, [(source, source + steps) for source in range(i...]
    all_to_all x1, starting transfers between devices: 7.41 us -> 13.9 us  [body(): lax.all_to_all(jnp.concatenate([block_chunk, gain_slots], axis=1), 'wt',...]
    convert_element_type x8, other arithmetic: 0.14 us -> 6.43 us  [body(): recv = shifted(piece, 'seq', -offset).astype(jnp.float32)]
    select_n x1 -> x7, other arithmetic: 0.01 us -> 5.69 us  [the longest x1 3.12 us: body(): jnp.where(dest_used[:, None, None], blocks[0][dest_source], jnp.zeros((),...]
  transfers between devices with their start and end apart: 25 -> 26, of which waited for: 15 -> 14; matrix products, arithmetic and copies ran while one was open for 7% -> 11% of each run, Pallas kernels for 0% -> 0%
where the time goes in v6:
time: 468 us; the launch traced here: 465 us
  waiting for transfers between devices  242 us (52%)
  starting transfers between devices  124 us (26%)
  other arithmetic  40.7 us (9%)
  local copies, waits for them, and re-layouts  28.2 us (6%)
  between operations  15.1 us (3%)
  matrix products  14.5 us (3%)
    all_to_all x1, waiting for transfers between devices, body(): lax.all_to_all(packed.reshape(groups, feat + pad_rows, tok_rows), 'wt', s...  80.1 us
    all_to_all x1, waiting for transfers between devices, body(): lax.all_to_all(outgoing.reshape(groups, CAP, BLK, BLK), 'wt', split_axis=...  50.9 us
    ppermute x16, starting transfers between devices, shifted(): lax.ppermute(value, axis, [(source, source + steps) for source in range(i...  48.9 us
    all_to_all x1, waiting for transfers between devices, body(): lax.all_to_all(jnp.concatenate([banded(grad_pair).astype(jnp.bfloat16), g...  27.5 us
    all_to_all x1, starting transfers between devices, body(): lax.all_to_all(banded(grad_query).astype(jnp.bfloat16), 'seq', split_axis...  27.2 us
    all_gather x1, waiting for transfers between devices, body(): lax.all_gather(gather_send, 'seq', axis=0, tiled=True)  26.5 us
    ppermute x16, waiting for transfers between devices, shifted(): lax.ppermute(value, axis, [(source, source + steps) for source in range(i...  25.5 us
    all_gather x1, waiting for transfers between devices, body(): lax.all_gather(jnp.concatenate([tokens_in, gain_rows, jnp.zeros((side_row...  18.6 us
  transfers between devices with their start and end apart: 26, of which 14 were waited for; matrix products, arithmetic and copies ran while one was open for 11% of the time, Pallas kernels for 0%

profile of v6, /device:TPU:6, one launch (start us, length us, event | category | flops | bytes accessed | tf_op | source)
XLA Modules:
  0.0 465.0 jit_solution(2145068847997919391)
XLA Ops:
  11.2 10.2 %all-to-all-start = ((bf16[32,1,2]{2,1,0:T(2,128)(2,1)}), bf16[32,1,2]{2,1,0:T(2,128)(2,1)S(1)}, u32[]{:S(2)}, u32[]{:S(2)}) async-start(bf16[32,1,2]{2,1,0:T(2,128)(2,1)} %all_to_all.28), calls=%async_computation | async-start | bytes 32768 | tf_op jit(solution)/shard_map/all_to_all | solution.py:104
  22.5 2.1 gather_fusion
  24.6 3.1 broadcast_select_fusion.1
  27.7 1.6 all-to-all-done
  29.3 8.4 %all-to-all-start.1 = ((bf16[32,2,128,128]{3,2,1,0:T(8,128)(2,1)}), bf16[32,2,128,128]{3,2,1,0:T(8,128)(2,1)}, u32[]{:S(2)}, u32[]{:S(2)}) async-start(bf16[32,2,128,128]{3,2,1,0:T(8,128)(2,1)} %broadcast_select_fusion.1), calls=%async_computation.1 | async-start | bytes 4194304 | tf_op jit(solution)/shard_map/all_to_all | solution.py:97
  39.5 50.9 %all-to-all-done.1 = bf16[32,2,128,128]{3,2,1,0:T(8,128)(2,1)} async-done(((bf16[32,2,128,128]{3,2,1,0:T(8,128)(2,1)}), bf16[32,2,128,128]{3,2,1,0:T(8,128)(2,1)}, u32[]{:S(2)}, u32[]{:S(2)}) %all-to-all-start.1) | async-done | bytes 2097184 | tf_op jit(solution)/shard_map/all_to_all | solution.py:97
  90.4 4.1 gather_fusion.1
  94.5 1.9 broadcast_select_fusion
  96.4 1.2 fusion.85
  97.6 18.6 %all-gather.3.cloned.1.call-done = bf16[232,4608]{0,1:T(8,128)(2,1)} async-done(((bf16[232,144]{0,1:T(8,128)(2,1)}), bf16[232,4608]{0,1:T(8,128)(2,1)}) %all-gather.3.cloned.1.call-update) | async-done | bytes 2138128 | tf_op jit(solution)/shard_map/all_gather | solution.py:118
  116.2 4.1 copy.63
  120.3 2.1 fusion.8
  122.4 1.6 slice_convert_fusion
  124.1 2.2 fusion.14
  127.7 2.1 collective-permute-start
  130.9 3.8 collective-permute-start.1
  135.3 8.0 %collective-permute-start.8 = (bf16[224,256]{1,0:T(8,128)(2,1)S(1)}, bf16[224,256]{1,0:T(8,128)(2,1)S(1)}, u32[]{:S(2)}, u32[]{:S(2)}) collective-permute-start(bf16[224,256]{1,0:T(8,128)(2,1)S(1)} %pad_maximum_fusion.4), channel_id=1, source_target_pairs={{0,256},{32,288},{64,320},{96,352},{128,384},{160,416},{192,448},{... | collective-permute-start | bytes 344072 | tf_op jit(solution)/shard_map/ppermute | solution.py:30
  143.3 1.8 collective-permute-start.7
  145.2 2.5 collective-permute-start.6
  147.7 2.0 collective-permute-start.5
  149.7 3.3 collective-permute-start.2
  153.0 12.5 %collective-permute-done.2 = bf16[224,256]{1,0:T(8,128)(2,1)S(1)} collective-permute-done((bf16[224,256]{1,0:T(8,128)(2,1)S(1)}, bf16[224,256]{1,0:T(8,128)(2,1)S(1)}, u32[]{:S(2)}, u32[]{:S(2)}) %collective-permute-start.2) | collective-permute-done | bytes 114720 | tf_op jit(solution)/shard_map/ppermute | solution.py:30
  165.5 7.3 %collective-permute-start.3 = (bf16[224,256]{1,0:T(8,128)(2,1)S(1)}, bf16[224,256]{1,0:T(8,128)(2,1)S(1)}, u32[]{:S(2)}, u32[]{:S(2)}) collective-permute-start(bf16[224,256]{1,0:T(8,128)(2,1)S(1)} %pad_maximum_fusion.4), channel_id=1, source_target_pairs={{0,96},{32,128},{64,160},{96,192},{128,224},{160,256},{192,288},{2... | collective-permute-start | bytes 344072 | tf_op jit(solution)/shard_map/ppermute | solution.py:30
  172.9 2.6 collective-permute-done.3
  175.5 9.9 %collective-permute-start.4 = (bf16[224,256]{1,0:T(8,128)(2,1)S(1)}, bf16[224,256]{1,0:T(8,128)(2,1)S(1)}, u32[]{:S(2)}, u32[]{:S(2)}) collective-permute-start(bf16[224,256]{1,0:T(8,128)(2,1)S(1)} %pad_maximum_fusion.4), channel_id=1, source_target_pairs={{0,128},{32,160},{64,192},{96,224},{128,256},{160,288},{192,320},{... | collective-permute-start | bytes 344072 | tf_op jit(solution)/shard_map/ppermute | solution.py:30
  185.4 2.1 collective-permute-done.4
  187.7 1.1 fusion.83
  188.8 2.0 fusion.89
  190.8 1.4 multiply_reduce_fusion
  192.2 1.1 fusion.13
  193.8 1.5 fusion.90
  195.9 1.3 collective-permute-start.10
  197.2 1.3 collective-permute-start.11
  198.5 1.3 collective-permute-start.12
  200.5 1.3 collective-permute-start.13
  202.4 1.3 collective-permute-start.14
  205.8 1.3 collective-permute-start.15
  207.1 1.3 collective-permute-start.16
  208.4 8.2 %collective-permute-done.12 = bf16[224,256]{1,0:T(8,128)(2,1)S(1)} collective-permute-done((bf16[224,256]{1,0:T(8,128)(2,1)S(1)}, bf16[224,256]{1,0:T(8,128)(2,1)S(1)}, u32[]{:S(2)}, u32[]{:S(2)}) %collective-permute-start.12) | collective-permute-done | bytes 114720 | tf_op jit(solution)/shard_map/ppermute | solution.py:30
  217.3 1.3 collective-permute-start.9
  218.6 0.9 convolution_convert_fusion.1
  219.6 1.2 copy.74
  220.8 27.2 %all-to-all-start.3 = ((bf16[16,288,128]{2,1,0:T(8,128)(2,1)}), bf16[16,288,128]{2,1,0:T(8,128)(2,1)}, u32[]{:S(2)}, u32[]{:S(2)}) async-start(bf16[16,288,128]{2,1,0:T(8,128)(2,1)} %bitcast.173), calls=%async_computation.3 | async-start | bytes 2359296 | tf_op jit(solution)/shard_map/all_to_all | solution.py:262
  248.9 0.9 convert_element_type.256
  250.8 0.9 convert_element_type.258
  254.5 1.1 select_convert_fusion
  255.6 2.1 collective-permute-start.17
  259.5 0.9 convolution_convert_fusion
  260.6 1.1 copy-done.4
  261.7 2.8 fusion.7
  264.8 1.1 pad_maximum_fusion.1
  265.9 7.7 %all-to-all-done.3 = bf16[16,288,128]{2,1,0:T(8,128)(2,1)} async-done(((bf16[16,288,128]{2,1,0:T(8,128)(2,1)}), bf16[16,288,128]{2,1,0:T(8,128)(2,1)}, u32[]{:S(2)}, u32[]{:S(2)}) %all-to-all-start.3) | async-done | bytes 1179680 | tf_op jit(solution)/shard_map/all_to_all | solution.py:262
  273.6 4.2 all-to-all-start.4
  278.1 1.4 convert_reduce_fusion.2
  279.6 27.5 %all-to-all-done.4 = bf16[16,304,128]{2,1,0:T(8,128)(2,1)S(1)} async-done(((bf16[16,304,128]{2,1,0:T(8,128)(2,1)}), bf16[16,304,128]{2,1,0:T(8,128)(2,1)S(1)}, u32[]{:S(2)}, u32[]{:S(2)}) %all-to-all-start.4) | async-done | bytes 1245216 | tf_op jit(solution)/shard_map/all_to_all | solution.py:278
  309.6 13.9 %all-to-all-start.5 = ((bf16[32,32,128]{2,1,0:T(8,128)(2,1)}), bf16[32,32,128]{2,1,0:T(8,128)(2,1)S(1)}, u32[]{:S(2)}, u32[]{:S(2)}) async-start(bf16[32,32,128]{2,1,0:T(8,128)(2,1)} %pad_maximum_fusion.2), calls=%async_computation.5 | async-start | bytes 524288 | tf_op jit(solution)/shard_map/all_to_all | solution.py:305
  323.5 4.1 copy.58
  327.7 3.7 pad_maximum_fusion
  331.4 3.5 all-to-all-done.5
  334.9 7.0 %all-to-all-start.2 = ((bf16[32,160,224]{2,1,0:T(8,128)(2,1)}), bf16[32,160,224]{2,1,0:T(8,128)(2,1)}, u32[]{:S(2)}, u32[]{:S(2)}) async-start(bf16[32,160,224]{2,1,0:T(8,128)(2,1)} %pad_maximum_fusion), calls=%async_computation.2 | async-start | bytes 5242880 | tf_op jit(solution)/shard_map/all_to_all | solution.py:233
  343.6 80.1 %all-to-all-done.2 = bf16[32,160,224]{2,1,0:T(8,128)(2,1)} async-done(((bf16[32,160,224]{2,1,0:T(8,128)(2,1)}), bf16[32,160,224]{2,1,0:T(8,128)(2,1)}, u32[]{:S(2)}, u32[]{:S(2)}) %all-to-all-start.2) | async-done | bytes 2293792 | tf_op jit(solution)/shard_map/all_to_all | solution.py:233
  423.7 2.2 convert_reduce_fusion
  426.6 26.5 %all-gather.5.cloned.1.call-done = bf16[8448,128]{1,0:T(8,128)(2,1)} async-done(((bf16[528,128]{1,0:T(8,128)(2,1)}), bf16[8448,128]{1,0:T(8,128)(2,1)}) %all-gather.5.cloned.1.call-update) | async-done | bytes 2162704 | tf_op jit(solution)/shard_map/all_gather | solution.py:329
  453.9 3.5 copy_bitcast_fusion
  (177 shorter events, 28.6 us)
Async XLA Ops:
  7.2 15.3 %copy-start = (bf16[1,64,128,128]{3,2,1,0:T(8,128)(2,1)S(1)}, bf16[1,64,128,128]{3,2,1,0:T(8,128)(2,1)}, u32[]{:S(2)}) copy-start(bf16[1,64,128,128]{3,2,1,0:T(8,128)(2,1)} %param.9) | copy-start | bytes 6291460
  9.7 14.9 %copy-start.15 = (s32[64]{0:T(128)}, s32[64]{0:T(128)S(1)}, u32[]{:S(2)}) copy-start(s32[64]{0:T(128)S(1)} %fusion.68) | copy-start | bytes 772
  11.2 18.1 %all-to-all-start = ((bf16[32,1,2]{2,1,0:T(2,128)(2,1)}), bf16[32,1,2]{2,1,0:T(2,128)(2,1)S(1)}, u32[]{:S(2)}, u32[]{:S(2)}) async-start(bf16[32,1,2]{2,1,0:T(2,128)(2,1)} %all_to_all.28), calls=%async_computation | async-start | bytes 32768 | tf_op jit(solution)/shard_map/all_to_all | solution.py:104
  27.7 10.1 %copy-start.12 = (f32[144]{0:T(256)S(1)}, f32[144]{0:T(256)}, u32[]{:S(2)}) copy-start(f32[144]{0:T(256)} %param.7) | copy-start | bytes 1732
  27.7 10.4 %copy-start.5 = (bf16[224,144]{0,1:T(8,128)(2,1)S(1)}, bf16[224,144]{0,1:T(8,128)(2,1)}, u32[]{:S(2)}) copy-start(bf16[224,144]{0,1:T(8,128)(2,1)} %param.6) | copy-start | bytes 193540
  27.7 11.4 %copy-start.14 = (s32[224]{0:T(256)S(1)}, s32[224]{0:T(256)}, u32[]{:S(2)}) copy-start(s32[224]{0:T(256)} %param.8) | copy-start | bytes 2692
  29.3 9.8 %copy-start.6 = (bf16[32,1,2]{2,1,0:T(2,128)(2,1)}, bf16[32,1,2]{2,1,0:T(2,128)(2,1)S(1)}, u32[]{:S(2)}) copy-start(bf16[32,1,2]{2,1,0:T(2,128)(2,1)S(1)} %all-to-all-done) | copy-start | bytes 388
  29.3 61.1 %all-to-all-start.1 = ((bf16[32,2,128,128]{3,2,1,0:T(8,128)(2,1)}), bf16[32,2,128,128]{3,2,1,0:T(8,128)(2,1)}, u32[]{:S(2)}, u32[]{:S(2)}) async-start(bf16[32,2,128,128]{3,2,1,0:T(8,128)(2,1)} %broadcast_select_fusion.1), calls=%async_computation.1 | async-start | bytes 4194304 | tf_op jit(solution)/shard_map/all_to_all | solution.py:97
  37.7 78.4 %all-gather.3.cloned.1.call-start = ((), (), s32[]{:S(2)}) async-start(), calls=%async_computation.6 | async-start | bytes 2433024 | tf_op jit(solution)/shard_map/all_gather | solution.py:118
  124.1 2.2 copy-start.1
  124.1 2.2 copy-start.3
  127.7 3.1 collective-permute-start
  130.9 18.8 %collective-permute-start.1 = (bf16[224,256]{1,0:T(8,128)(2,1)S(1)}, bf16[224,256]{1,0:T(8,128)(2,1)S(1)}, u32[]{:S(2)}, u32[]{:S(2)}) collective-permute-start(bf16[224,256]{1,0:T(8,128)(2,1)S(1)} %pad_maximum_fusion.4), channel_id=1, source_target_pairs={{0,32},{32,64},{64,96},{96,128},{128,160},{160,192},{192,224},{224... | collective-permute-start | bytes 344072 | tf_op jit(solution)/shard_map/ppermute | solution.py:30
  135.3 52.4 %collective-permute-start.8 = (bf16[224,256]{1,0:T(8,128)(2,1)S(1)}, bf16[224,256]{1,0:T(8,128)(2,1)S(1)}, u32[]{:S(2)}, u32[]{:S(2)}) collective-permute-start(bf16[224,256]{1,0:T(8,128)(2,1)S(1)} %pad_maximum_fusion.4), channel_id=1, source_target_pairs={{0,256},{32,288},{64,320},{96,352},{128,384},{160,416},{192,448},{... | collective-permute-start | bytes 344072 | tf_op jit(solution)/shard_map/ppermute | solution.py:30
  143.3 44.3 %collective-permute-start.7 = (bf16[224,256]{1,0:T(8,128)(2,1)S(1)}, bf16[224,256]{1,0:T(8,128)(2,1)S(1)}, u32[]{:S(2)}, u32[]{:S(2)}) collective-permute-start(bf16[224,256]{1,0:T(8,128)(2,1)S(1)} %pad_maximum_fusion.4), channel_id=1, source_target_pairs={{0,224},{32,256},{64,288},{96,320},{128,352},{160,384},{192,416},{... | collective-permute-start | bytes 344072 | tf_op jit(solution)/shard_map/ppermute | solution.py:30
  145.2 42.5 %collective-permute-start.6 = (bf16[224,256]{1,0:T(8,128)(2,1)S(1)}, bf16[224,256]{1,0:T(8,128)(2,1)S(1)}, u32[]{:S(2)}, u32[]{:S(2)}) collective-permute-start(bf16[224,256]{1,0:T(8,128)(2,1)S(1)} %pad_maximum_fusion.4), channel_id=1, source_target_pairs={{0,192},{32,224},{64,256},{96,288},{128,320},{160,352},{192,384},{... | collective-permute-start | bytes 344072 | tf_op jit(solution)/shard_map/ppermute | solution.py:30
  147.7 39.9 %collective-permute-start.5 = (bf16[224,256]{1,0:T(8,128)(2,1)S(1)}, bf16[224,256]{1,0:T(8,128)(2,1)S(1)}, u32[]{:S(2)}, u32[]{:S(2)}) collective-permute-start(bf16[224,256]{1,0:T(8,128)(2,1)S(1)} %pad_maximum_fusion.4), channel_id=1, source_target_pairs={{0,160},{32,192},{64,224},{96,256},{128,288},{160,320},{192,352},{... | collective-permute-start | bytes 344072 | tf_op jit(solution)/shard_map/ppermute | solution.py:30
  149.7 15.9 %collective-permute-start.2 = (bf16[224,256]{1,0:T(8,128)(2,1)S(1)}, bf16[224,256]{1,0:T(8,128)(2,1)S(1)}, u32[]{:S(2)}, u32[]{:S(2)}) collective-permute-start(bf16[224,256]{1,0:T(8,128)(2,1)S(1)} %pad_maximum_fusion.4), channel_id=1, source_target_pairs={{0,64},{32,96},{64,128},{96,160},{128,192},{160,224},{192,256},{22... | collective-permute-start | bytes 344072 | tf_op jit(solution)/shard_map/ppermute | solution.py:30
  165.5 9.9 %collective-permute-start.3 = (bf16[224,256]{1,0:T(8,128)(2,1)S(1)}, bf16[224,256]{1,0:T(8,128)(2,1)S(1)}, u32[]{:S(2)}, u32[]{:S(2)}) collective-permute-start(bf16[224,256]{1,0:T(8,128)(2,1)S(1)} %pad_maximum_fusion.4), channel_id=1, source_target_pairs={{0,96},{32,128},{64,160},{96,192},{128,224},{160,256},{192,288},{2... | collective-permute-start | bytes 344072 | tf_op jit(solution)/shard_map/ppermute | solution.py:30
  175.5 12.1 %collective-permute-start.4 = (bf16[224,256]{1,0:T(8,128)(2,1)S(1)}, bf16[224,256]{1,0:T(8,128)(2,1)S(1)}, u32[]{:S(2)}, u32[]{:S(2)}) collective-permute-start(bf16[224,256]{1,0:T(8,128)(2,1)S(1)} %pad_maximum_fusion.4), channel_id=1, source_target_pairs={{0,128},{32,160},{64,192},{96,224},{128,256},{160,288},{192,320},{... | collective-permute-start | bytes 344072 | tf_op jit(solution)/shard_map/ppermute | solution.py:30
  187.7 1.1 copy-start.17
  195.9 9.9 %collective-permute-start.10 = (bf16[224,256]{1,0:T(8,128)(2,1)S(1)}, bf16[224,256]{1,0:T(8,128)(2,1)S(1)}, u32[]{:S(2)}, u32[]{:S(2)}) collective-permute-start(bf16[224,256]{1,0:T(8,128)(2,1)S(1)} %pad_maximum_fusion.6), channel_id=1, source_target_pairs={{64,0},{96,32},{128,64},{160,96},{192,128},{224,160},{256,192},{28... | collective-permute-start | bytes 344072 | tf_op jit(solution)/shard_map/ppermute | solution.py:30
  197.2 9.9 %collective-permute-start.11 = (bf16[224,256]{1,0:T(8,128)(2,1)S(1)}, bf16[224,256]{1,0:T(8,128)(2,1)S(1)}, u32[]{:S(2)}, u32[]{:S(2)}) collective-permute-start(bf16[224,256]{1,0:T(8,128)(2,1)S(1)} %pad_maximum_fusion.7), channel_id=1, source_target_pairs={{96,0},{128,32},{160,64},{192,96},{224,128},{256,160},{288,192},{3... | collective-permute-start | bytes 344072 | tf_op jit(solution)/shard_map/ppermute | solution.py:30
  198.5 18.2 %collective-permute-start.12 = (bf16[224,256]{1,0:T(8,128)(2,1)S(1)}, bf16[224,256]{1,0:T(8,128)(2,1)S(1)}, u32[]{:S(2)}, u32[]{:S(2)}) collective-permute-start(bf16[224,256]{1,0:T(8,128)(2,1)S(1)} %pad_maximum_fusion.8), channel_id=1, source_target_pairs={{128,0},{160,32},{192,64},{224,96},{256,128},{288,160},{320,192},{... | collective-permute-start | bytes 344072 | tf_op jit(solution)/shard_map/ppermute | solution.py:30
  200.5 49.4 %collective-permute-start.13 = (bf16[224,256]{1,0:T(8,128)(2,1)}, bf16[224,256]{1,0:T(8,128)(2,1)}, u32[]{:S(2)}, u32[]{:S(2)}) collective-permute-start(bf16[224,256]{1,0:T(8,128)(2,1)} %pad_maximum_fusion.9), channel_id=1, source_target_pairs={{160,0},{192,32},{224,64},{256,96},{288,128},{320,160},{352,192},{... | collective-permute-start | bytes 344072 | tf_op jit(solution)/shard_map/ppermute | solution.py:30
  202.4 48.3 %collective-permute-start.14 = (bf16[224,256]{1,0:T(8,128)(2,1)}, bf16[224,256]{1,0:T(8,128)(2,1)}, u32[]{:S(2)}, u32[]{:S(2)}) collective-permute-start(bf16[224,256]{1,0:T(8,128)(2,1)} %pad_maximum_fusion.10), channel_id=1, source_target_pairs={{192,0},{224,32},{256,64},{288,96},{320,128},{352,160},{384,192},{... | collective-permute-start | bytes 344072 | tf_op jit(solution)/shard_map/ppermute | solution.py:30
  205.8 10.9 %copy-start.8 = (bf16[224,256]{1,0:T(8,128)(2,1)}, bf16[224,256]{1,0:T(8,128)(2,1)S(1)}, u32[]{:S(2)}) copy-start(bf16[224,256]{1,0:T(8,128)(2,1)S(1)} %collective-permute-done.10) | copy-start | bytes 344068
  205.8 45.9 %collective-permute-start.15 = (bf16[224,256]{1,0:T(8,128)(2,1)}, bf16[224,256]{1,0:T(8,128)(2,1)}, u32[]{:S(2)}, u32[]{:S(2)}) collective-permute-start(bf16[224,256]{1,0:T(8,128)(2,1)} %pad_maximum_fusion.11), channel_id=1, source_target_pairs={{224,0},{256,32},{288,64},{320,96},{352,128},{384,160},{416,192},{... | collective-permute-start | bytes 344072 | tf_op jit(solution)/shard_map/ppermute | solution.py:30
  207.1 9.6 %copy-start.10 = (bf16[224,256]{1,0:T(8,128)(2,1)}, bf16[224,256]{1,0:T(8,128)(2,1)S(1)}, u32[]{:S(2)}) copy-start(bf16[224,256]{1,0:T(8,128)(2,1)S(1)} %collective-permute-done.11) | copy-start | bytes 344068
  207.1 45.5 %collective-permute-start.16 = (bf16[224,256]{1,0:T(8,128)(2,1)}, bf16[224,256]{1,0:T(8,128)(2,1)}, u32[]{:S(2)}, u32[]{:S(2)}) collective-permute-start(bf16[224,256]{1,0:T(8,128)(2,1)} %pad_maximum_fusion.12), channel_id=1, source_target_pairs={{256,0},{288,32},{320,64},{352,96},{384,128},{416,160},{448,192},{... | collective-permute-start | bytes 344072 | tf_op jit(solution)/shard_map/ppermute | solution.py:30
  216.7 0.6 copy-start.11
  217.3 36.2 %collective-permute-start.9 = (bf16[224,256]{1,0:T(8,128)(2,1)}, bf16[224,256]{1,0:T(8,128)(2,1)}, u32[]{:S(2)}, u32[]{:S(2)}) collective-permute-start(bf16[224,256]{1,0:T(8,128)(2,1)} %pad_maximum_fusion.5), channel_id=1, source_target_pairs={{32,0},{64,32},{96,64},{128,96},{160,128},{192,160},{224,192},{256... | collective-permute-start | bytes 344072 | tf_op jit(solution)/shard_map/ppermute | solution.py:30
  219.5 28.4 %copy-start.9 = (bf16[224,256]{1,0:T(8,128)(2,1)S(1)}, bf16[224,256]{1,0:T(8,128)(2,1)}, u32[]{:S(2)}) copy-start(bf16[224,256]{1,0:T(8,128)(2,1)} %copy-done.8) | copy-start | bytes 344068
  220.8 52.8 %all-to-all-start.3 = ((bf16[16,288,128]{2,1,0:T(8,128)(2,1)}), bf16[16,288,128]{2,1,0:T(8,128)(2,1)}, u32[]{:S(2)}, u32[]{:S(2)}) async-start(bf16[16,288,128]{2,1,0:T(8,128)(2,1)} %bitcast.173), calls=%async_computation.3 | async-start | bytes 2359296 | tf_op jit(solution)/shard_map/all_to_all | solution.py:262
  255.5 3.9 copy-start.2
  255.6 3.3 collective-permute-start.17
  260.4 1.3 copy-start.4
  264.8 13.2 %copy-start.7 = (bf16[32,1,2]{2,1,0:T(2,128)(2,1)S(1)}, bf16[32,1,2]{2,1,0:T(2,128)(2,1)}, u32[]{:S(2)}) copy-start(bf16[32,1,2]{2,1,0:T(2,128)(2,1)} %copy-done.6) | copy-start | bytes 388
  264.8 13.3 %copy-start.16 = (s32[64]{0:T(128)S(1)}, s32[64]{0:T(128)}, u32[]{:S(2)}) copy-start(s32[64]{0:T(128)} %copy-done.15) | copy-start | bytes 772
  273.6 33.5 %all-to-all-start.4 = ((bf16[16,304,128]{2,1,0:T(8,128)(2,1)}), bf16[16,304,128]{2,1,0:T(8,128)(2,1)S(1)}, u32[]{:S(2)}, u32[]{:S(2)}) async-start(bf16[16,304,128]{2,1,0:T(8,128)(2,1)} %pad_maximum_fusion.1), calls=%async_computation.4 | async-start | bytes 2490368 | tf_op jit(solution)/shard_map/all_to_all | solution.py:278
  309.6 25.3 %all-to-all-start.5 = ((bf16[32,32,128]{2,1,0:T(8,128)(2,1)}), bf16[32,32,128]{2,1,0:T(8,128)(2,1)S(1)}, u32[]{:S(2)}, u32[]{:S(2)}) async-start(bf16[32,32,128]{2,1,0:T(8,128)(2,1)} %pad_maximum_fusion.2), calls=%async_computation.5 | async-start | bytes 524288 | tf_op jit(solution)/shard_map/all_to_all | solution.py:305
  334.9 88.8 %all-to-all-start.2 = ((bf16[32,160,224]{2,1,0:T(8,128)(2,1)}), bf16[32,160,224]{2,1,0:T(8,128)(2,1)}, u32[]{:S(2)}, u32[]{:S(2)}) async-start(bf16[32,160,224]{2,1,0:T(8,128)(2,1)} %pad_maximum_fusion), calls=%async_computation.2 | async-start | bytes 5242880 | tf_op jit(solution)/shard_map/all_to_all | solution.py:233
  341.9 111.2 %all-gather.5.cloned.1.call-start = ((), (), s32[]{:S(2)}) async-start(), calls=%async_computation.7 | async-start | bytes 2297856 | tf_op jit(solution)/shard_map/all_gather | solution.py:329
  341.9 83.9 %copy-start.13 = (f32[144]{0:T(256)S(1)}, f32[144]{0:T(256)}, u32[]{:S(2)}) copy-start(f32[144]{0:T(256)} %param.7) | copy-start | bytes 1732
Sparse Core Ops, SparseCore 0:
  42.3 73.8 all-gather.2
  345.3 107.7 all-gather.4

commit v7 on v5

--- a/solution.py
+++ b/solution.py
@@ -144,20 +144,15 @@
     own_pair = jnp.where(is_even, rotate(pair_proj, cos_table, sin_table), pair_proj).astype(
         jnp.bfloat16
     )
-    partner = from_partner(own_pair, "wt", 0)
-    key_rows = jnp.where(is_even, own_pair, partner)
-    value_rows = jnp.where(is_even, partner, own_pair)
     reach_slabs = lax.axis_size("seq") // 2
     window = reach_slabs * tok_rows
-    key_value = jnp.concatenate([key_rows, value_rows], axis=1)
-    key_list = [key_rows]
-    value_list = [value_rows]
+    own_list = [own_pair]
     for offset in range(1, reach_slabs + 1):
-        prev = shifted(key_value, "seq", offset)
-        key_list.append(prev[:, :HD])
-        value_list.append(prev[:, HD:])
-    key_all = jnp.concatenate(key_list, axis=0)
-    value_all = jnp.concatenate(value_list, axis=0)
+        own_list.append(shifted(own_pair, "seq", offset))
+    own_all = jnp.concatenate(own_list, axis=0)
+    partner_all = from_partner(own_all, "wt", 0)
+    key_all = jnp.where(is_even, own_all, partner_all)
+    value_all = jnp.where(is_even, partner_all, own_all)
     local_index = jnp.arange(tok_rows, dtype=jnp.int32)
     query_index = slab_index * tok_rows + local_index
     key_index = jnp.concatenate(
@@ -184,22 +179,13 @@
     query_grad = (rotate(rot_grad, cos_table, -sin_table) * query_scale).astype(jnp.bfloat16)
     key_grads = contract_rows(score_low, query_rot)
     value_grads = contract_rows(probs_low, out_grad)
-    key_total = key_grads[:tok_rows]
-    value_total = value_grads[:tok_rows]
+    outbound = jnp.where(is_even, value_grads, key_grads).astype(jnp.bfloat16)
+    partner_grads = from_partner(outbound, "wt", 0).astype(jnp.float32)
+    own_grads = jnp.where(is_even, key_grads, value_grads) + partner_grads
+    pair_total = own_grads[:tok_rows]
     for offset in range(1, reach_slabs + 1):
-        piece = jnp.concatenate(
-            [
-                key_grads[offset * tok_rows : (offset + 1) * tok_rows].astype(jnp.bfloat16),
-                value_grads[offset * tok_rows : (offset + 1) * tok_rows].astype(jnp.bfloat16),
-            ],
-            axis=1,
-        )
-        recv = shifted(piece, "seq", -offset).astype(jnp.float32)
-        key_total = key_total + recv[:, :HD]
-        value_total = value_total + recv[:, HD:]
-    outbound = jnp.where(is_even, value_total, key_total)
-    partner_grad = from_partner(outbound.astype(jnp.bfloat16), "wt", 0).astype(outbound.dtype)
-    pair_total = jnp.where(is_even, key_total, value_total) + partner_grad
+        piece = own_grads[offset * tok_rows : (offset + 1) * tok_rows].astype(jnp.bfloat16)
+        pair_total = pair_total + shifted(piece, "seq", -offset).astype(jnp.float32)
     pair_grad = jnp.where(is_even, rotate(pair_total, cos_table, -sin_table), pair_total).astype(
         jnp.bfloat16
     )

time: 463 us -> 431 us (0.931)
  waiting for transfers between devices: 279 us -> 256 us
  starting transfers between devices: 90.6 us -> 83.1 us
    ppermute x16, waiting for transfers between devices: 44.4 us -> 19.4 us  [shifted(): lax.ppermute(value, axis, [(source, source + steps) for source in range(i...]
    all_to_all x1, starting transfers between devices: 15.7 us -> 9.24 us  [body(): lax.all_to_all(jnp.concatenate([block_send.astype(jnp.bfloat16), gain_sen...]
  transfers between devices with their start and end apart: 25 -> 25, of which waited for: 15 -> 14; matrix products, arithmetic and copies ran while one was open for 7% -> 8% of each run, Pallas kernels for 0% -> 0%
where the time goes in v7:
time: 431 us; the launch traced here: 429 us
  waiting for transfers between devices  256 us (59%)
  starting transfers between devices  83.1 us (19%)
  local copies, waits for them, and re-layouts  40.1 us (9%)
  other arithmetic  21.1 us (5%)
  between operations  14.9 us (3%)
  matrix products  14.7 us (3%)
    all_to_all x1, waiting for transfers between devices, body(): lax.all_to_all(packed.reshape(groups, feat + pad_rows, tok_rows), 'wt', s...  79.3 us
    all_to_all x1, waiting for transfers between devices, body(): lax.all_to_all(jnp.concatenate([block_send.astype(jnp.bfloat16), gain_sen...  52.4 us
    all_to_all x1, waiting for transfers between devices, body(): lax.all_to_all(outgoing[:dump_slot].reshape(groups, CAP, BLK, BLK), 'wt',...  51 us
    ppermute x16, starting transfers between devices, shifted(): lax.ppermute(value, axis, [(source, source + steps) for source in range(i...  35.6 us
    all_gather x1, waiting for transfers between devices, body(): lax.all_gather(gather_send, 'seq', axis=0, tiled=True)  30.8 us
    ppermute x16, waiting for transfers between devices, shifted(): lax.ppermute(value, axis, [(source, source + steps) for source in range(i...  19.4 us
    all_gather x1, waiting for transfers between devices, body(): lax.all_gather(jnp.concatenate([tokens_in, gain_rows, jnp.zeros((side_row...  15.7 us
    all_to_all x1, starting transfers between devices, body(): lax.all_to_all(outgoing_pos[:dump_slot].reshape(groups, CAP), 'wt', split...  10.2 us
  transfers between devices with their start and end apart: 25, of which 14 were waited for; matrix products, arithmetic and copies ran while one was open for 8% of the time, Pallas kernels for 0%

profile of v7, /device:TPU:6, one launch (start us, length us, event | category | flops | bytes accessed | tf_op | source)
XLA Modules:
  0.0 429.4 jit_solution(4075557428488757041)
XLA Ops:
  9.5 0.8 scatter_custom_fusion
  10.3 0.7 all_to_all.24
  11.1 10.2 %all-to-all-start = ((bf16[32,1,2]{2,1,0:T(2,128)(2,1)}), bf16[32,1,2]{2,1,0:T(2,128)(2,1)S(1)}, u32[]{:S(2)}, u32[]{:S(2)}) async-start(bf16[32,1,2]{2,1,0:T(2,128)(2,1)} %all_to_all.24), calls=%async_computation | async-start | bytes 32768 | tf_op jit(solution)/shard_map/all_to_all | solution.py:99
  21.8 6.7 %scatter_fusion = bf16[65,128,128]{2,1,0:T(8,128)(2,1)S(1)} fusion(bf16[65,128,128]{2,1,0:T(8,128)(2,1)S(1)} %broadcast_in_dim.31, s32[64]{0:T(128)S(1)} %fusion.74, bf16[64,128,128]{2,1,0:T(8,128)(2,1)} %bitcast.154), kind=kCustom, calls=%fused_computation.3 | custom fusion | bytes 6291712 | tf_op jit(solution)/shard_map/scatter | solution.py:84
  28.5 1.5 slice.186
  30.0 9.9 %all-to-all-start.1 = ((bf16[32,2,128,128]{3,2,1,0:T(8,128)(2,1)}), bf16[32,2,128,128]{3,2,1,0:T(8,128)(2,1)S(1)}, u32[]{:S(2)}, u32[]{:S(2)}) async-start(bf16[32,2,128,128]{3,2,1,0:T(8,128)(2,1)} %bitcast.146), calls=%async_computation.1 | async-start | bytes 4194304 | tf_op jit(solution)/shard_map/all_to_all | solution.py:92
  40.2 0.8 concatenate.50
  41.5 51.0 %all-to-all-done.1 = bf16[32,2,128,128]{3,2,1,0:T(8,128)(2,1)S(1)} async-done(((bf16[32,2,128,128]{3,2,1,0:T(8,128)(2,1)}), bf16[32,2,128,128]{3,2,1,0:T(8,128)(2,1)S(1)}, u32[]{:S(2)}, u32[]{:S(2)}) %all-to-all-start.1) | async-done | bytes 2097184 | tf_op jit(solution)/shard_map/all_to_all | solution.py:92
  92.5 1.3 copy-done.2
  94.4 6.6 %scatter_fusion.1 = bf16[73,128,128]{2,1,0:T(8,128)(2,1)S(1)} fusion(bf16[73,128,128]{2,1,0:T(8,128)(2,1)S(1)} %broadcast_in_dim.27, s32[64]{0:T(128)S(1)} %fusion.75, bf16[64,128,128]{2,1,0:T(8,128)(2,1)} %bitcast.145), kind=kCustom, calls=%fused_computation.4 | custom fusion | bytes 6291712 | tf_op jit(solution)/shard_map/scatter | solution.py:136
  101.1 1.6 fusion.93
  102.7 15.7 %all-gather.3.cloned.1.call-done = bf16[232,4608]{0,1:T(8,128)(2,1)} async-done(((bf16[232,144]{0,1:T(8,128)(2,1)}), bf16[232,4608]{0,1:T(8,128)(2,1)}) %all-gather.3.cloned.1.call-update) | async-done | bytes 2138128 | tf_op jit(solution)/shard_map/all_gather | solution.py:113
  118.4 2.8 copy.55
  121.7 1.6 slice_convert_fusion
  123.4 2.2 fusion.14
  125.6 0.8 fusion.85
  127.0 3.8 collective-permute-start
  130.8 3.6 collective-permute-start.1
  134.3 4.2 collective-permute-start.2
  138.6 4.9 %collective-permute-start.3 = (bf16[224,128]{1,0:T(8,128)(2,1)S(1)}, bf16[224,128]{1,0:T(8,128)(2,1)S(1)}, u32[]{:S(2)}, u32[]{:S(2)}) collective-permute-start(bf16[224,128]{1,0:T(8,128)(2,1)S(1)} %get-tuple-element.9), channel_id=1, source_target_pairs={{0,128},{32,160},{64,192},{96,224},{128,256},{160,288},{192,320},{... | collective-permute-start | bytes 172040 | tf_op jit(solution)/shard_map/ppermute | solution.py:30
  143.5 4.1 collective-permute-start.4
  147.7 1.3 collective-permute-start.5
  149.0 1.8 collective-permute-start.6
  150.9 1.3 collective-permute-start.7
  152.7 1.5 collective-permute-done.7
  154.2 2.1 collective-permute-start.8
  156.3 0.9 fusion.87
  158.0 1.1 fusion.89
  159.1 1.4 multiply_reduce_fusion
  160.6 1.2 fusion.13
  162.3 1.1 select_convert_fusion
  163.3 2.2 collective-permute-start.9
  167.4 1.3 collective-permute-start.10
  168.7 1.3 collective-permute-start.11
  170.0 1.3 collective-permute-start.12
  171.3 2.6 fusion.96
  173.9 1.3 collective-permute-start.13
  175.2 1.3 collective-permute-start.14
  176.5 1.3 collective-permute-start.15
  177.8 1.3 collective-permute-start.16
  179.4 1.5 collective-permute-start.17
  180.9 0.9 fusion.83
  181.8 4.8 %collective-permute-done.13 = bf16[224,128]{1,0:T(8,128)(2,1)S(1)} collective-permute-done((bf16[224,128]{1,0:T(8,128)(2,1)S(1)}, bf16[224,128]{1,0:T(8,128)(2,1)S(1)}, u32[]{:S(2)}, u32[]{:S(2)}) %collective-permute-start.13) | collective-permute-done | bytes 57376 | tf_op jit(solution)/shard_map/ppermute | solution.py:30
  186.6 3.2 collective-permute-done.14
  189.8 9.2 %collective-permute-done.15 = bf16[224,128]{1,0:T(8,128)(2,1)S(1)} collective-permute-done((bf16[224,128]{1,0:T(8,128)(2,1)S(1)}, bf16[224,128]{1,0:T(8,128)(2,1)S(1)}, u32[]{:S(2)}, u32[]{:S(2)}) %collective-permute-start.15) | collective-permute-done | bytes 57376 | tf_op jit(solution)/shard_map/ppermute | solution.py:30
  199.7 0.9 fusion.81
  200.6 1.8 maximum_maximum_fusion
  202.4 3.8 gather_fusion
  206.2 3.6 copy.52
  209.8 2.8 fusion.7
  213.0 3.1 pad_maximum_fusion.1
  216.1 9.2 %all-to-all-start.3 = ((bf16[16,528,128]{2,1,0:T(8,128)(2,1)}), bf16[16,528,128]{2,1,0:T(8,128)(2,1)S(1)}, u32[]{:S(2)}, u32[]{:S(2)}) async-start(bf16[16,528,128]{2,1,0:T(8,128)(2,1)} %pad_maximum_fusion.1), calls=%async_computation.3 | async-start | bytes 4325376 | tf_op jit(solution)/shard_map/all_to_all | solution.py:254
  225.4 52.4 %all-to-all-done.3 = bf16[16,528,128]{2,1,0:T(8,128)(2,1)S(1)} async-done(((bf16[16,528,128]{2,1,0:T(8,128)(2,1)}), bf16[16,528,128]{2,1,0:T(8,128)(2,1)S(1)}, u32[]{:S(2)}, u32[]{:S(2)}) %all-to-all-start.3) | async-done | bytes 2162720 | tf_op jit(solution)/shard_map/all_to_all | solution.py:254
  278.9 0.7 pad_maximum_fusion.2
  279.7 7.4 %all-to-all-start.4 = ((bf16[32,32,128]{2,1,0:T(8,128)(2,1)}), bf16[32,32,128]{2,1,0:T(8,128)(2,1)S(1)}, u32[]{:S(2)}, u32[]{:S(2)}) async-start(bf16[32,32,128]{2,1,0:T(8,128)(2,1)} %pad_maximum_fusion.2), calls=%async_computation.4 | async-start | bytes 524288 | tf_op jit(solution)/shard_map/all_to_all | solution.py:273
  287.1 2.8 copy.51
  290.0 2.0 pad_maximum_fusion
  292.0 6.2 %all-to-all-done.4 = bf16[32,32,128]{2,1,0:T(8,128)(2,1)S(1)} async-done(((bf16[32,32,128]{2,1,0:T(8,128)(2,1)}), bf16[32,32,128]{2,1,0:T(8,128)(2,1)S(1)}, u32[]{:S(2)}, u32[]{:S(2)}) %all-to-all-start.4) | async-done | bytes 262176 | tf_op jit(solution)/shard_map/all_to_all | solution.py:273
  298.2 6.3 %all-to-all-start.2 = ((bf16[32,160,224]{2,1,0:T(8,128)(2,1)}), bf16[32,160,224]{2,1,0:T(8,128)(2,1)S(1)}, u32[]{:S(2)}, u32[]{:S(2)}) async-start(bf16[32,160,224]{2,1,0:T(8,128)(2,1)} %pad_maximum_fusion), calls=%async_computation.2 | async-start | bytes 5242880 | tf_op jit(solution)/shard_map/all_to_all | solution.py:209
  306.2 79.3 %all-to-all-done.2 = bf16[32,160,224]{2,1,0:T(8,128)(2,1)S(1)} async-done(((bf16[32,160,224]{2,1,0:T(8,128)(2,1)}), bf16[32,160,224]{2,1,0:T(8,128)(2,1)S(1)}, u32[]{:S(2)}, u32[]{:S(2)}) %all-to-all-start.2) | async-done | bytes 2293792 | tf_op jit(solution)/shard_map/all_to_all | solution.py:209
  386.0 0.7 fusion.42
  386.7 30.8 %all-gather.5.cloned.1.call-done = bf16[8448,128]{1,0:T(8,128)(2,1)} async-done(((bf16[528,128]{1,0:T(8,128)(2,1)}), bf16[8448,128]{1,0:T(8,128)(2,1)}) %all-gather.5.cloned.1.call-update) | async-done | bytes 2162704 | tf_op jit(solution)/shard_map/all_gather | solution.py:297
  417.5 3.5 copy_bitcast_fusion
  421.0 0.9 slice_convert_fusion.2
  (122 shorter events, 14.1 us)
Async XLA Ops:
  11.1 18.9 %all-to-all-start = ((bf16[32,1,2]{2,1,0:T(2,128)(2,1)}), bf16[32,1,2]{2,1,0:T(2,128)(2,1)S(1)}, u32[]{:S(2)}, u32[]{:S(2)}) async-start(bf16[32,1,2]{2,1,0:T(2,128)(2,1)} %all_to_all.24), calls=%async_computation | async-start | bytes 32768 | tf_op jit(solution)/shard_map/all_to_all | solution.py:99
  29.9 10.0 %copy-start.5 = (f32[144]{0:T(256)S(1)}, f32[144]{0:T(256)}, u32[]{:S(2)}) copy-start(f32[144]{0:T(256)} %param.7) | copy-start | bytes 1732
  29.9 10.3 %copy-start.4 = (bf16[224,144]{0,1:T(8,128)(2,1)S(1)}, bf16[224,144]{0,1:T(8,128)(2,1)}, u32[]{:S(2)}) copy-start(bf16[224,144]{0,1:T(8,128)(2,1)} %param.6) | copy-start | bytes 193540
  30.0 11.3 %copy-start.6 = (s32[224]{0:T(256)S(1)}, s32[224]{0:T(256)}, u32[]{:S(2)}) copy-start(s32[224]{0:T(256)} %param.8) | copy-start | bytes 2692
  30.0 62.6 %all-to-all-start.1 = ((bf16[32,2,128,128]{3,2,1,0:T(8,128)(2,1)}), bf16[32,2,128,128]{3,2,1,0:T(8,128)(2,1)S(1)}, u32[]{:S(2)}, u32[]{:S(2)}) async-start(bf16[32,2,128,128]{3,2,1,0:T(8,128)(2,1)} %bitcast.146), calls=%async_computation.1 | async-start | bytes 4194304 | tf_op jit(solution)/shard_map/all_to_all | solution.py:92
  39.9 78.5 %all-gather.3.cloned.1.call-start = ((), (), s32[]{:S(2)}) async-start(), calls=%async_computation.5 | async-start | bytes 2433024 | tf_op jit(solution)/shard_map/all_gather | solution.py:113
  92.5 1.3 copy-start.2
  123.4 2.2 copy-start.3
  125.6 30.8 %copy-start.1 = (bf16[36,128,128]{2,1,0:T(8,128)(2,1)S(1)}, bf16[36,128,128]{2,1,0:T(8,128)(2,1)}, u32[]{:S(2)}) copy-start(bf16[36,128,128]{2,1,0:T(8,128)(2,1)} %get-tuple-element.13) | copy-start | bytes 3538948
  127.0 20.7 %collective-permute-start = (bf16[224,128]{1,0:T(8,128)(2,1)S(1)}, bf16[224,128]{1,0:T(8,128)(2,1)S(1)}, u32[]{:S(2)}, u32[]{:S(2)}) collective-permute-start(bf16[224,128]{1,0:T(8,128)(2,1)S(1)} %get-tuple-element.9), channel_id=1, source_target_pairs={{0,32},{32,64},{64,96},{96,128},{128,160},{160,192},{192,224},{224... | collective-permute-start | bytes 172040 | tf_op jit(solution)/shard_map/ppermute | solution.py:30
  130.8 18.3 %collective-permute-start.1 = (bf16[224,128]{1,0:T(8,128)(2,1)S(1)}, bf16[224,128]{1,0:T(8,128)(2,1)S(1)}, u32[]{:S(2)}, u32[]{:S(2)}) collective-permute-start(bf16[224,128]{1,0:T(8,128)(2,1)S(1)} %get-tuple-element.9), channel_id=1, source_target_pairs={{0,64},{32,96},{64,128},{96,160},{128,192},{160,224},{192,256},{22... | collective-permute-start | bytes 172040 | tf_op jit(solution)/shard_map/ppermute | solution.py:30
  134.3 16.5 %collective-permute-start.2 = (bf16[224,128]{1,0:T(8,128)(2,1)S(1)}, bf16[224,128]{1,0:T(8,128)(2,1)S(1)}, u32[]{:S(2)}, u32[]{:S(2)}) collective-permute-start(bf16[224,128]{1,0:T(8,128)(2,1)S(1)} %get-tuple-element.9), channel_id=1, source_target_pairs={{0,96},{32,128},{64,160},{96,192},{128,224},{160,256},{192,288},{2... | collective-permute-start | bytes 172040 | tf_op jit(solution)/shard_map/ppermute | solution.py:30
  138.6 13.6 %collective-permute-start.3 = (bf16[224,128]{1,0:T(8,128)(2,1)S(1)}, bf16[224,128]{1,0:T(8,128)(2,1)S(1)}, u32[]{:S(2)}, u32[]{:S(2)}) collective-permute-start(bf16[224,128]{1,0:T(8,128)(2,1)S(1)} %get-tuple-element.9), channel_id=1, source_target_pairs={{0,128},{32,160},{64,192},{96,224},{128,256},{160,288},{192,320},{... | collective-permute-start | bytes 172040 | tf_op jit(solution)/shard_map/ppermute | solution.py:30
  143.5 8.7 %collective-permute-start.4 = (bf16[224,128]{1,0:T(8,128)(2,1)S(1)}, bf16[224,128]{1,0:T(8,128)(2,1)S(1)}, u32[]{:S(2)}, u32[]{:S(2)}) collective-permute-start(bf16[224,128]{1,0:T(8,128)(2,1)S(1)} %get-tuple-element.9), channel_id=1, source_target_pairs={{0,160},{32,192},{64,224},{96,256},{128,288},{160,320},{192,352},{... | collective-permute-start | bytes 172040 | tf_op jit(solution)/shard_map/ppermute | solution.py:30
  147.7 4.5 %collective-permute-start.5 = (bf16[224,128]{1,0:T(8,128)(2,1)S(1)}, bf16[224,128]{1,0:T(8,128)(2,1)S(1)}, u32[]{:S(2)}, u32[]{:S(2)}) collective-permute-start(bf16[224,128]{1,0:T(8,128)(2,1)S(1)} %get-tuple-element.9), channel_id=1, source_target_pairs={{0,192},{32,224},{64,256},{96,288},{128,320},{160,352},{192,384},{... | collective-permute-start | bytes 172040 | tf_op jit(solution)/shard_map/ppermute | solution.py:30
  149.0 3.6 collective-permute-start.6
  150.9 3.3 collective-permute-start.7
  154.2 3.8 collective-permute-start.8
  158.0 1.1 copy-start.7
  163.3 3.8 collective-permute-start.9
  167.4 9.1 %collective-permute-start.10 = (bf16[224,128]{1,0:T(8,128)(2,1)S(1)}, bf16[224,128]{1,0:T(8,128)(2,1)S(1)}, u32[]{:S(2)}, u32[]{:S(2)}) collective-permute-start(bf16[224,128]{1,0:T(8,128)(2,1)S(1)} %get-tuple-element.15), channel_id=1, source_target_pairs={{32,0},{64,32},{96,64},{128,96},{160,128},{192,160},{224,192},{256... | collective-permute-start | bytes 172040 | tf_op jit(solution)/shard_map/ppermute | solution.py:30
  168.7 9.1 %collective-permute-start.11 = (bf16[224,128]{1,0:T(8,128)(2,1)S(1)}, bf16[224,128]{1,0:T(8,128)(2,1)S(1)}, u32[]{:S(2)}, u32[]{:S(2)}) collective-permute-start(bf16[224,128]{1,0:T(8,128)(2,1)S(1)} %get-tuple-element.22), channel_id=1, source_target_pairs={{64,0},{96,32},{128,64},{160,96},{192,128},{224,160},{256,192},{28... | collective-permute-start | bytes 172040 | tf_op jit(solution)/shard_map/ppermute | solution.py:30
  170.0 9.4 %collective-permute-start.12 = (bf16[224,128]{1,0:T(8,128)(2,1)S(1)}, bf16[224,128]{1,0:T(8,128)(2,1)S(1)}, u32[]{:S(2)}, u32[]{:S(2)}) collective-permute-start(bf16[224,128]{1,0:T(8,128)(2,1)S(1)} %get-tuple-element.21), channel_id=1, source_target_pairs={{96,0},{128,32},{160,64},{192,96},{224,128},{256,160},{288,192},{3... | collective-permute-start | bytes 172040 | tf_op jit(solution)/shard_map/ppermute | solution.py:30
  173.9 12.7 %collective-permute-start.13 = (bf16[224,128]{1,0:T(8,128)(2,1)S(1)}, bf16[224,128]{1,0:T(8,128)(2,1)S(1)}, u32[]{:S(2)}, u32[]{:S(2)}) collective-permute-start(bf16[224,128]{1,0:T(8,128)(2,1)S(1)} %get-tuple-element.20), channel_id=1, source_target_pairs={{128,0},{160,32},{192,64},{224,96},{256,128},{288,160},{320,192},{... | collective-permute-start | bytes 172040 | tf_op jit(solution)/shard_map/ppermute | solution.py:30
  175.2 14.6 %collective-permute-start.14 = (bf16[224,128]{1,0:T(8,128)(2,1)S(1)}, bf16[224,128]{1,0:T(8,128)(2,1)S(1)}, u32[]{:S(2)}, u32[]{:S(2)}) collective-permute-start(bf16[224,128]{1,0:T(8,128)(2,1)S(1)} %get-tuple-element.19), channel_id=1, source_target_pairs={{160,0},{192,32},{224,64},{256,96},{288,128},{320,160},{352,192},{... | collective-permute-start | bytes 172040 | tf_op jit(solution)/shard_map/ppermute | solution.py:30
  176.5 22.5 %collective-permute-start.15 = (bf16[224,128]{1,0:T(8,128)(2,1)S(1)}, bf16[224,128]{1,0:T(8,128)(2,1)S(1)}, u32[]{:S(2)}, u32[]{:S(2)}) collective-permute-start(bf16[224,128]{1,0:T(8,128)(2,1)S(1)} %get-tuple-element.18), channel_id=1, source_target_pairs={{192,0},{224,32},{256,64},{288,96},{320,128},{352,160},{384,192},{... | collective-permute-start | bytes 172040 | tf_op jit(solution)/shard_map/ppermute | solution.py:30
  177.8 21.2 %collective-permute-start.16 = (bf16[224,128]{1,0:T(8,128)(2,1)S(1)}, bf16[224,128]{1,0:T(8,128)(2,1)S(1)}, u32[]{:S(2)}, u32[]{:S(2)}) collective-permute-start(bf16[224,128]{1,0:T(8,128)(2,1)S(1)} %get-tuple-element.17), channel_id=1, source_target_pairs={{224,0},{256,32},{288,64},{320,96},{352,128},{384,160},{416,192},{... | collective-permute-start | bytes 172040 | tf_op jit(solution)/shard_map/ppermute | solution.py:30
  179.4 19.6 %collective-permute-start.17 = (bf16[224,128]{1,0:T(8,128)(2,1)S(1)}, bf16[224,128]{1,0:T(8,128)(2,1)S(1)}, u32[]{:S(2)}, u32[]{:S(2)}) collective-permute-start(bf16[224,128]{1,0:T(8,128)(2,1)S(1)} %get-tuple-element.16), channel_id=1, source_target_pairs={{256,0},{288,32},{320,64},{352,96},{384,128},{416,160},{448,192},{... | collective-permute-start | bytes 172040 | tf_op jit(solution)/shard_map/ppermute | solution.py:30
  206.2 3.7 copy-start
  216.1 61.7 %all-to-all-start.3 = ((bf16[16,528,128]{2,1,0:T(8,128)(2,1)}), bf16[16,528,128]{2,1,0:T(8,128)(2,1)S(1)}, u32[]{:S(2)}, u32[]{:S(2)}) async-start(bf16[16,528,128]{2,1,0:T(8,128)(2,1)} %pad_maximum_fusion.1), calls=%async_computation.3 | async-start | bytes 4325376 | tf_op jit(solution)/shard_map/all_to_all | solution.py:254
  279.7 18.6 %all-to-all-start.4 = ((bf16[32,32,128]{2,1,0:T(8,128)(2,1)}), bf16[32,32,128]{2,1,0:T(8,128)(2,1)S(1)}, u32[]{:S(2)}, u32[]{:S(2)}) async-start(bf16[32,32,128]{2,1,0:T(8,128)(2,1)} %pad_maximum_fusion.2), calls=%async_computation.4 | async-start | bytes 524288 | tf_op jit(solution)/shard_map/all_to_all | solution.py:273
  298.2 87.3 %all-to-all-start.2 = ((bf16[32,160,224]{2,1,0:T(8,128)(2,1)}), bf16[32,160,224]{2,1,0:T(8,128)(2,1)S(1)}, u32[]{:S(2)}, u32[]{:S(2)}) async-start(bf16[32,160,224]{2,1,0:T(8,128)(2,1)} %pad_maximum_fusion), calls=%async_computation.2 | async-start | bytes 5242880 | tf_op jit(solution)/shard_map/all_to_all | solution.py:209
  304.5 113.0 %all-gather.5.cloned.1.call-start = ((), (), s32[]{:S(2)}) async-start(), calls=%async_computation.6 | async-start | bytes 2297856 | tf_op jit(solution)/shard_map/all_gather | solution.py:297
Sparse Core Ops, SparseCore 0:
  44.4 73.9 all-gather.2
  308.0 109.4 all-gather.4

commit v8 on v7

--- a/solution.py
+++ b/solution.py
@@ -11,6 +11,7 @@
 
 query_scale = 144.0 ** (-0.5)
 soft_cap = 50.0
+WT = ("chip", "core")
 norm_eps = 1e-06
 
 
@@ -65,9 +66,9 @@
 def body(tokens_in, norm_gain, positions, blocks, slot_code, out_grad):
     tok_rows = tokens_in.shape[0]
     feat = tokens_in.shape[1]
-    groups = lax.axis_size("wt")
+    groups = lax.axis_size(WT)
     slab_index = lax.axis_index("seq")
-    is_even = lax.axis_index("wt") % 2 == 0
+    is_even = lax.axis_index(WT) % 2 == 0
     pos_count = 2 * (D // BLK)
     row_blocks = pos_count // 2
     slot_codes = slot_code[0]
@@ -91,14 +92,14 @@
     arrived, arrived_pos = (
         lax.all_to_all(
             outgoing[:dump_slot].reshape(groups, CAP, BLK, BLK),
-            "wt",
+            WT,
             split_axis=0,
             concat_axis=0,
             tiled=True,
         ),
         lax.all_to_all(
             outgoing_pos[:dump_slot].reshape(groups, CAP),
-            "wt",
+            WT,
             split_axis=0,
             concat_axis=0,
             tiled=True,
@@ -110,14 +111,24 @@
     gain_lo = gain_rest - gain_mid
     gain_rows = jnp.stack([gain_hi, gain_mid, gain_lo]).astype(jnp.bfloat16)
     side_rows = 8
-    gathered = lax.all_gather(
+    half = lax.all_gather(
         jnp.concatenate(
             [tokens_in, gain_rows, jnp.zeros((side_rows - 3, feat), jnp.bfloat16)], axis=0
         ),
-        "wt",
+        "chip",
         axis=1,
         tiled=True,
     )
+    other_half = from_partner(half, "core", 0)
+    first_core = lax.axis_index("core") == 0
+    chips = lax.axis_size("chip")
+    gathered = jnp.stack(
+        [
+            jnp.where(first_core, half, other_half).reshape(-1, chips, feat),
+            jnp.where(first_core, other_half, half).reshape(-1, chips, feat),
+        ],
+        axis=2,
+    ).reshape(-1, chips * 2 * feat)
     tokens_full = gathered[:tok_rows]
     gain_parts = gathered[tok_rows : tok_rows + 3].astype(jnp.float32)
     gain_full = (gain_parts[0] + gain_parts[1]) + gain_parts[2]
@@ -150,7 +161,7 @@
     for offset in range(1, reach_slabs + 1):
         own_list.append(shifted(own_pair, "seq", offset))
     own_all = jnp.concatenate(own_list, axis=0)
-    partner_all = from_partner(own_all, "wt", 0)
+    partner_all = from_partner(own_all, "core", 0)
     key_all = jnp.where(is_even, own_all, partner_all)
     value_all = jnp.where(is_even, partner_all, own_all)
     local_index = jnp.arange(tok_rows, dtype=jnp.int32)
@@ -180,7 +191,7 @@
     key_grads = contract_rows(score_low, query_rot)
     value_grads = contract_rows(probs_low, out_grad)
     outbound = jnp.where(is_even, value_grads, key_grads).astype(jnp.bfloat16)
-    partner_grads = from_partner(outbound, "wt", 0).astype(jnp.float32)
+    partner_grads = from_partner(outbound, "core", 0).astype(jnp.float32)
     own_grads = jnp.where(is_even, key_grads, value_grads) + partner_grads
     pair_total = own_grads[:tok_rows]
     for offset in range(1, reach_slabs + 1):
@@ -208,7 +219,7 @@
     scattered = jnp.sum(
         lax.all_to_all(
             packed.reshape(groups, feat + pad_rows, tok_rows),
-            "wt",
+            WT,
             split_axis=0,
             concat_axis=0,
             tiled=True,
@@ -272,7 +283,7 @@
     ).reshape(groups, side, BLK)
     wt_recv = lax.all_to_all(
         jnp.concatenate([block_chunk, gain_slots], axis=1),
-        "wt",
+        WT,
         split_axis=0,
         concat_axis=0,
         tiled=True,
@@ -313,18 +324,22 @@
 
 
 def solution(mesh):
+    seq_count, wt_count = mesh.devices.shape
+    split_mesh = jax.sharding.Mesh(
+        mesh.devices.reshape(seq_count, wt_count // 2, 2), ("seq", "chip", "core")
+    )
     placed = (
-        P("seq", "wt"),
-        P("wt"),
+        P("seq", WT),
+        P(WT),
         P("seq"),
-        P("wt", None, None, None),
-        P("wt", None),
-        P("seq", "wt"),
+        P(WT, None, None, None),
+        P(WT, None),
+        P("seq", WT),
     )
     return jax.shard_map(
         body,
-        mesh=mesh,
+        mesh=split_mesh,
         in_specs=placed,
-        out_specs=(P("seq", "wt"), P("seq", "wt"), P("wt"), P("wt", None, None, None)),
+        out_specs=(P("seq", WT), P("seq", WT), P(WT), P(WT, None, None, None)),
         check_vma=False,
     )

time: 431 us -> 467 us (1.084)
  local copies, waits for them, and re-layouts: 40.1 us -> 67.3 us
  waiting for transfers between devices: 256 us -> 238 us
  starting transfers between devices: 83.1 us -> 101 us
  other arithmetic: 21.1 us -> 26.9 us
    all_to_all x4, waiting for transfers between devices: 137 us -> 85.9 us  [the longest x1 79.6 us: body(): lax.all_to_all(packed.reshape(groups, feat + pad_rows, tok_rows), WT, spl...]
    all_gather x1, waiting for transfers between devices: 15.7 us -> 55.4 us  [body(): lax.all_gather(jnp.concatenate([tokens_in, gain_rows, jnp.zeros((side_row...]
    convert_element_type x0 -> x3, local copies, waits for them, and re-layouts: none -> 12.5 us  [the longest x2 10.9 us: body(): full_f32 = tokens_full.astype(jnp.float32)]
    ppermute x16, starting transfers between devices: 35.6 us -> 47.6 us  [shifted(): lax.ppermute(value, axis, [(source, source + steps) for source in range(i...]
    ppermute x16, waiting for transfers between devices: 19.4 us -> 13.2 us  [shifted(): lax.ppermute(value, axis, [(source, source + steps) for source in range(i...]
  transfers between devices with their start and end apart: 25 -> 26, of which waited for: 14 -> 15; matrix products, arithmetic and copies ran while one was open for 8% -> 13% of each run, Pallas kernels for 0% -> 0%
where the time goes in v8:
time: 467 us; the launch traced here: 465 us
  waiting for transfers between devices  238 us (51%)
  starting transfers between devices  101 us (22%)
  local copies, waits for them, and re-layouts  67.3 us (14%)
  other arithmetic  26.9 us (6%)
  matrix products  16.7 us (4%)
  between operations  14.9 us (3%)
    all_to_all x1, waiting for transfers between devices, body(): lax.all_to_all(packed.reshape(groups, feat + pad_rows, tok_rows), WT, spl...  79.6 us
    all_gather x1, waiting for transfers between devices, body(): lax.all_gather(jnp.concatenate([tokens_in, gain_rows, jnp.zeros((side_row...  55.4 us
    all_to_all x1, waiting for transfers between devices, body(): lax.all_to_all(jnp.concatenate([block_send.astype(jnp.bfloat16), gain_sen...  52.4 us
    ppermute x16, starting transfers between devices, shifted(): lax.ppermute(value, axis, [(source, source + steps) for source in range(i...  47.6 us
    all_gather x1, waiting for transfers between devices, body(): lax.all_gather(gather_send, 'seq', axis=0, tiled=True)  29.4 us
    ppermute x16, waiting for transfers between devices, shifted(): lax.ppermute(value, axis, [(source, source + steps) for source in range(i...  13.2 us
    all_to_all x1, starting transfers between devices, body(): lax.all_to_all(jnp.concatenate([block_send.astype(jnp.bfloat16), gain_sen...  11.3 us
    convert_element_type x2, local copies, waits for them, and re-layouts, body(): full_f32 = tokens_full.astype(jnp.float32)  10.9 us
  transfers between devices with their start and end apart: 26, of which 15 were waited for; matrix products, arithmetic and copies ran while one was open for 13% of the time, Pallas kernels for 0%

profile of v8, /device:TPU:6, one launch (start us, length us, event | category | flops | bytes accessed | tf_op | source)
XLA Modules:
  0.0 465.3 jit_solution(13582906249132133294)
XLA Ops:
  8.2 1.6 concatenate.50
  13.7 10.2 %all-to-all-start = ((bf16[32,1,2]{2,1,0:T(2,128)(2,1)}), bf16[32,1,2]{2,1,0:T(2,128)(2,1)S(1)}, u32[]{:S(2)}, u32[]{:S(2)}) async-start(bf16[32,1,2]{2,1,0:T(2,128)(2,1)} %all_to_all.24), calls=%async_computation | async-start | bytes 32768 | tf_op jit(solution)/shard_map/all_to_all | solution.py:100
  24.5 6.7 %scatter_fusion = bf16[65,128,128]{2,1,0:T(8,128)(2,1)S(1)} fusion(bf16[65,128,128]{2,1,0:T(8,128)(2,1)S(1)} %broadcast_in_dim.31, s32[64]{0:T(128)S(1)} %fusion.76, bf16[64,128,128]{2,1,0:T(8,128)(2,1)} %bitcast.181), kind=kCustom, calls=%fused_computation.3 | custom fusion | bytes 6291712 | tf_op jit(solution)/shard_map/scatter | solution.py:85
  31.2 1.5 slice.191
  32.6 9.8 %all-to-all-start.1 = ((bf16[32,2,128,128]{3,2,1,0:T(8,128)(2,1)}), bf16[32,2,128,128]{3,2,1,0:T(8,128)(2,1)}, u32[]{:S(2)}, u32[]{:S(2)}) async-start(bf16[32,2,128,128]{3,2,1,0:T(8,128)(2,1)} %bitcast.176), calls=%async_computation.1 | async-start | bytes 4194304 | tf_op jit(solution)/shard_map/all_to_all | solution.py:93
  43.1 55.4 %all-gather.3.cloned.1.call-done = bf16[232,2304]{0,1:T(8,128)(2,1)} async-done(((bf16[232,144]{0,1:T(8,128)(2,1)}), bf16[232,2304]{0,1:T(8,128)(2,1)}) %all-gather.3.cloned.1.call-update) | async-done | bytes 1069072 | tf_op jit(solution)/shard_map/all_gather | solution.py:114
  98.5 1.7 copy.101
  100.2 1.9 collective-permute-start
  104.8 1.4 copy.102
  106.2 1.4 broadcast_select_fusion.1
  108.7 2.7 fusion.87
  112.2 1.6 copy.104
  113.9 2.0 broadcast_in_dim.27
  115.9 9.9 %scatter_fusion.1 = bf16[73,128,128]{2,1,0:T(8,128)(2,1)} fusion(bf16[73,128,128]{2,1,0:T(8,128)(2,1)} %broadcast_in_dim.27, s32[64]{0:T(128)S(1)} %copy-done.15, bf16[64,128,128]{2,1,0:T(8,128)(2,1)} %bitcast.12), kind=kCustom, calls=%fused_computation.4 | custom fusion | bytes 6291712 | tf_op jit(solution)/shard_map/scatter | solution.py:147
  125.8 1.9 fusion.88
  130.3 1.9 collective-permute-start.1
  132.2 2.8 maximum_convert_fusion
  134.9 2.9 copy.109
  138.5 5.0 %copy.107 = f32[224,16,2,144]{0,3,2,1:T(8,128)} copy(f32[224,16,2,144]{0,3,1,2:T(8,128)} %maximum_convert_fusion) | data formatting | bytes 8257536 | tf_op jit(solution)/shard_map/convert_element_type | solution.py:135
  143.5 6.0 %copy.108 = f32[224,4608]{1,0:T(8,128)} copy(f32[224,4608]{0,1:T(8,128)} %bitcast.170) | data formatting | bytes 8257536 | tf_op jit(solution)/shard_map/convert_element_type | solution.py:135
  149.4 11.0 %collective-permute-start.8 = (bf16[224,128]{1,0:T(8,128)(2,1)}, bf16[224,128]{1,0:T(8,128)(2,1)S(1)}, u32[]{:S(2)}, u32[]{:S(2)}) collective-permute-start(bf16[224,128]{1,0:T(8,128)(2,1)} %get-tuple-element.9), channel_id=1, source_target_pairs={{0,256},{32,288},{64,320},{96,352},{128,384},{160,416},{192,448},{... | collective-permute-start | bytes 172040 | tf_op jit(solution)/shard_map/ppermute | solution.py:31
  160.4 2.7 collective-permute-start.7
  163.1 4.7 %collective-permute-start.6 = (bf16[224,128]{1,0:T(8,128)(2,1)}, bf16[224,128]{1,0:T(8,128)(2,1)S(1)}, u32[]{:S(2)}, u32[]{:S(2)}) collective-permute-start(bf16[224,128]{1,0:T(8,128)(2,1)} %get-tuple-element.9), channel_id=1, source_target_pairs={{0,192},{32,224},{64,256},{96,288},{128,320},{160,352},{192,384},{... | collective-permute-start | bytes 172040 | tf_op jit(solution)/shard_map/ppermute | solution.py:31
  167.9 1.3 collective-permute-start.5
  169.2 2.5 collective-permute-start.2
  171.8 1.4 constant_dynamic-update-slice_fusion.7
  173.9 5.9 %collective-permute-start.3 = (bf16[224,128]{1,0:T(8,128)(2,1)}, bf16[224,128]{1,0:T(8,128)(2,1)S(1)}, u32[]{:S(2)}, u32[]{:S(2)}) collective-permute-start(bf16[224,128]{1,0:T(8,128)(2,1)} %get-tuple-element.9), channel_id=1, source_target_pairs={{0,96},{32,128},{64,160},{96,192},{128,224},{160,256},{192,288},{2... | collective-permute-start | bytes 172040 | tf_op jit(solution)/shard_map/ppermute | solution.py:31
  180.4 1.5 collective-permute-done.3
  181.9 6.7 %collective-permute-start.4 = (bf16[224,128]{1,0:T(8,128)(2,1)}, bf16[224,128]{1,0:T(8,128)(2,1)S(1)}, u32[]{:S(2)}, u32[]{:S(2)}) collective-permute-start(bf16[224,128]{1,0:T(8,128)(2,1)} %get-tuple-element.9), channel_id=1, source_target_pairs={{0,128},{32,160},{64,192},{96,224},{128,256},{160,288},{192,320},{... | collective-permute-start | bytes 172040 | tf_op jit(solution)/shard_map/ppermute | solution.py:31
  189.3 1.5 collective-permute-done.4
  193.9 1.9 collective-permute-start.9
  197.9 1.1 fusion.83
  199.0 1.4 multiply_reduce_fusion.1
  200.5 1.2 fusion.6
  202.2 1.1 select_convert_fusion
  203.3 2.0 collective-permute-start.10
  207.3 1.6 collective-permute-start.11
  208.8 1.3 collective-permute-start.18
  210.1 1.3 collective-permute-start.17
  211.4 0.9 fusion.10
  212.4 1.3 collective-permute-start.16
  213.7 1.3 collective-permute-start.15
  215.0 1.3 collective-permute-start.14
  216.3 5.5 %collective-permute-done.18 = bf16[224,128]{1,0:T(8,128)(2,1)S(1)} collective-permute-done((bf16[224,128]{1,0:T(8,128)(2,1)S(1)}, bf16[224,128]{1,0:T(8,128)(2,1)S(1)}, u32[]{:S(2)}, u32[]{:S(2)}) %collective-permute-start.18) | collective-permute-done | bytes 57376 | tf_op jit(solution)/shard_map/ppermute | solution.py:31
  221.8 1.3 collective-permute-start.13
  223.1 1.5 collective-permute-start.12
  224.6 2.7 fusion.93
  227.3 1.5 collective-permute-done.16
  229.6 1.7 collective-permute-done.12
  233.0 1.8 maximum_maximum_fusion
  234.8 4.0 gather_fusion
  238.8 2.3 copy.112
  241.6 4.8 %fusion = (f32[4608]{0:T(1024)S(1)}, f32[224]{0:T(256)S(1)}, bf16[4608,224]{0,1:T(8,128)(2,1)}) fusion(f32[224,4608]{1,0:T(8,128)S(1)} %copy-done.1, f32[224]{0:T(256)S(1)} %add_rsqrt_fusion, f32[4608]{0:T(1024)S(1)} %copy-done.9, f32[4608,224]{0,1:T(8,128)} %fusion.93, bf16[4608,128]{1,0:T(8,128)(2,1)S(1)} %bitcast.174, bf16[224,128]{1,0:T(8,128)(2,1)S(1)} %fusion.61), kind=kOutput, calls=%fused_computation.12 | convolution fusion | flops 272493856 | bytes 11597568 | tf_op jit(solution)/shard_map/dot_general | solution.py:55
  246.7 1.5 pad_maximum_fusion.1
  248.2 11.3 %all-to-all-start.3 = ((bf16[16,528,128]{2,1,0:T(8,128)(2,1)}), bf16[16,528,128]{2,1,0:T(8,128)(2,1)S(1)}, u32[]{:S(2)}, u32[]{:S(2)}) async-start(bf16[16,528,128]{2,1,0:T(8,128)(2,1)} %pad_maximum_fusion.1), calls=%async_computation.3 | async-start | bytes 4325376 | tf_op jit(solution)/shard_map/all_to_all | solution.py:265
  259.6 52.4 %all-to-all-done.3 = bf16[16,528,128]{2,1,0:T(8,128)(2,1)S(1)} async-done(((bf16[16,528,128]{2,1,0:T(8,128)(2,1)}), bf16[16,528,128]{2,1,0:T(8,128)(2,1)S(1)}, u32[]{:S(2)}, u32[]{:S(2)}) %all-to-all-start.3) | async-done | bytes 2162720 | tf_op jit(solution)/shard_map/all_to_all | solution.py:265
  313.9 10.1 %all-to-all-start.4 = ((bf16[32,32,128]{2,1,0:T(8,128)(2,1)}), bf16[32,32,128]{2,1,0:T(8,128)(2,1)S(1)}, u32[]{:S(2)}, u32[]{:S(2)}) async-start(bf16[32,32,128]{2,1,0:T(8,128)(2,1)} %pad_maximum_fusion.3), calls=%async_computation.4 | async-start | bytes 524288 | tf_op jit(solution)/shard_map/all_to_all | solution.py:284
  324.0 2.8 copy.106
  326.9 2.0 pad_maximum_fusion
  328.9 6.2 %all-to-all-done.4 = bf16[32,32,128]{2,1,0:T(8,128)(2,1)S(1)} async-done(((bf16[32,32,128]{2,1,0:T(8,128)(2,1)}), bf16[32,32,128]{2,1,0:T(8,128)(2,1)S(1)}, u32[]{:S(2)}, u32[]{:S(2)}) %all-to-all-start.4) | async-done | bytes 262176 | tf_op jit(solution)/shard_map/all_to_all | solution.py:284
  335.1 6.3 %all-to-all-start.2 = ((bf16[32,160,224]{2,1,0:T(8,128)(2,1)}), bf16[32,160,224]{2,1,0:T(8,128)(2,1)S(1)}, u32[]{:S(2)}, u32[]{:S(2)}) async-start(bf16[32,160,224]{2,1,0:T(8,128)(2,1)} %pad_maximum_fusion), calls=%async_computation.2 | async-start | bytes 5242880 | tf_op jit(solution)/shard_map/all_to_all | solution.py:220
  343.2 79.6 %all-to-all-done.2 = bf16[32,160,224]{2,1,0:T(8,128)(2,1)S(1)} async-done(((bf16[32,160,224]{2,1,0:T(8,128)(2,1)}), bf16[32,160,224]{2,1,0:T(8,128)(2,1)S(1)}, u32[]{:S(2)}, u32[]{:S(2)}) %all-to-all-start.2) | async-done | bytes 2293792 | tf_op jit(solution)/shard_map/all_to_all | solution.py:220
  424.0 29.4 %all-gather.5.cloned.1.call-done = bf16[8448,128]{1,0:T(8,128)(2,1)} async-done(((bf16[528,128]{1,0:T(8,128)(2,1)}), bf16[8448,128]{1,0:T(8,128)(2,1)}) %all-gather.5.cloned.1.call-update) | async-done | bytes 2162704 | tf_op jit(solution)/shard_map/all_gather | solution.py:308
  454.2 3.5 copy_bitcast_fusion
  (161 shorter events, 32.8 us)
Async XLA Ops:
  7.2 91.3 %all-gather.3.cloned.1.call-start = ((), (), s32[]{:S(2)}) async-start(), calls=%async_computation.5 | async-start | bytes 1253376 | tf_op jit(solution)/shard_map/all_gather | solution.py:114
  13.7 18.9 %all-to-all-start = ((bf16[32,1,2]{2,1,0:T(2,128)(2,1)}), bf16[32,1,2]{2,1,0:T(2,128)(2,1)S(1)}, u32[]{:S(2)}, u32[]{:S(2)}) async-start(bf16[32,1,2]{2,1,0:T(2,128)(2,1)} %all_to_all.24), calls=%async_computation | async-start | bytes 32768 | tf_op jit(solution)/shard_map/all_to_all | solution.py:100
  32.6 81.2 %all-to-all-start.1 = ((bf16[32,2,128,128]{3,2,1,0:T(8,128)(2,1)}), bf16[32,2,128,128]{3,2,1,0:T(8,128)(2,1)}, u32[]{:S(2)}, u32[]{:S(2)}) async-start(bf16[32,2,128,128]{3,2,1,0:T(8,128)(2,1)} %bitcast.176), calls=%async_computation.1 | async-start | bytes 4194304 | tf_op jit(solution)/shard_map/all_to_all | solution.py:93
  42.5 60.4 %copy-start.16 = (s32[224]{0:T(256)S(1)}, s32[224]{0:T(256)}, u32[]{:S(2)}) copy-start(s32[224]{0:T(256)} %param.8) | copy-start | bytes 2692
  98.5 7.7 %copy-start.6 = (bf16[232,2304]{0,1:T(8,128)(2,1)S(1)}, bf16[232,2304]{0,1:T(8,128)(2,1)}, u32[]{:S(2)}) copy-start(bf16[232,2304]{0,1:T(8,128)(2,1)} %all-gather.3.cloned.1.call-done) | copy-start | bytes 3207172
  100.2 4.6 collective-permute-start
  102.2 2.6 copy-start.17
  103.6 4.1 copy-start.14
  113.8 2.0 copy-start.15
  125.8 2.4 copy-start.2
  127.7 2.5 copy-start.4
  127.7 1.3 copy-start.11
  130.3 38.9 %collective-permute-start.1 = (bf16[224,128]{1,0:T(8,128)(2,1)}, bf16[224,128]{1,0:T(8,128)(2,1)}, u32[]{:S(2)}, u32[]{:S(2)}) collective-permute-start(bf16[224,128]{1,0:T(8,128)(2,1)} %get-tuple-element.9), channel_id=1, source_target_pairs={{0,32},{32,64},{64,96},{96,128},{128,160},{160,192},{192,224},{224... | collective-permute-start | bytes 172040 | tf_op jit(solution)/shard_map/ppermute | solution.py:31
  143.4 52.4 %copy-start.3 = (bf16[224,16,2,144]{0,3,2,1:T(8,128)(2,1)S(1)}, bf16[224,16,2,144]{0,3,2,1:T(8,128)(2,1)}, u32[]{:S(2)}) copy-start(bf16[224,16,2,144]{0,3,2,1:T(8,128)(2,1)} %copy.104) | copy-start | bytes 6193156
  149.4 43.9 %collective-permute-start.8 = (bf16[224,128]{1,0:T(8,128)(2,1)}, bf16[224,128]{1,0:T(8,128)(2,1)S(1)}, u32[]{:S(2)}, u32[]{:S(2)}) collective-permute-start(bf16[224,128]{1,0:T(8,128)(2,1)} %get-tuple-element.9), channel_id=1, source_target_pairs={{0,256},{32,288},{64,320},{96,352},{128,384},{160,416},{192,448},{... | collective-permute-start | bytes 172040 | tf_op jit(solution)/shard_map/ppermute | solution.py:31
  160.4 32.3 %collective-permute-start.7 = (bf16[224,128]{1,0:T(8,128)(2,1)}, bf16[224,128]{1,0:T(8,128)(2,1)S(1)}, u32[]{:S(2)}, u32[]{:S(2)}) collective-permute-start(bf16[224,128]{1,0:T(8,128)(2,1)} %get-tuple-element.9), channel_id=1, source_target_pairs={{0,224},{32,256},{64,288},{96,320},{128,352},{160,384},{192,416},{... | collective-permute-start | bytes 172040 | tf_op jit(solution)/shard_map/ppermute | solution.py:31
  163.1 28.9 %collective-permute-start.6 = (bf16[224,128]{1,0:T(8,128)(2,1)}, bf16[224,128]{1,0:T(8,128)(2,1)S(1)}, u32[]{:S(2)}, u32[]{:S(2)}) collective-permute-start(bf16[224,128]{1,0:T(8,128)(2,1)} %get-tuple-element.9), channel_id=1, source_target_pairs={{0,192},{32,224},{64,256},{96,288},{128,320},{160,352},{192,384},{... | collective-permute-start | bytes 172040 | tf_op jit(solution)/shard_map/ppermute | solution.py:31
  167.9 23.5 %collective-permute-start.5 = (bf16[224,128]{1,0:T(8,128)(2,1)}, bf16[224,128]{1,0:T(8,128)(2,1)S(1)}, u32[]{:S(2)}, u32[]{:S(2)}) collective-permute-start(bf16[224,128]{1,0:T(8,128)(2,1)} %get-tuple-element.9), channel_id=1, source_target_pairs={{0,160},{32,192},{64,224},{96,256},{128,288},{160,320},{192,352},{... | collective-permute-start | bytes 172040 | tf_op jit(solution)/shard_map/ppermute | solution.py:31
  169.2 4.7 %collective-permute-start.2 = (bf16[224,128]{1,0:T(8,128)(2,1)}, bf16[224,128]{1,0:T(8,128)(2,1)S(1)}, u32[]{:S(2)}, u32[]{:S(2)}) collective-permute-start(bf16[224,128]{1,0:T(8,128)(2,1)} %get-tuple-element.9), channel_id=1, source_target_pairs={{0,64},{32,96},{64,128},{96,160},{128,192},{160,224},{192,256},{22... | collective-permute-start | bytes 172040 | tf_op jit(solution)/shard_map/ppermute | solution.py:31
  173.9 8.0 %collective-permute-start.3 = (bf16[224,128]{1,0:T(8,128)(2,1)}, bf16[224,128]{1,0:T(8,128)(2,1)S(1)}, u32[]{:S(2)}, u32[]{:S(2)}) collective-permute-start(bf16[224,128]{1,0:T(8,128)(2,1)} %get-tuple-element.9), channel_id=1, source_target_pairs={{0,96},{32,128},{64,160},{96,192},{128,224},{160,256},{192,288},{2... | collective-permute-start | bytes 172040 | tf_op jit(solution)/shard_map/ppermute | solution.py:31
  181.9 8.8 %collective-permute-start.4 = (bf16[224,128]{1,0:T(8,128)(2,1)}, bf16[224,128]{1,0:T(8,128)(2,1)S(1)}, u32[]{:S(2)}, u32[]{:S(2)}) collective-permute-start(bf16[224,128]{1,0:T(8,128)(2,1)} %get-tuple-element.9), channel_id=1, source_target_pairs={{0,128},{32,160},{64,192},{96,224},{128,256},{160,288},{192,320},{... | collective-permute-start | bytes 172040 | tf_op jit(solution)/shard_map/ppermute | solution.py:31
  189.3 7.4 %copy-start.12 = (f32[64]{0:T(128)S(1)}, f32[64]{0:T(128)}, u32[]{:S(2)}) copy-start(f32[64]{0:T(128)} %multiply_power_fusion) | copy-start | bytes 772
  193.9 4.0 collective-permute-start.9
  195.8 2.1 copy-start.7
  195.8 2.1 copy-start.18
  195.9 2.1 copy-start.19
  197.9 1.1 copy-start.21
  203.3 3.8 collective-permute-start.10
  207.0 4.4 copy-start
  207.0 4.4 copy-start.8
  207.3 7.7 %collective-permute-start.11 = (bf16[224,128]{1,0:T(8,128)(2,1)S(1)}, bf16[224,128]{1,0:T(8,128)(2,1)S(1)}, u32[]{:S(2)}, u32[]{:S(2)}) collective-permute-start(bf16[224,128]{1,0:T(8,128)(2,1)S(1)} %get-tuple-element.19), channel_id=1, source_target_pairs={{32,0},{64,32},{96,64},{128,96},{160,128},{192,160},{224,192},{256... | collective-permute-start | bytes 172040 | tf_op jit(solution)/shard_map/ppermute | solution.py:31
  208.8 13.0 %collective-permute-start.18 = (bf16[224,128]{1,0:T(8,128)(2,1)S(1)}, bf16[224,128]{1,0:T(8,128)(2,1)S(1)}, u32[]{:S(2)}, u32[]{:S(2)}) collective-permute-start(bf16[224,128]{1,0:T(8,128)(2,1)S(1)} %get-tuple-element.20), channel_id=1, source_target_pairs={{256,0},{288,32},{320,64},{352,96},{384,128},{416,160},{448,192},{... | collective-permute-start | bytes 172040 | tf_op jit(solution)/shard_map/ppermute | solution.py:31
  210.1 13.0 %collective-permute-start.17 = (bf16[224,128]{1,0:T(8,128)(2,1)S(1)}, bf16[224,128]{1,0:T(8,128)(2,1)S(1)}, u32[]{:S(2)}, u32[]{:S(2)}) collective-permute-start(bf16[224,128]{1,0:T(8,128)(2,1)S(1)} %get-tuple-element.21), channel_id=1, source_target_pairs={{224,0},{256,32},{288,64},{320,96},{352,128},{384,160},{416,192},{... | collective-permute-start | bytes 172040 | tf_op jit(solution)/shard_map/ppermute | solution.py:31
  212.4 16.5 %collective-permute-start.16 = (bf16[224,128]{1,0:T(8,128)(2,1)S(1)}, bf16[224,128]{1,0:T(8,128)(2,1)S(1)}, u32[]{:S(2)}, u32[]{:S(2)}) collective-permute-start(bf16[224,128]{1,0:T(8,128)(2,1)S(1)} %get-tuple-element.22), channel_id=1, source_target_pairs={{192,0},{224,32},{256,64},{288,96},{320,128},{352,160},{384,192},{... | collective-permute-start | bytes 172040 | tf_op jit(solution)/shard_map/ppermute | solution.py:31
  213.7 15.2 %collective-permute-start.15 = (bf16[224,128]{1,0:T(8,128)(2,1)S(1)}, bf16[224,128]{1,0:T(8,128)(2,1)S(1)}, u32[]{:S(2)}, u32[]{:S(2)}) collective-permute-start(bf16[224,128]{1,0:T(8,128)(2,1)S(1)} %get-tuple-element.23), channel_id=1, source_target_pairs={{160,0},{192,32},{224,64},{256,96},{288,128},{320,160},{352,192},{... | collective-permute-start | bytes 172040 | tf_op jit(solution)/shard_map/ppermute | solution.py:31
  215.0 14.6 %collective-permute-start.14 = (bf16[224,128]{1,0:T(8,128)(2,1)S(1)}, bf16[224,128]{1,0:T(8,128)(2,1)S(1)}, u32[]{:S(2)}, u32[]{:S(2)}) collective-permute-start(bf16[224,128]{1,0:T(8,128)(2,1)S(1)} %get-tuple-element.24), channel_id=1, source_target_pairs={{128,0},{160,32},{192,64},{224,96},{256,128},{288,160},{320,192},{... | collective-permute-start | bytes 172040 | tf_op jit(solution)/shard_map/ppermute | solution.py:31
  221.8 7.8 %collective-permute-start.13 = (bf16[224,128]{1,0:T(8,128)(2,1)S(1)}, bf16[224,128]{1,0:T(8,128)(2,1)S(1)}, u32[]{:S(2)}, u32[]{:S(2)}) collective-permute-start(bf16[224,128]{1,0:T(8,128)(2,1)S(1)} %get-tuple-element.25), channel_id=1, source_target_pairs={{96,0},{128,32},{160,64},{192,96},{224,128},{256,160},{288,192},{3... | collective-permute-start | bytes 172040 | tf_op jit(solution)/shard_map/ppermute | solution.py:31
  223.1 8.3 %collective-permute-start.12 = (bf16[224,128]{1,0:T(8,128)(2,1)S(1)}, bf16[224,128]{1,0:T(8,128)(2,1)S(1)}, u32[]{:S(2)}, u32[]{:S(2)}) collective-permute-start(bf16[224,128]{1,0:T(8,128)(2,1)S(1)} %get-tuple-element.26), channel_id=1, source_target_pairs={{64,0},{96,32},{128,64},{160,96},{192,128},{224,160},{256,192},{28... | collective-permute-start | bytes 172040 | tf_op jit(solution)/shard_map/ppermute | solution.py:31
  232.1 1.0 copy-start.20
  234.8 6.3 %copy-start.5 = (bf16[36,128,128]{2,1,0:T(8,128)(2,1)S(1)}, bf16[36,128,128]{2,1,0:T(8,128)(2,1)}, u32[]{:S(2)}) copy-start(bf16[36,128,128]{2,1,0:T(8,128)(2,1)} %copy-done.4) | copy-start | bytes 3538948
  238.8 2.8 copy-start.1
  238.8 2.8 copy-start.9
  248.2 63.8 %all-to-all-start.3 = ((bf16[16,528,128]{2,1,0:T(8,128)(2,1)}), bf16[16,528,128]{2,1,0:T(8,128)(2,1)S(1)}, u32[]{:S(2)}, u32[]{:S(2)}) async-start(bf16[16,528,128]{2,1,0:T(8,128)(2,1)} %pad_maximum_fusion.1), calls=%async_computation.3 | async-start | bytes 4325376 | tf_op jit(solution)/shard_map/all_to_all | solution.py:265
  313.9 21.2 %all-to-all-start.4 = ((bf16[32,32,128]{2,1,0:T(8,128)(2,1)}), bf16[32,32,128]{2,1,0:T(8,128)(2,1)S(1)}, u32[]{:S(2)}, u32[]{:S(2)}) async-start(bf16[32,32,128]{2,1,0:T(8,128)(2,1)} %pad_maximum_fusion.3), calls=%async_computation.4 | async-start | bytes 524288 | tf_op jit(solution)/shard_map/all_to_all | solution.py:284
  335.1 87.7 %all-to-all-start.2 = ((bf16[32,160,224]{2,1,0:T(8,128)(2,1)}), bf16[32,160,224]{2,1,0:T(8,128)(2,1)S(1)}, u32[]{:S(2)}, u32[]{:S(2)}) async-start(bf16[32,160,224]{2,1,0:T(8,128)(2,1)} %pad_maximum_fusion), calls=%async_computation.2 | async-start | bytes 5242880 | tf_op jit(solution)/shard_map/all_to_all | solution.py:220
  341.4 112.0 %all-gather.5.cloned.1.call-start = ((), (), s32[]{:S(2)}) async-start(), calls=%async_computation.6 | async-start | bytes 2297856 | tf_op jit(solution)/shard_map/all_gather | solution.py:308
  341.5 81.8 %copy-start.10 = (bf16[224,144]{0,1:T(8,128)(2,1)S(1)}, bf16[224,144]{0,1:T(8,128)(2,1)}, u32[]{:S(2)}) copy-start(bf16[224,144]{0,1:T(8,128)(2,1)} %param.6) | copy-start | bytes 193540
  341.5 81.8 %copy-start.13 = (f32[144]{0:T(256)S(1)}, f32[144]{0:T(256)}, u32[]{:S(2)}) copy-start(f32[144]{0:T(256)} %param.7) | copy-start | bytes 1732
Sparse Core Ops, SparseCore 0:
  11.6 86.8 all-gather.2
  344.9 108.4 all-gather.4

commit v9 on v7

--- a/solution.py
+++ b/solution.py
@@ -81,7 +81,12 @@
     dump_slot = groups * CAP
     slot_dest = jnp.where(is_live, target_user * CAP + slot_rank, dump_slot)
     block_place = (slot_codes - target_user * pos_count).astype(jnp.float32)
-    outgoing = jnp.zeros((dump_slot + 1, BLK, BLK), jnp.bfloat16).at[slot_dest].set(blocks[0])
+    dest_match = slot_dest[:, None] == jnp.arange(dump_slot, dtype=jnp.int32)[None, :]
+    dest_source = jnp.sum(
+        jnp.where(dest_match, jnp.arange(slot_dest.shape[0], dtype=jnp.int32)[:, None], 0), axis=0
+    )
+    dest_used = jnp.any(dest_match, axis=0)
+    outgoing = jnp.where(dest_used[:, None, None], blocks[0][dest_source], jnp.zeros((), jnp.bfloat16))
     outgoing_pos = (
         jnp.full((dump_slot + 1,), -1.0, jnp.float32)
         .at[slot_dest]
@@ -90,7 +95,7 @@
     )
     arrived, arrived_pos = (
         lax.all_to_all(
-            outgoing[:dump_slot].reshape(groups, CAP, BLK, BLK),
+            outgoing.reshape(groups, CAP, BLK, BLK),
             "wt",
             split_axis=0,
             concat_axis=0,
@@ -130,10 +135,15 @@
     scaled = tokens_in.astype(jnp.float32) * inv_rms[:, None]
     arrival = arrived_pos.reshape(-1).astype(jnp.int32)
     arrival = jnp.where(arrival < 0, pos_count, arrival)
-    weight_table = (
-        jnp.zeros((pos_count + 1, BLK, BLK), jnp.bfloat16)
-        .at[arrival]
-        .set(arrived.reshape(-1, BLK, BLK))
+    place_match = arrival[:, None] == jnp.arange(pos_count, dtype=jnp.int32)[None, :]
+    place_source = jnp.sum(
+        jnp.where(place_match, jnp.arange(arrival.shape[0], dtype=jnp.int32)[:, None], 0), axis=0
+    )
+    place_used = jnp.any(place_match, axis=0)
+    weight_table = jnp.where(
+        place_used[:, None, None],
+        arrived.reshape(-1, BLK, BLK)[place_source],
+        jnp.zeros((), jnp.bfloat16),
     )
     w_query = weight_table[:row_blocks].reshape(D, HD)
     w_pair = weight_table[row_blocks:pos_count].reshape(D, HD)
@@ -194,20 +204,9 @@
     row_top = lax.reduce_precision(row_part, exponent_bits=8, mantissa_bits=7)
     row_hi = row_top.astype(jnp.bfloat16)
     row_lo = (row_part - row_top).astype(jnp.bfloat16)
-    pad_rows = 16
-    extra_rows = jnp.concatenate(
-        [row_hi[None], row_lo[None], jnp.zeros((pad_rows - 2, tok_rows), jnp.bfloat16)], axis=0
-    )
-    packed = jnp.concatenate(
-        [
-            contribution.astype(jnp.bfloat16).reshape(groups, feat, tok_rows),
-            jnp.broadcast_to(extra_rows[None], (groups, pad_rows, tok_rows)),
-        ],
-        axis=1,
-    ).reshape(groups * (feat + pad_rows), tok_rows)
     scattered = jnp.sum(
         lax.all_to_all(
-            packed.reshape(groups, feat + pad_rows, tok_rows),
+            contribution.astype(jnp.bfloat16).reshape(groups, feat, tok_rows),
             "wt",
             split_axis=0,
             concat_axis=0,
@@ -215,12 +214,7 @@
         ).astype(jnp.float32),
         axis=0,
     )
-    normed_grad = scattered[:feat].astype(jnp.float32).T
-    row_dots = scattered[feat].astype(jnp.float32) + scattered[feat + 1].astype(jnp.float32)
-    scaled_grad = normed_grad * norm_gain[None, :]
-    tokens_grad = (inv_rms[:, None] * (scaled_grad - scaled * (row_dots / D)[:, None])).astype(
-        jnp.bfloat16
-    )
+    normed_grad = scattered.T
     grad_query = contract_rows(normed, query_grad)
     grad_pair = contract_rows(normed, pair_grad)
     grad_table = jnp.concatenate(
@@ -267,8 +261,16 @@
     chunk_dest = jnp.transpose(chunk_pair.reshape(2, per_chunk, feat), (1, 0, 2)).reshape(
         per_chunk, 2 * feat
     )
-    gain_slots = lax.dynamic_update_slice(
-        jnp.zeros((groups, side * BLK), jnp.bfloat16), chunk_dest, (slab_index * per_chunk, 0)
+    row_cols = jnp.concatenate([row_hi, row_lo])
+    gain_slots = jnp.concatenate(
+        [
+            lax.dynamic_update_slice(
+                jnp.zeros((groups, 2 * feat), jnp.bfloat16), chunk_dest, (slab_index * per_chunk, 0)
+            ),
+            jnp.broadcast_to(row_cols[None], (groups, 2 * tok_rows)),
+            jnp.zeros((groups, side * BLK - 2 * feat - 2 * tok_rows), jnp.bfloat16),
+        ],
+        axis=1,
     ).reshape(groups, side, BLK)
     wt_recv = lax.all_to_all(
         jnp.concatenate([block_chunk, gain_slots], axis=1),
@@ -281,8 +283,14 @@
     owned_band = jnp.concatenate([returned, jnp.zeros((1, band, BLK), jnp.float32)], axis=0)[
         slot_dest
     ]
-    gain_recv = wt_recv[:, band_rows:].reshape(groups, side * BLK)[:, : 2 * feat]
-    gain_recv = gain_recv.astype(jnp.float32)
+    slot_recv = wt_recv[:, band_rows:].reshape(groups, side * BLK)
+    gain_recv = slot_recv[:, : 2 * feat].astype(jnp.float32)
+    row_recv = slot_recv[:, 2 * feat : 2 * feat + 2 * tok_rows].astype(jnp.float32)
+    row_dots = jnp.sum(row_recv[:, :tok_rows] + row_recv[:, tok_rows:], axis=0)
+    scaled_grad = normed_grad * norm_gain[None, :]
+    tokens_grad = (inv_rms[:, None] * (scaled_grad - scaled * (row_dots / D)[:, None])).astype(
+        jnp.bfloat16
+    )
     gain_mine = jnp.sum(gain_recv[:, :feat] + gain_recv[:, feat:], axis=0)
     mine_top = lax.reduce_precision(gain_mine, exponent_bits=8, mantissa_bits=7)
     mine_pair = jnp.stack([mine_top, gain_mine - mine_top]).astype(jnp.bfloat16).reshape(-1)

time: 431 us -> 426 us (0.988)
  other arithmetic: 21.1 us -> 30.3 us
  local copies, waits for them, and re-layouts: 40.1 us -> 31 us
    scatter x2 -> x0, local copies, waits for them, and re-layouts: 13.3 us -> none  [the longest x1 6.65 us: body(): jnp.zeros((dump_slot + 1, BLK, BLK), jnp.bfloat16).at[slot_dest]]
    all_to_all x2, waiting for transfers between devices: 130 us -> 123 us  [the longest x1 72.5 us: body(): lax.all_to_all(contribution.astype(jnp.bfloat16).reshape(groups, feat, to...]
    gather x0 -> x2, local copies, waits for them, and re-layouts: none -> 6.16 us  [the longest x1 4.02 us: body(): arrived.reshape(-1, BLK, BLK)[place_source]]
    select_n x1 -> x7, other arithmetic: 0.01 us -> 5.69 us  [the longest x1 3.12 us: body(): jnp.where(dest_used[:, None, None], blocks[0][dest_source], jnp.zeros((),...]
  transfers between devices with their start and end apart: 25 -> 25, of which waited for: 14 -> 16; matrix products, arithmetic and copies ran while one was open for 8% -> 7% of each run, Pallas kernels for 0% -> 0%
where the time goes in v9:
time: 426 us; the launch traced here: 425 us
  waiting for transfers between devices  253 us (59%)
  starting transfers between devices  82.4 us (19%)
  local copies, waits for them, and re-layouts  31 us (7%)
  other arithmetic  30.3 us (7%)
  between operations  14.9 us (3%)
  matrix products  12.6 us (3%)
    all_to_all x1, waiting for transfers between devices, body(): lax.all_to_all(contribution.astype(jnp.bfloat16).reshape(groups, feat, to...  72.5 us
    all_to_all x1, waiting for transfers between devices, body(): lax.all_to_all(jnp.concatenate([block_send.astype(jnp.bfloat16), gain_sen...  52.4 us
    all_to_all x1, waiting for transfers between devices, body(): lax.all_to_all(outgoing.reshape(groups, CAP, BLK, BLK), 'wt', split_axis=...  50.7 us
    ppermute x16, starting transfers between devices, shifted(): lax.ppermute(value, axis, [(source, source + steps) for source in range(i...  35.6 us
    all_gather x1, waiting for transfers between devices, body(): lax.all_gather(gather_send, 'seq', axis=0, tiled=True)  30 us
    ppermute x16, waiting for transfers between devices, shifted(): lax.ppermute(value, axis, [(source, source + steps) for source in range(i...  19.3 us
    all_gather x1, waiting for transfers between devices, body(): lax.all_gather(jnp.concatenate([tokens_in, gain_rows, jnp.zeros((side_row...  18.6 us
    all_to_all x1, starting transfers between devices, body(): lax.all_to_all(outgoing_pos[:dump_slot].reshape(groups, CAP), 'wt', split...  10.2 us
  transfers between devices with their start and end apart: 25, of which 16 were waited for; matrix products, arithmetic and copies ran while one was open for 7% of the time, Pallas kernels for 0%

profile of v9, /device:TPU:6, one launch (start us, length us, event | category | flops | bytes accessed | tf_op | source)
XLA Modules:
  0.0 424.5 jit_solution(9458968723817488811)
XLA Ops:
  7.2 0.8 fusion.79
  9.7 0.8 scatter_custom_fusion
  11.2 10.2 %all-to-all-start = ((bf16[32,1,2]{2,1,0:T(2,128)(2,1)}), bf16[32,1,2]{2,1,0:T(2,128)(2,1)S(1)}, u32[]{:S(2)}, u32[]{:S(2)}) async-start(bf16[32,1,2]{2,1,0:T(2,128)(2,1)} %all_to_all.24), calls=%async_computation | async-start | bytes 32768 | tf_op jit(solution)/shard_map/all_to_all | solution.py:104
  22.5 2.1 gather_fusion
  24.6 3.1 broadcast_select_fusion.1
  27.7 1.6 all-to-all-done
  29.3 8.4 %all-to-all-start.1 = ((bf16[32,2,128,128]{3,2,1,0:T(8,128)(2,1)}), bf16[32,2,128,128]{3,2,1,0:T(8,128)(2,1)}, u32[]{:S(2)}, u32[]{:S(2)}) async-start(bf16[32,2,128,128]{3,2,1,0:T(8,128)(2,1)} %broadcast_select_fusion.1), calls=%async_computation.1 | async-start | bytes 4194304 | tf_op jit(solution)/shard_map/all_to_all | solution.py:97
  39.7 50.7 %all-to-all-done.1 = bf16[32,2,128,128]{3,2,1,0:T(8,128)(2,1)} async-done(((bf16[32,2,128,128]{3,2,1,0:T(8,128)(2,1)}), bf16[32,2,128,128]{3,2,1,0:T(8,128)(2,1)}, u32[]{:S(2)}, u32[]{:S(2)}) %all-to-all-start.1) | async-done | bytes 2097184 | tf_op jit(solution)/shard_map/all_to_all | solution.py:97
  90.4 4.0 gather_fusion.1
  94.4 1.9 broadcast_select_fusion
  96.3 1.2 fusion.95
  97.6 18.6 %all-gather.3.cloned.1.call-done = bf16[232,4608]{0,1:T(8,128)(2,1)} async-done(((bf16[232,144]{0,1:T(8,128)(2,1)}), bf16[232,4608]{0,1:T(8,128)(2,1)}) %all-gather.3.cloned.1.call-update) | async-done | bytes 2138128 | tf_op jit(solution)/shard_map/all_gather | solution.py:118
  116.2 4.1 copy.55
  120.3 2.1 fusion.8
  122.4 1.6 slice_convert_fusion
  124.1 2.2 fusion.14
  126.3 0.8 fusion.87
  127.7 3.8 collective-permute-start
  131.5 3.6 collective-permute-start.1
  135.0 4.2 collective-permute-start.2
  139.3 4.9 %collective-permute-start.3 = (bf16[224,128]{1,0:T(8,128)(2,1)S(1)}, bf16[224,128]{1,0:T(8,128)(2,1)S(1)}, u32[]{:S(2)}, u32[]{:S(2)}) collective-permute-start(bf16[224,128]{1,0:T(8,128)(2,1)S(1)} %get-tuple-element.9), channel_id=1, source_target_pairs={{0,128},{32,160},{64,192},{96,224},{128,256},{160,288},{192,320},{... | collective-permute-start | bytes 172040 | tf_op jit(solution)/shard_map/ppermute | solution.py:30
  144.2 4.1 collective-permute-start.4
  148.4 1.3 collective-permute-start.5
  149.7 1.8 collective-permute-start.6
  151.6 1.3 collective-permute-start.7
  153.4 1.5 collective-permute-done.7
  154.9 2.1 collective-permute-start.8
  157.0 0.8 fusion.89
  158.7 1.1 fusion.91
  159.8 1.4 multiply_reduce_fusion
  161.2 1.2 fusion.13
  162.9 1.0 select_convert_fusion
  164.0 2.2 collective-permute-start.9
  168.0 1.3 collective-permute-start.10
  169.3 1.3 collective-permute-start.11
  170.6 1.3 collective-permute-start.12
  172.6 1.3 collective-permute-start.13
  173.9 1.3 collective-permute-start.14
  175.2 1.3 collective-permute-start.15
  176.8 1.3 collective-permute-start.16
  178.1 1.9 collective-permute-done.12
  180.0 1.5 collective-permute-start.17
  181.5 0.9 fusion.85
  182.5 2.8 collective-permute-done.13
  185.2 3.4 collective-permute-done.14
  188.6 9.0 %collective-permute-done.15 = bf16[224,128]{1,0:T(8,128)(2,1)S(1)} collective-permute-done((bf16[224,128]{1,0:T(8,128)(2,1)S(1)}, bf16[224,128]{1,0:T(8,128)(2,1)S(1)}, u32[]{:S(2)}, u32[]{:S(2)}) %collective-permute-start.15) | collective-permute-done | bytes 57376 | tf_op jit(solution)/shard_map/ppermute | solution.py:30
  198.3 0.9 fusion.83
  199.3 2.8 fusion.5
  202.0 1.7 maximum_maximum_fusion
  203.8 3.8 gather_fusion.2
  207.6 3.5 copy.52
  211.3 3.1 pad_maximum_fusion
  214.4 9.5 %all-to-all-start.3 = ((bf16[16,528,128]{2,1,0:T(8,128)(2,1)}), bf16[16,528,128]{2,1,0:T(8,128)(2,1)}, u32[]{:S(2)}, u32[]{:S(2)}) async-start(bf16[16,528,128]{2,1,0:T(8,128)(2,1)} %pad_maximum_fusion), calls=%async_computation.3 | async-start | bytes 4325376 | tf_op jit(solution)/shard_map/all_to_all | solution.py:248
  224.0 52.4 %all-to-all-done.3 = bf16[16,528,128]{2,1,0:T(8,128)(2,1)} async-done(((bf16[16,528,128]{2,1,0:T(8,128)(2,1)}), bf16[16,528,128]{2,1,0:T(8,128)(2,1)}, u32[]{:S(2)}, u32[]{:S(2)}) %all-to-all-start.3) | async-done | bytes 2162720 | tf_op jit(solution)/shard_map/all_to_all | solution.py:248
  276.4 1.9 convert_reduce_fusion.1
  279.6 7.3 %all-to-all-start.4 = ((bf16[32,32,128]{2,1,0:T(8,128)(2,1)}), bf16[32,32,128]{2,1,0:T(8,128)(2,1)S(1)}, u32[]{:S(2)}, u32[]{:S(2)}) async-start(bf16[32,32,128]{2,1,0:T(8,128)(2,1)} %pad_maximum_fusion.1), calls=%async_computation.4 | async-start | bytes 524288 | tf_op jit(solution)/shard_map/all_to_all | solution.py:275
  286.9 4.1 copy.51
  291.0 7.3 %all-to-all-done.4 = bf16[32,32,128]{2,1,0:T(8,128)(2,1)S(1)} async-done(((bf16[32,32,128]{2,1,0:T(8,128)(2,1)}), bf16[32,32,128]{2,1,0:T(8,128)(2,1)S(1)}, u32[]{:S(2)}, u32[]{:S(2)}) %all-to-all-start.4) | async-done | bytes 262176 | tf_op jit(solution)/shard_map/all_to_all | solution.py:275
  298.4 7.0 %all-to-all-start.2 = ((bf16[32,144,224]{2,1,0:T(8,128)(2,1)}), bf16[32,144,224]{2,1,0:T(8,128)(2,1)}, u32[]{:S(2)}, u32[]{:S(2)}) async-start(bf16[32,144,224]{2,1,0:T(8,128)(2,1)} %bitcast.152), calls=%async_computation.2 | async-start | bytes 4718592 | tf_op jit(solution)/shard_map/all_to_all | solution.py:208
  307.0 72.5 %all-to-all-done.2 = bf16[32,144,224]{2,1,0:T(8,128)(2,1)} async-done(((bf16[32,144,224]{2,1,0:T(8,128)(2,1)}), bf16[32,144,224]{2,1,0:T(8,128)(2,1)}, u32[]{:S(2)}, u32[]{:S(2)}) %all-to-all-start.2) | async-done | bytes 2064416 | tf_op jit(solution)/shard_map/all_to_all | solution.py:208
  379.6 2.1 convert_reduce_fusion
  382.6 30.0 %all-gather.5.cloned.1.call-done = bf16[8448,128]{1,0:T(8,128)(2,1)} async-done(((bf16[528,128]{1,0:T(8,128)(2,1)}), bf16[8448,128]{1,0:T(8,128)(2,1)}) %all-gather.5.cloned.1.call-update) | async-done | bytes 2162704 | tf_op jit(solution)/shard_map/all_gather | solution.py:305
  412.6 3.5 copy_bitcast_fusion
  416.1 0.9 slice_convert_fusion.2
  (133 shorter events, 16.0 us)
Async XLA Ops:
  7.2 15.3 %copy-start = (bf16[1,64,128,128]{3,2,1,0:T(8,128)(2,1)S(1)}, bf16[1,64,128,128]{3,2,1,0:T(8,128)(2,1)}, u32[]{:S(2)}) copy-start(bf16[1,64,128,128]{3,2,1,0:T(8,128)(2,1)} %param.9) | copy-start | bytes 6291460
  11.2 18.1 %all-to-all-start = ((bf16[32,1,2]{2,1,0:T(2,128)(2,1)}), bf16[32,1,2]{2,1,0:T(2,128)(2,1)S(1)}, u32[]{:S(2)}, u32[]{:S(2)}) async-start(bf16[32,1,2]{2,1,0:T(2,128)(2,1)} %all_to_all.24), calls=%async_computation | async-start | bytes 32768 | tf_op jit(solution)/shard_map/all_to_all | solution.py:104
  27.7 10.1 %copy-start.4 = (f32[144]{0:T(256)S(1)}, f32[144]{0:T(256)}, u32[]{:S(2)}) copy-start(f32[144]{0:T(256)} %param.7) | copy-start | bytes 1732
  27.7 10.4 %copy-start.3 = (bf16[224,144]{0,1:T(8,128)(2,1)S(1)}, bf16[224,144]{0,1:T(8,128)(2,1)}, u32[]{:S(2)}) copy-start(bf16[224,144]{0,1:T(8,128)(2,1)} %param.6) | copy-start | bytes 193540
  27.7 11.4 %copy-start.5 = (s32[224]{0:T(256)S(1)}, s32[224]{0:T(256)}, u32[]{:S(2)}) copy-start(s32[224]{0:T(256)} %param.8) | copy-start | bytes 2692
  29.3 61.1 %all-to-all-start.1 = ((bf16[32,2,128,128]{3,2,1,0:T(8,128)(2,1)}), bf16[32,2,128,128]{3,2,1,0:T(8,128)(2,1)}, u32[]{:S(2)}, u32[]{:S(2)}) async-start(bf16[32,2,128,128]{3,2,1,0:T(8,128)(2,1)} %broadcast_select_fusion.1), calls=%async_computation.1 | async-start | bytes 4194304 | tf_op jit(solution)/shard_map/all_to_all | solution.py:97
  37.7 78.4 %all-gather.3.cloned.1.call-start = ((), (), s32[]{:S(2)}) async-start(), calls=%async_computation.5 | async-start | bytes 2433024 | tf_op jit(solution)/shard_map/all_gather | solution.py:118
  124.0 2.2 copy-start.1
  124.1 2.2 copy-start.2
  127.7 20.7 %collective-permute-start = (bf16[224,128]{1,0:T(8,128)(2,1)S(1)}, bf16[224,128]{1,0:T(8,128)(2,1)S(1)}, u32[]{:S(2)}, u32[]{:S(2)}) collective-permute-start(bf16[224,128]{1,0:T(8,128)(2,1)S(1)} %get-tuple-element.9), channel_id=1, source_target_pairs={{0,32},{32,64},{64,96},{96,128},{128,160},{160,192},{192,224},{224... | collective-permute-start | bytes 172040 | tf_op jit(solution)/shard_map/ppermute | solution.py:30
  131.5 18.2 %collective-permute-start.1 = (bf16[224,128]{1,0:T(8,128)(2,1)S(1)}, bf16[224,128]{1,0:T(8,128)(2,1)S(1)}, u32[]{:S(2)}, u32[]{:S(2)}) collective-permute-start(bf16[224,128]{1,0:T(8,128)(2,1)S(1)} %get-tuple-element.9), channel_id=1, source_target_pairs={{0,64},{32,96},{64,128},{96,160},{128,192},{160,224},{192,256},{22... | collective-permute-start | bytes 172040 | tf_op jit(solution)/shard_map/ppermute | solution.py:30
  135.0 16.5 %collective-permute-start.2 = (bf16[224,128]{1,0:T(8,128)(2,1)S(1)}, bf16[224,128]{1,0:T(8,128)(2,1)S(1)}, u32[]{:S(2)}, u32[]{:S(2)}) collective-permute-start(bf16[224,128]{1,0:T(8,128)(2,1)S(1)} %get-tuple-element.9), channel_id=1, source_target_pairs={{0,96},{32,128},{64,160},{96,192},{128,224},{160,256},{192,288},{2... | collective-permute-start | bytes 172040 | tf_op jit(solution)/shard_map/ppermute | solution.py:30
  139.3 13.6 %collective-permute-start.3 = (bf16[224,128]{1,0:T(8,128)(2,1)S(1)}, bf16[224,128]{1,0:T(8,128)(2,1)S(1)}, u32[]{:S(2)}, u32[]{:S(2)}) collective-permute-start(bf16[224,128]{1,0:T(8,128)(2,1)S(1)} %get-tuple-element.9), channel_id=1, source_target_pairs={{0,128},{32,160},{64,192},{96,224},{128,256},{160,288},{192,320},{... | collective-permute-start | bytes 172040 | tf_op jit(solution)/shard_map/ppermute | solution.py:30
  144.2 8.7 %collective-permute-start.4 = (bf16[224,128]{1,0:T(8,128)(2,1)S(1)}, bf16[224,128]{1,0:T(8,128)(2,1)S(1)}, u32[]{:S(2)}, u32[]{:S(2)}) collective-permute-start(bf16[224,128]{1,0:T(8,128)(2,1)S(1)} %get-tuple-element.9), channel_id=1, source_target_pairs={{0,160},{32,192},{64,224},{96,256},{128,288},{160,320},{192,352},{... | collective-permute-start | bytes 172040 | tf_op jit(solution)/shard_map/ppermute | solution.py:30
  148.4 4.6 %collective-permute-start.5 = (bf16[224,128]{1,0:T(8,128)(2,1)S(1)}, bf16[224,128]{1,0:T(8,128)(2,1)S(1)}, u32[]{:S(2)}, u32[]{:S(2)}) collective-permute-start(bf16[224,128]{1,0:T(8,128)(2,1)S(1)} %get-tuple-element.9), channel_id=1, source_target_pairs={{0,192},{32,224},{64,256},{96,288},{128,320},{160,352},{192,384},{... | collective-permute-start | bytes 172040 | tf_op jit(solution)/shard_map/ppermute | solution.py:30
  149.7 3.6 collective-permute-start.6
  151.6 3.3 collective-permute-start.7
  154.9 3.8 collective-permute-start.8
  158.7 1.1 copy-start.6
  164.0 3.8 collective-permute-start.9
  168.0 7.2 %collective-permute-start.10 = (bf16[224,128]{1,0:T(8,128)(2,1)S(1)}, bf16[224,128]{1,0:T(8,128)(2,1)S(1)}, u32[]{:S(2)}, u32[]{:S(2)}) collective-permute-start(bf16[224,128]{1,0:T(8,128)(2,1)S(1)} %get-tuple-element.15), channel_id=1, source_target_pairs={{32,0},{64,32},{96,64},{128,96},{160,128},{192,160},{224,192},{256... | collective-permute-start | bytes 172040 | tf_op jit(solution)/shard_map/ppermute | solution.py:30
  169.3 7.5 %collective-permute-start.11 = (bf16[224,128]{1,0:T(8,128)(2,1)S(1)}, bf16[224,128]{1,0:T(8,128)(2,1)S(1)}, u32[]{:S(2)}, u32[]{:S(2)}) collective-permute-start(bf16[224,128]{1,0:T(8,128)(2,1)S(1)} %get-tuple-element.22), channel_id=1, source_target_pairs={{64,0},{96,32},{128,64},{160,96},{192,128},{224,160},{256,192},{28... | collective-permute-start | bytes 172040 | tf_op jit(solution)/shard_map/ppermute | solution.py:30
  170.6 9.4 %collective-permute-start.12 = (bf16[224,128]{1,0:T(8,128)(2,1)S(1)}, bf16[224,128]{1,0:T(8,128)(2,1)S(1)}, u32[]{:S(2)}, u32[]{:S(2)}) collective-permute-start(bf16[224,128]{1,0:T(8,128)(2,1)S(1)} %get-tuple-element.21), channel_id=1, source_target_pairs={{96,0},{128,32},{160,64},{192,96},{224,128},{256,160},{288,192},{3... | collective-permute-start | bytes 172040 | tf_op jit(solution)/shard_map/ppermute | solution.py:30
  172.6 12.6 %collective-permute-start.13 = (bf16[224,128]{1,0:T(8,128)(2,1)S(1)}, bf16[224,128]{1,0:T(8,128)(2,1)S(1)}, u32[]{:S(2)}, u32[]{:S(2)}) collective-permute-start(bf16[224,128]{1,0:T(8,128)(2,1)S(1)} %get-tuple-element.20), channel_id=1, source_target_pairs={{128,0},{160,32},{192,64},{224,96},{256,128},{288,160},{320,192},{... | collective-permute-start | bytes 172040 | tf_op jit(solution)/shard_map/ppermute | solution.py:30
  173.9 14.7 %collective-permute-start.14 = (bf16[224,128]{1,0:T(8,128)(2,1)S(1)}, bf16[224,128]{1,0:T(8,128)(2,1)S(1)}, u32[]{:S(2)}, u32[]{:S(2)}) collective-permute-start(bf16[224,128]{1,0:T(8,128)(2,1)S(1)} %get-tuple-element.19), channel_id=1, source_target_pairs={{160,0},{192,32},{224,64},{256,96},{288,128},{320,160},{352,192},{... | collective-permute-start | bytes 172040 | tf_op jit(solution)/shard_map/ppermute | solution.py:30
  175.2 22.4 %collective-permute-start.15 = (bf16[224,128]{1,0:T(8,128)(2,1)S(1)}, bf16[224,128]{1,0:T(8,128)(2,1)S(1)}, u32[]{:S(2)}, u32[]{:S(2)}) collective-permute-start(bf16[224,128]{1,0:T(8,128)(2,1)S(1)} %get-tuple-element.18), channel_id=1, source_target_pairs={{192,0},{224,32},{256,64},{288,96},{320,128},{352,160},{384,192},{... | collective-permute-start | bytes 172040 | tf_op jit(solution)/shard_map/ppermute | solution.py:30
  176.8 20.8 %collective-permute-start.16 = (bf16[224,128]{1,0:T(8,128)(2,1)S(1)}, bf16[224,128]{1,0:T(8,128)(2,1)S(1)}, u32[]{:S(2)}, u32[]{:S(2)}) collective-permute-start(bf16[224,128]{1,0:T(8,128)(2,1)S(1)} %get-tuple-element.17), channel_id=1, source_target_pairs={{224,0},{256,32},{288,64},{320,96},{352,128},{384,160},{416,192},{... | collective-permute-start | bytes 172040 | tf_op jit(solution)/shard_map/ppermute | solution.py:30
  180.0 17.6 %collective-permute-start.17 = (bf16[224,128]{1,0:T(8,128)(2,1)S(1)}, bf16[224,128]{1,0:T(8,128)(2,1)S(1)}, u32[]{:S(2)}, u32[]{:S(2)}) collective-permute-start(bf16[224,128]{1,0:T(8,128)(2,1)S(1)} %get-tuple-element.16), channel_id=1, source_target_pairs={{256,0},{288,32},{320,64},{352,96},{384,128},{416,160},{448,192},{... | collective-permute-start | bytes 172040 | tf_op jit(solution)/shard_map/ppermute | solution.py:30
  214.4 62.0 %all-to-all-start.3 = ((bf16[16,528,128]{2,1,0:T(8,128)(2,1)}), bf16[16,528,128]{2,1,0:T(8,128)(2,1)}, u32[]{:S(2)}, u32[]{:S(2)}) async-start(bf16[16,528,128]{2,1,0:T(8,128)(2,1)} %pad_maximum_fusion), calls=%async_computation.3 | async-start | bytes 4325376 | tf_op jit(solution)/shard_map/all_to_all | solution.py:248
  279.6 18.8 %all-to-all-start.4 = ((bf16[32,32,128]{2,1,0:T(8,128)(2,1)}), bf16[32,32,128]{2,1,0:T(8,128)(2,1)S(1)}, u32[]{:S(2)}, u32[]{:S(2)}) async-start(bf16[32,32,128]{2,1,0:T(8,128)(2,1)} %pad_maximum_fusion.1), calls=%async_computation.4 | async-start | bytes 524288 | tf_op jit(solution)/shard_map/all_to_all | solution.py:275
  298.4 81.2 %all-to-all-start.2 = ((bf16[32,144,224]{2,1,0:T(8,128)(2,1)}), bf16[32,144,224]{2,1,0:T(8,128)(2,1)}, u32[]{:S(2)}, u32[]{:S(2)}) async-start(bf16[32,144,224]{2,1,0:T(8,128)(2,1)} %bitcast.152), calls=%async_computation.2 | async-start | bytes 4718592 | tf_op jit(solution)/shard_map/all_to_all | solution.py:208
  305.3 107.3 %all-gather.5.cloned.1.call-start = ((), (), s32[]{:S(2)}) async-start(), calls=%async_computation.6 | async-start | bytes 2297856 | tf_op jit(solution)/shard_map/all_gather | solution.py:305
Sparse Core Ops, SparseCore 0:
  42.2 73.8 all-gather.2
  308.8 103.7 all-gather.4

commit v10 on v9

--- a/solution.py
+++ b/solution.py
@@ -11,6 +11,7 @@
 
 query_scale = 144.0 ** (-0.5)
 soft_cap = 50.0
+WT = ("chip", "core")
 norm_eps = 1e-06
 
 
@@ -65,9 +66,9 @@
 def body(tokens_in, norm_gain, positions, blocks, slot_code, out_grad):
     tok_rows = tokens_in.shape[0]
     feat = tokens_in.shape[1]
-    groups = lax.axis_size("wt")
+    groups = lax.axis_size(WT)
     slab_index = lax.axis_index("seq")
-    is_even = lax.axis_index("wt") % 2 == 0
+    is_even = lax.axis_index(WT) % 2 == 0
     pos_count = 2 * (D // BLK)
     row_blocks = pos_count // 2
     slot_codes = slot_code[0]
@@ -96,14 +97,14 @@
     arrived, arrived_pos = (
         lax.all_to_all(
             outgoing.reshape(groups, CAP, BLK, BLK),
-            "wt",
+            WT,
             split_axis=0,
             concat_axis=0,
             tiled=True,
         ),
         lax.all_to_all(
             outgoing_pos[:dump_slot].reshape(groups, CAP),
-            "wt",
+            WT,
             split_axis=0,
             concat_axis=0,
             tiled=True,
@@ -119,7 +120,7 @@
         jnp.concatenate(
             [tokens_in, gain_rows, jnp.zeros((side_rows - 3, feat), jnp.bfloat16)], axis=0
         ),
-        "wt",
+        WT,
         axis=1,
         tiled=True,
     )
@@ -160,7 +161,7 @@
     for offset in range(1, reach_slabs + 1):
         own_list.append(shifted(own_pair, "seq", offset))
     own_all = jnp.concatenate(own_list, axis=0)
-    partner_all = from_partner(own_all, "wt", 0)
+    partner_all = from_partner(own_all, "core", 0)
     key_all = jnp.where(is_even, own_all, partner_all)
     value_all = jnp.where(is_even, partner_all, own_all)
     local_index = jnp.arange(tok_rows, dtype=jnp.int32)
@@ -190,7 +191,7 @@
     key_grads = contract_rows(score_low, query_rot)
     value_grads = contract_rows(probs_low, out_grad)
     outbound = jnp.where(is_even, value_grads, key_grads).astype(jnp.bfloat16)
-    partner_grads = from_partner(outbound, "wt", 0).astype(jnp.float32)
+    partner_grads = from_partner(outbound, "core", 0).astype(jnp.float32)
     own_grads = jnp.where(is_even, key_grads, value_grads) + partner_grads
     pair_total = own_grads[:tok_rows]
     for offset in range(1, reach_slabs + 1):
@@ -204,10 +205,16 @@
     row_top = lax.reduce_precision(row_part, exponent_bits=8, mantissa_bits=7)
     row_hi = row_top.astype(jnp.bfloat16)
     row_lo = (row_part - row_top).astype(jnp.bfloat16)
+    chips = lax.axis_size("chip")
+    core_index = lax.axis_index("core")
+    by_core = contribution.reshape(chips, 2, feat, tok_rows)
+    keep = lax.dynamic_index_in_dim(by_core, core_index, axis=1, keepdims=False)
+    give = lax.dynamic_index_in_dim(by_core, 1 - core_index, axis=1, keepdims=False)
+    from_other = from_partner(give.astype(jnp.bfloat16), "core", 0).astype(jnp.float32)
     scattered = jnp.sum(
         lax.all_to_all(
-            contribution.astype(jnp.bfloat16).reshape(groups, feat, tok_rows),
-            "wt",
+            (keep + from_other).astype(jnp.bfloat16),
+            "chip",
             split_axis=0,
             concat_axis=0,
             tiled=True,
@@ -274,7 +281,7 @@
     ).reshape(groups, side, BLK)
     wt_recv = lax.all_to_all(
         jnp.concatenate([block_chunk, gain_slots], axis=1),
-        "wt",
+        WT,
         split_axis=0,
         concat_axis=0,
         tiled=True,
@@ -321,18 +328,22 @@
 
 
 def solution(mesh):
+    seq_count, wt_count = mesh.devices.shape
+    split_mesh = jax.sharding.Mesh(
+        mesh.devices.reshape(seq_count, wt_count // 2, 2), ("seq", "chip", "core")
+    )
     placed = (
-        P("seq", "wt"),
-        P("wt"),
+        P("seq", WT),
+        P(WT),
         P("seq"),
-        P("wt", None, None, None),
-        P("wt", None),
-        P("seq", "wt"),
+        P(WT, None, None, None),
+        P(WT, None),
+        P("seq", WT),
     )
     return jax.shard_map(
         body,
-        mesh=mesh,
+        mesh=split_mesh,
         in_specs=placed,
-        out_specs=(P("seq", "wt"), P("seq", "wt"), P("wt"), P("wt", None, None, None)),
+        out_specs=(P("seq", WT), P("seq", WT), P(WT), P(WT, None, None, None)),
         check_vma=False,
     )

time: 426 us -> 401 us (0.941)
  waiting for transfers between devices: 253 us -> 185 us
  blocking collectives: 0 us -> 52.7 us
  starting transfers between devices: 82.4 us -> 76.5 us
    all_to_all x4 -> x3, waiting for transfers between devices: 132 us -> 54.8 us  [the longest x1 50.7 us: body(): lax.all_to_all(outgoing.reshape(groups, CAP, BLK, BLK), WT, split_axis=0,...]
    all_to_all x0 -> x1, blocking collectives: none -> 52.7 us  [body(): lax.all_to_all((keep + from_other).astype(jnp.bfloat16), 'chip', split_ax...]
    all_to_all x4 -> x3, starting transfers between devices: 32.9 us -> 25 us  [the longest x1 10.2 us: body(): lax.all_to_all(outgoing_pos[:dump_slot].reshape(groups, CAP), WT, split_a...]
    all_gather x1, waiting for transfers between devices: 30 us -> 37.1 us  [body(): lax.all_gather(gather_send, 'seq', axis=0, tiled=True)]
    add x0 -> x1, local copies, waits for them, and re-layouts: none -> 5.78 us  [body(): contribution = contract(w_query, query_grad) + contract(w_pair, pair_grad)]
  transfers between devices with their start and end apart: 25 -> 25, of which waited for: 16 -> 15; matrix products, arithmetic and copies ran while one was open for 7% -> 7% of each run, Pallas kernels for 0% -> 0%
where the time goes in v10:
time: 401 us; the launch traced here: 400 us
  waiting for transfers between devices  185 us (46%)
  starting transfers between devices  76.5 us (19%)
  blocking collectives  52.7 us (13%)
  local copies, waits for them, and re-layouts  30.3 us (8%)
  other arithmetic  27.2 us (7%)
  between operations  14.9 us (4%)
  matrix products  13.4 us (3%)
    all_to_all x1, blocking collectives, body(): lax.all_to_all((keep + from_other).astype(jnp.bfloat16), 'chip', split_ax...  52.7 us
    all_to_all x1, waiting for transfers between devices, body(): lax.all_to_all(jnp.concatenate([block_send.astype(jnp.bfloat16), gain_sen...  52.5 us
    all_to_all x1, waiting for transfers between devices, body(): lax.all_to_all(outgoing.reshape(groups, CAP, BLK, BLK), WT, split_axis=0,...  50.7 us
    all_gather x1, waiting for transfers between devices, body(): lax.all_gather(gather_send, 'seq', axis=0, tiled=True)  37.1 us
    ppermute x16, starting transfers between devices, shifted(): lax.ppermute(value, axis, [(source, source + steps) for source in range(i...  35.6 us
    all_gather x1, waiting for transfers between devices, body(): lax.all_gather(jnp.concatenate([tokens_in, gain_rows, jnp.zeros((side_row...  20.3 us
    ppermute x16, waiting for transfers between devices, shifted(): lax.ppermute(value, axis, [(source, source + steps) for source in range(i...  19.3 us
    all_to_all x1, starting transfers between devices, body(): lax.all_to_all(outgoing_pos[:dump_slot].reshape(groups, CAP), WT, split_a...  10.2 us
  transfers between devices with their start and end apart: 25, of which 15 were waited for; matrix products, arithmetic and copies ran while one was open for 7% of the time, Pallas kernels for 0%

profile of v10, /device:TPU:6, one launch (start us, length us, event | category | flops | bytes accessed | tf_op | source)
XLA Modules:
  0.0 399.7 jit_solution(4535110481211264242)
XLA Ops:
  7.2 0.8 fusion.81
  10.5 0.8 scatter_custom_fusion
  12.0 10.2 %all-to-all-start = ((bf16[32,1,2]{2,1,0:T(2,128)(2,1)}), bf16[32,1,2]{2,1,0:T(2,128)(2,1)S(1)}, u32[]{:S(2)}, u32[]{:S(2)}) async-start(bf16[32,1,2]{2,1,0:T(2,128)(2,1)} %all_to_all.24), calls=%async_computation | async-start | bytes 32768 | tf_op jit(solution)/shard_map/all_to_all | solution.py:105
  22.5 2.1 gather_fusion
  24.6 3.1 broadcast_select_fusion.1
  27.7 2.3 all-to-all-done
  30.1 7.6 %all-to-all-start.1 = ((bf16[32,2,128,128]{3,2,1,0:T(8,128)(2,1)}), bf16[32,2,128,128]{3,2,1,0:T(8,128)(2,1)S(1)}, u32[]{:S(2)}, u32[]{:S(2)}) async-start(bf16[32,2,128,128]{3,2,1,0:T(8,128)(2,1)} %broadcast_select_fusion.1), calls=%async_computation.1 | async-start | bytes 4194304 | tf_op jit(solution)/shard_map/all_to_all | solution.py:98
  39.6 50.7 %all-to-all-done.1 = bf16[32,2,128,128]{3,2,1,0:T(8,128)(2,1)S(1)} async-done(((bf16[32,2,128,128]{3,2,1,0:T(8,128)(2,1)}), bf16[32,2,128,128]{3,2,1,0:T(8,128)(2,1)S(1)}, u32[]{:S(2)}, u32[]{:S(2)}) %all-to-all-start.1) | async-done | bytes 2097184 | tf_op jit(solution)/shard_map/all_to_all | solution.py:98
  90.3 2.4 gather_fusion.1
  92.7 1.9 broadcast_select_fusion
  94.6 1.2 fusion.97
  95.9 20.3 %all-gather.3.cloned.1.call-done = bf16[232,4608]{0,1:T(8,128)(2,1)} async-done(((bf16[232,144]{0,1:T(8,128)(2,1)}), bf16[232,4608]{0,1:T(8,128)(2,1)}) %all-gather.3.cloned.1.call-update) | async-done | bytes 2138128 | tf_op jit(solution)/shard_map/all_gather | solution.py:119
  116.2 2.8 copy.55
  119.5 1.6 slice_convert_fusion
  121.1 2.2 fusion.14
  123.3 0.8 fusion.89
  124.8 3.8 collective-permute-start
  128.5 3.6 collective-permute-start.1
  132.1 4.2 %collective-permute-start.2 = (bf16[224,128]{1,0:T(8,128)(2,1)S(1)}, bf16[224,128]{1,0:T(8,128)(2,1)S(1)}, u32[]{:S(2)}, u32[]{:S(2)}) collective-permute-start(bf16[224,128]{1,0:T(8,128)(2,1)S(1)} %get-tuple-element.9), channel_id=1, source_target_pairs={{0,96},{32,128},{64,160},{96,192},{128,224},{160,256},{192,288},{2... | collective-permute-start | bytes 172040 | tf_op jit(solution)/shard_map/ppermute | solution.py:31
  136.4 4.9 %collective-permute-start.3 = (bf16[224,128]{1,0:T(8,128)(2,1)S(1)}, bf16[224,128]{1,0:T(8,128)(2,1)S(1)}, u32[]{:S(2)}, u32[]{:S(2)}) collective-permute-start(bf16[224,128]{1,0:T(8,128)(2,1)S(1)} %get-tuple-element.9), channel_id=1, source_target_pairs={{0,128},{32,160},{64,192},{96,224},{128,256},{160,288},{192,320},{... | collective-permute-start | bytes 172040 | tf_op jit(solution)/shard_map/ppermute | solution.py:31
  141.3 4.1 %collective-permute-start.4 = (bf16[224,128]{1,0:T(8,128)(2,1)S(1)}, bf16[224,128]{1,0:T(8,128)(2,1)S(1)}, u32[]{:S(2)}, u32[]{:S(2)}) collective-permute-start(bf16[224,128]{1,0:T(8,128)(2,1)S(1)} %get-tuple-element.9), channel_id=1, source_target_pairs={{0,160},{32,192},{64,224},{96,256},{128,288},{160,320},{192,352},{... | collective-permute-start | bytes 172040 | tf_op jit(solution)/shard_map/ppermute | solution.py:31
  145.5 1.3 collective-permute-start.5
  146.8 1.8 collective-permute-start.6
  148.6 1.3 collective-permute-start.7
  150.4 1.5 collective-permute-done.7
  152.0 2.1 collective-permute-start.8
  154.1 0.8 fusion.91
  155.8 1.1 fusion.93
  156.9 1.4 multiply_reduce_fusion
  158.3 1.2 fusion.13
  160.0 1.1 select_convert_fusion
  161.1 2.2 collective-permute-start.9
  165.1 1.3 collective-permute-start.10
  166.4 1.3 collective-permute-start.11
  167.7 1.3 collective-permute-start.12
  169.7 1.3 collective-permute-start.13
  171.0 1.3 collective-permute-start.14
  172.3 1.3 collective-permute-start.15
  173.9 1.3 collective-permute-start.16
  175.2 1.9 collective-permute-done.12
  177.1 1.5 collective-permute-start.17
  178.6 0.9 fusion.87
  179.5 2.8 collective-permute-done.13
  182.4 3.3 collective-permute-done.14
  185.6 9.1 %collective-permute-done.15 = bf16[224,128]{1,0:T(8,128)(2,1)S(1)} collective-permute-done((bf16[224,128]{1,0:T(8,128)(2,1)S(1)}, bf16[224,128]{1,0:T(8,128)(2,1)S(1)}, u32[]{:S(2)}, u32[]{:S(2)}) %collective-permute-start.15) | collective-permute-done | bytes 57376 | tf_op jit(solution)/shard_map/ppermute | solution.py:31
  195.4 0.9 fusion.85
  196.4 3.5 fusion.5
  199.9 1.7 maximum_maximum_fusion
  201.6 3.8 gather_fusion.2
  205.4 2.1 copy.52
  207.8 1.5 pad_maximum_fusion
  209.3 9.5 %all-to-all-start.3 = ((bf16[16,528,128]{2,1,0:T(8,128)(2,1)}), bf16[16,528,128]{2,1,0:T(8,128)(2,1)}, u32[]{:S(2)}, u32[]{:S(2)}) async-start(bf16[16,528,128]{2,1,0:T(8,128)(2,1)} %pad_maximum_fusion), calls=%async_computation.3 | async-start | bytes 4325376 | tf_op jit(solution)/shard_map/all_to_all | solution.py:255
  218.8 52.5 %all-to-all-done.3 = bf16[16,528,128]{2,1,0:T(8,128)(2,1)} async-done(((bf16[16,528,128]{2,1,0:T(8,128)(2,1)}), bf16[16,528,128]{2,1,0:T(8,128)(2,1)}, u32[]{:S(2)}, u32[]{:S(2)}) %all-to-all-start.3) | async-done | bytes 2162720 | tf_op jit(solution)/shard_map/all_to_all | solution.py:255
  271.3 1.9 convert_reduce_fusion
  274.5 7.2 %all-to-all-start.4 = ((bf16[32,32,128]{2,1,0:T(8,128)(2,1)}), bf16[32,32,128]{2,1,0:T(8,128)(2,1)S(1)}, u32[]{:S(2)}, u32[]{:S(2)}) async-start(bf16[32,32,128]{2,1,0:T(8,128)(2,1)} %pad_maximum_fusion.1), calls=%async_computation.4 | async-start | bytes 524288 | tf_op jit(solution)/shard_map/all_to_all | solution.py:282
  281.8 5.8 %copy.51 = f32[4608,224]{1,0:T(8,128)} copy(f32[4608,224]{0,1:T(8,128)} %get-tuple-element.51) | data formatting | bytes 8257536 | tf_op jit(solution)/shard_map/add | solution.py:203
  287.6 1.8 fusion.18
  289.4 2.0 collective-permute-start.18
  291.4 1.8 all-to-all-done.4
  294.8 2.0 fusion.15
  296.8 52.7 %all_to_all.30 = bf16[16,144,224]{2,1,0:T(8,128)(2,1)S(1)} all-to-all(bf16[16,144,224]{2,1,0:T(8,128)(2,1)S(1)} %fusion.15), channel_id=1, replica_groups=mesh['seq'=16,'chip'=16,'core'=2] {'chip'}, dimensions={0} | all-to-all | bytes 2064384 | tf_op jit(solution)/shard_map/all_to_all | solution.py:215
  350.6 37.1 %all-gather.5.cloned.1.call-done = bf16[8448,128]{1,0:T(8,128)(2,1)} async-done(((bf16[528,128]{1,0:T(8,128)(2,1)}), bf16[8448,128]{1,0:T(8,128)(2,1)}) %all-gather.5.cloned.1.call-update) | async-done | bytes 2162704 | tf_op jit(solution)/shard_map/all_gather | solution.py:312
  387.7 3.7 copy_bitcast_fusion
  391.3 0.9 slice_convert_fusion.2
  (136 shorter events, 16.6 us)
Async XLA Ops:
  7.2 15.3 %copy-start = (bf16[1,64,128,128]{3,2,1,0:T(8,128)(2,1)S(1)}, bf16[1,64,128,128]{3,2,1,0:T(8,128)(2,1)}, u32[]{:S(2)}) copy-start(bf16[1,64,128,128]{3,2,1,0:T(8,128)(2,1)} %param.9) | copy-start | bytes 6291460
  12.0 18.1 %all-to-all-start = ((bf16[32,1,2]{2,1,0:T(2,128)(2,1)}), bf16[32,1,2]{2,1,0:T(2,128)(2,1)S(1)}, u32[]{:S(2)}, u32[]{:S(2)}) async-start(bf16[32,1,2]{2,1,0:T(2,128)(2,1)} %all_to_all.24), calls=%async_computation | async-start | bytes 32768 | tf_op jit(solution)/shard_map/all_to_all | solution.py:105
  27.7 10.0 %copy-start.4 = (f32[144]{0:T(256)S(1)}, f32[144]{0:T(256)}, u32[]{:S(2)}) copy-start(f32[144]{0:T(256)} %param.7) | copy-start | bytes 1732
  27.7 10.3 %copy-start.3 = (bf16[224,144]{0,1:T(8,128)(2,1)S(1)}, bf16[224,144]{0,1:T(8,128)(2,1)}, u32[]{:S(2)}) copy-start(bf16[224,144]{0,1:T(8,128)(2,1)} %param.6) | copy-start | bytes 193540
  27.7 11.4 %copy-start.5 = (s32[224]{0:T(256)S(1)}, s32[224]{0:T(256)}, u32[]{:S(2)}) copy-start(s32[224]{0:T(256)} %param.8) | copy-start | bytes 2692
  30.1 60.2 %all-to-all-start.1 = ((bf16[32,2,128,128]{3,2,1,0:T(8,128)(2,1)}), bf16[32,2,128,128]{3,2,1,0:T(8,128)(2,1)S(1)}, u32[]{:S(2)}, u32[]{:S(2)}) async-start(bf16[32,2,128,128]{3,2,1,0:T(8,128)(2,1)} %broadcast_select_fusion.1), calls=%async_computation.1 | async-start | bytes 4194304 | tf_op jit(solution)/shard_map/all_to_all | solution.py:98
  37.7 78.5 %all-gather.3.cloned.1.call-start = ((), (), s32[]{:S(2)}) async-start(), calls=%async_computation.5 | async-start | bytes 2433024 | tf_op jit(solution)/shard_map/all_gather | solution.py:119
  121.1 2.2 copy-start.2
  124.8 20.7 %collective-permute-start = (bf16[224,128]{1,0:T(8,128)(2,1)S(1)}, bf16[224,128]{1,0:T(8,128)(2,1)S(1)}, u32[]{:S(2)}, u32[]{:S(2)}) collective-permute-start(bf16[224,128]{1,0:T(8,128)(2,1)S(1)} %get-tuple-element.9), channel_id=1, source_target_pairs={{0,32},{32,64},{64,96},{96,128},{128,160},{160,192},{192,224},{224... | collective-permute-start | bytes 172040 | tf_op jit(solution)/shard_map/ppermute | solution.py:31
  128.5 18.2 %collective-permute-start.1 = (bf16[224,128]{1,0:T(8,128)(2,1)S(1)}, bf16[224,128]{1,0:T(8,128)(2,1)S(1)}, u32[]{:S(2)}, u32[]{:S(2)}) collective-permute-start(bf16[224,128]{1,0:T(8,128)(2,1)S(1)} %get-tuple-element.9), channel_id=1, source_target_pairs={{0,64},{32,96},{64,128},{96,160},{128,192},{160,224},{192,256},{22... | collective-permute-start | bytes 172040 | tf_op jit(solution)/shard_map/ppermute | solution.py:31
  132.1 16.5 %collective-permute-start.2 = (bf16[224,128]{1,0:T(8,128)(2,1)S(1)}, bf16[224,128]{1,0:T(8,128)(2,1)S(1)}, u32[]{:S(2)}, u32[]{:S(2)}) collective-permute-start(bf16[224,128]{1,0:T(8,128)(2,1)S(1)} %get-tuple-element.9), channel_id=1, source_target_pairs={{0,96},{32,128},{64,160},{96,192},{128,224},{160,256},{192,288},{2... | collective-permute-start | bytes 172040 | tf_op jit(solution)/shard_map/ppermute | solution.py:31
  136.4 13.6 %collective-permute-start.3 = (bf16[224,128]{1,0:T(8,128)(2,1)S(1)}, bf16[224,128]{1,0:T(8,128)(2,1)S(1)}, u32[]{:S(2)}, u32[]{:S(2)}) collective-permute-start(bf16[224,128]{1,0:T(8,128)(2,1)S(1)} %get-tuple-element.9), channel_id=1, source_target_pairs={{0,128},{32,160},{64,192},{96,224},{128,256},{160,288},{192,320},{... | collective-permute-start | bytes 172040 | tf_op jit(solution)/shard_map/ppermute | solution.py:31
  141.3 8.7 %collective-permute-start.4 = (bf16[224,128]{1,0:T(8,128)(2,1)S(1)}, bf16[224,128]{1,0:T(8,128)(2,1)S(1)}, u32[]{:S(2)}, u32[]{:S(2)}) collective-permute-start(bf16[224,128]{1,0:T(8,128)(2,1)S(1)} %get-tuple-element.9), channel_id=1, source_target_pairs={{0,160},{32,192},{64,224},{96,256},{128,288},{160,320},{192,352},{... | collective-permute-start | bytes 172040 | tf_op jit(solution)/shard_map/ppermute | solution.py:31
  145.5 4.6 %collective-permute-start.5 = (bf16[224,128]{1,0:T(8,128)(2,1)S(1)}, bf16[224,128]{1,0:T(8,128)(2,1)S(1)}, u32[]{:S(2)}, u32[]{:S(2)}) collective-permute-start(bf16[224,128]{1,0:T(8,128)(2,1)S(1)} %get-tuple-element.9), channel_id=1, source_target_pairs={{0,192},{32,224},{64,256},{96,288},{128,320},{160,352},{192,384},{... | collective-permute-start | bytes 172040 | tf_op jit(solution)/shard_map/ppermute | solution.py:31
  146.8 3.6 collective-permute-start.6
  148.6 3.3 collective-permute-start.7
  152.0 3.8 collective-permute-start.8
  155.8 1.1 copy-start.6
  161.1 3.8 collective-permute-start.9
  165.1 7.2 %collective-permute-start.10 = (bf16[224,128]{1,0:T(8,128)(2,1)S(1)}, bf16[224,128]{1,0:T(8,128)(2,1)S(1)}, u32[]{:S(2)}, u32[]{:S(2)}) collective-permute-start(bf16[224,128]{1,0:T(8,128)(2,1)S(1)} %get-tuple-element.14), channel_id=1, source_target_pairs={{32,0},{64,32},{96,64},{128,96},{160,128},{192,160},{224,192},{256... | collective-permute-start | bytes 172040 | tf_op jit(solution)/shard_map/ppermute | solution.py:31
  166.4 7.5 %collective-permute-start.11 = (bf16[224,128]{1,0:T(8,128)(2,1)S(1)}, bf16[224,128]{1,0:T(8,128)(2,1)S(1)}, u32[]{:S(2)}, u32[]{:S(2)}) collective-permute-start(bf16[224,128]{1,0:T(8,128)(2,1)S(1)} %get-tuple-element.21), channel_id=1, source_target_pairs={{64,0},{96,32},{128,64},{160,96},{192,128},{224,160},{256,192},{28... | collective-permute-start | bytes 172040 | tf_op jit(solution)/shard_map/ppermute | solution.py:31
  167.7 9.4 %collective-permute-start.12 = (bf16[224,128]{1,0:T(8,128)(2,1)S(1)}, bf16[224,128]{1,0:T(8,128)(2,1)S(1)}, u32[]{:S(2)}, u32[]{:S(2)}) collective-permute-start(bf16[224,128]{1,0:T(8,128)(2,1)S(1)} %get-tuple-element.20), channel_id=1, source_target_pairs={{96,0},{128,32},{160,64},{192,96},{224,128},{256,160},{288,192},{3... | collective-permute-start | bytes 172040 | tf_op jit(solution)/shard_map/ppermute | solution.py:31
  169.7 12.7 %collective-permute-start.13 = (bf16[224,128]{1,0:T(8,128)(2,1)S(1)}, bf16[224,128]{1,0:T(8,128)(2,1)S(1)}, u32[]{:S(2)}, u32[]{:S(2)}) collective-permute-start(bf16[224,128]{1,0:T(8,128)(2,1)S(1)} %get-tuple-element.19), channel_id=1, source_target_pairs={{128,0},{160,32},{192,64},{224,96},{256,128},{288,160},{320,192},{... | collective-permute-start | bytes 172040 | tf_op jit(solution)/shard_map/ppermute | solution.py:31
  171.0 14.6 %collective-permute-start.14 = (bf16[224,128]{1,0:T(8,128)(2,1)S(1)}, bf16[224,128]{1,0:T(8,128)(2,1)S(1)}, u32[]{:S(2)}, u32[]{:S(2)}) collective-permute-start(bf16[224,128]{1,0:T(8,128)(2,1)S(1)} %get-tuple-element.18), channel_id=1, source_target_pairs={{160,0},{192,32},{224,64},{256,96},{288,128},{320,160},{352,192},{... | collective-permute-start | bytes 172040 | tf_op jit(solution)/shard_map/ppermute | solution.py:31
  172.3 22.4 %collective-permute-start.15 = (bf16[224,128]{1,0:T(8,128)(2,1)S(1)}, bf16[224,128]{1,0:T(8,128)(2,1)S(1)}, u32[]{:S(2)}, u32[]{:S(2)}) collective-permute-start(bf16[224,128]{1,0:T(8,128)(2,1)S(1)} %get-tuple-element.17), channel_id=1, source_target_pairs={{192,0},{224,32},{256,64},{288,96},{320,128},{352,160},{384,192},{... | collective-permute-start | bytes 172040 | tf_op jit(solution)/shard_map/ppermute | solution.py:31
  173.9 20.8 %collective-permute-start.16 = (bf16[224,128]{1,0:T(8,128)(2,1)S(1)}, bf16[224,128]{1,0:T(8,128)(2,1)S(1)}, u32[]{:S(2)}, u32[]{:S(2)}) collective-permute-start(bf16[224,128]{1,0:T(8,128)(2,1)S(1)} %get-tuple-element.16), channel_id=1, source_target_pairs={{224,0},{256,32},{288,64},{320,96},{352,128},{384,160},{416,192},{... | collective-permute-start | bytes 172040 | tf_op jit(solution)/shard_map/ppermute | solution.py:31
  177.1 17.7 %collective-permute-start.17 = (bf16[224,128]{1,0:T(8,128)(2,1)S(1)}, bf16[224,128]{1,0:T(8,128)(2,1)S(1)}, u32[]{:S(2)}, u32[]{:S(2)}) collective-permute-start(bf16[224,128]{1,0:T(8,128)(2,1)S(1)} %get-tuple-element.15), channel_id=1, source_target_pairs={{256,0},{288,32},{320,64},{352,96},{384,128},{416,160},{448,192},{... | collective-permute-start | bytes 172040 | tf_op jit(solution)/shard_map/ppermute | solution.py:31
  209.3 62.0 %all-to-all-start.3 = ((bf16[16,528,128]{2,1,0:T(8,128)(2,1)}), bf16[16,528,128]{2,1,0:T(8,128)(2,1)}, u32[]{:S(2)}, u32[]{:S(2)}) async-start(bf16[16,528,128]{2,1,0:T(8,128)(2,1)} %pad_maximum_fusion), calls=%async_computation.3 | async-start | bytes 4325376 | tf_op jit(solution)/shard_map/all_to_all | solution.py:255
  274.5 18.7 %all-to-all-start.4 = ((bf16[32,32,128]{2,1,0:T(8,128)(2,1)}), bf16[32,32,128]{2,1,0:T(8,128)(2,1)S(1)}, u32[]{:S(2)}, u32[]{:S(2)}) async-start(bf16[32,32,128]{2,1,0:T(8,128)(2,1)} %pad_maximum_fusion.1), calls=%async_computation.4 | async-start | bytes 524288 | tf_op jit(solution)/shard_map/all_to_all | solution.py:282
  281.7 105.9 %all-gather.5.cloned.1.call-start = ((), (), s32[]{:S(2)}) async-start(), calls=%async_computation.6 | async-start | bytes 2297856 | tf_op jit(solution)/shard_map/all_gather | solution.py:312
  289.4 5.4 %collective-permute-start.18 = (bf16[16,144,224]{2,1,0:T(8,128)(2,1)S(1)}, bf16[16,144,224]{2,1,0:T(8,128)(2,1)S(1)}, u32[]{:S(2)}, u32[]{:S(2)}) collective-permute-start(bf16[16,144,224]{2,1,0:T(8,128)(2,1)S(1)} %fusion.18), channel_id=1, source_target_pairs={{0,1},{1,0},{2,3},{3,2},{4,5},{5,4},{6,7},{7,6},{8,9},{9,8},{10,11... | collective-permute-start | bytes 3096584 | tf_op jit(solution)/shard_map/ppermute | solution.py:25
  387.7 5.2 %copy-start.1 = (bf16[1,64,128,128]{3,2,1,0:T(8,128)(2,1)S(1)}, bf16[1,64,128,128]{3,2,1,0:T(8,128)(2,1)}, u32[]{:S(2)}) copy-start(bf16[1,64,128,128]{3,2,1,0:T(8,128)(2,1)} %param.9) | copy-start | bytes 6291460
Sparse Core Ops, SparseCore 0:
  42.2 73.9 all-gather.2
  294.9 92.6 all-gather.4

commit v11 on v10

--- a/solution.py
+++ b/solution.py
@@ -301,28 +301,20 @@
     gain_mine = jnp.sum(gain_recv[:, :feat] + gain_recv[:, feat:], axis=0)
     mine_top = lax.reduce_precision(gain_mine, exponent_bits=8, mantissa_bits=7)
     mine_pair = jnp.stack([mine_top, gain_mine - mine_top]).astype(jnp.bfloat16).reshape(-1)
-    owned_rows = slots * band
-    gather_send = jnp.concatenate(
-        [
-            owned_band.reshape(owned_rows, BLK).astype(jnp.bfloat16),
-            jnp.pad(mine_pair, (0, side * BLK - 2 * feat)).reshape(side, BLK),
-        ],
-        axis=0,
-    )
-    gathered_back = lax.all_gather(gather_send, "seq", axis=0, tiled=True).reshape(
-        n_seq, owned_rows + side, BLK
-    )
-    block_grads = (
-        jnp.transpose(
-            gathered_back[:, :owned_rows]
-            .astype(jnp.float32)
-            .reshape(n_seq, slots, band, BLK),
-            (1, 0, 2, 3),
-        )
-        .reshape(slots, BLK, BLK)
-        .astype(jnp.bfloat16)
-    )
-    gain_back = gathered_back[:, owned_rows:].reshape(n_seq, side * BLK).astype(jnp.float32)
+    gathered_back = lax.all_gather(
+        jnp.concatenate(
+            [
+                owned_band.astype(jnp.bfloat16),
+                jnp.pad(mine_pair, (0, band * BLK - 2 * feat)).reshape(1, band, BLK),
+            ],
+            axis=0,
+        ),
+        "seq",
+        axis=1,
+        tiled=True,
+    )
+    block_grads = gathered_back[:slots]
+    gain_back = gathered_back[slots].reshape(n_seq, band * BLK).astype(jnp.float32)
     gain_total = jnp.sum(gain_back[:, :feat] + gain_back[:, feat : 2 * feat], axis=0)
     return (attn_rows, tokens_grad, gain_total, block_grads[None])
 

time: 401 us -> 404 us (level)
  waiting for transfers between devices: 185 us -> 190 us
    all_gather x1, waiting for transfers between devices: 37.1 us -> 42.1 us  [body(): lax.all_gather(jnp.concatenate([owned_band.astype(jnp.bfloat16), jnp.pad(...]
where the time goes in v11:
time: 404 us; the launch traced here: 402 us
  waiting for transfers between devices  190 us (47%)
  starting transfers between devices  76.5 us (19%)
  blocking collectives  50.5 us (12%)
  local copies, waits for them, and re-layouts  29.8 us (7%)
  other arithmetic  27.1 us (7%)
  between operations  14.9 us (4%)
  matrix products  13.4 us (3%)
    all_to_all x1, waiting for transfers between devices, body(): lax.all_to_all(jnp.concatenate([block_send.astype(jnp.bfloat16), gain_sen...  52.5 us
    all_to_all x1, waiting for transfers between devices, body(): lax.all_to_all(outgoing.reshape(groups, CAP, BLK, BLK), WT, split_axis=0,...  50.7 us
    all_to_all x1, blocking collectives, body(): lax.all_to_all((keep + from_other).astype(jnp.bfloat16), 'chip', split_ax...  50.5 us
    all_gather x1, waiting for transfers between devices, body(): lax.all_gather(jnp.concatenate([owned_band.astype(jnp.bfloat16), jnp.pad(...  42.1 us
    ppermute x16, starting transfers between devices, shifted(): lax.ppermute(value, axis, [(source, source + steps) for source in range(i...  35.6 us
    all_gather x1, waiting for transfers between devices, body(): lax.all_gather(jnp.concatenate([tokens_in, gain_rows, jnp.zeros((side_row...  20.3 us
    ppermute x16, waiting for transfers between devices, shifted(): lax.ppermute(value, axis, [(source, source + steps) for source in range(i...  19.3 us
    all_to_all x1, starting transfers between devices, body(): lax.all_to_all(outgoing_pos[:dump_slot].reshape(groups, CAP), WT, split_a...  10.2 us
  transfers between devices with their start and end apart: 25, of which 15 were waited for; matrix products, arithmetic and copies ran while one was open for 7% of the time, Pallas kernels for 0%

profile of v11, /device:TPU:6, one launch (start us, length us, event | category | flops | bytes accessed | tf_op | source)
XLA Modules:
  0.0 402.0 jit_solution(9375914404051137103)
XLA Ops:
  7.2 0.8 fusion.81
  10.5 0.8 scatter_custom_fusion
  12.0 10.2 %all-to-all-start = ((bf16[32,1,2]{2,1,0:T(2,128)(2,1)}), bf16[32,1,2]{2,1,0:T(2,128)(2,1)S(1)}, u32[]{:S(2)}, u32[]{:S(2)}) async-start(bf16[32,1,2]{2,1,0:T(2,128)(2,1)} %all_to_all.24), calls=%async_computation | async-start | bytes 32768 | tf_op jit(solution)/shard_map/all_to_all | solution.py:105
  22.5 2.1 gather_fusion
  24.6 3.1 broadcast_select_fusion.1
  27.7 2.3 all-to-all-done
  30.1 7.6 %all-to-all-start.1 = ((bf16[32,2,128,128]{3,2,1,0:T(8,128)(2,1)}), bf16[32,2,128,128]{3,2,1,0:T(8,128)(2,1)S(1)}, u32[]{:S(2)}, u32[]{:S(2)}) async-start(bf16[32,2,128,128]{3,2,1,0:T(8,128)(2,1)} %broadcast_select_fusion.1), calls=%async_computation.1 | async-start | bytes 4194304 | tf_op jit(solution)/shard_map/all_to_all | solution.py:98
  39.6 50.7 %all-to-all-done.1 = bf16[32,2,128,128]{3,2,1,0:T(8,128)(2,1)S(1)} async-done(((bf16[32,2,128,128]{3,2,1,0:T(8,128)(2,1)}), bf16[32,2,128,128]{3,2,1,0:T(8,128)(2,1)S(1)}, u32[]{:S(2)}, u32[]{:S(2)}) %all-to-all-start.1) | async-done | bytes 2097184 | tf_op jit(solution)/shard_map/all_to_all | solution.py:98
  90.3 2.4 gather_fusion.1
  92.7 1.9 broadcast_select_fusion
  94.6 1.2 fusion.97
  95.9 20.3 %all-gather.3.cloned.1.call-done = bf16[232,4608]{0,1:T(8,128)(2,1)} async-done(((bf16[232,144]{0,1:T(8,128)(2,1)}), bf16[232,4608]{0,1:T(8,128)(2,1)}) %all-gather.3.cloned.1.call-update) | async-done | bytes 2138128 | tf_op jit(solution)/shard_map/all_gather | solution.py:119
  116.2 2.8 copy.49
  119.5 1.6 slice_convert_fusion
  121.1 2.2 fusion.14
  123.3 0.8 fusion.89
  124.8 3.8 collective-permute-start
  128.5 3.6 collective-permute-start.1
  132.1 4.2 %collective-permute-start.2 = (bf16[224,128]{1,0:T(8,128)(2,1)S(1)}, bf16[224,128]{1,0:T(8,128)(2,1)S(1)}, u32[]{:S(2)}, u32[]{:S(2)}) collective-permute-start(bf16[224,128]{1,0:T(8,128)(2,1)S(1)} %get-tuple-element.9), channel_id=1, source_target_pairs={{0,96},{32,128},{64,160},{96,192},{128,224},{160,256},{192,288},{2... | collective-permute-start | bytes 172040 | tf_op jit(solution)/shard_map/ppermute | solution.py:31
  136.4 4.9 %collective-permute-start.3 = (bf16[224,128]{1,0:T(8,128)(2,1)S(1)}, bf16[224,128]{1,0:T(8,128)(2,1)S(1)}, u32[]{:S(2)}, u32[]{:S(2)}) collective-permute-start(bf16[224,128]{1,0:T(8,128)(2,1)S(1)} %get-tuple-element.9), channel_id=1, source_target_pairs={{0,128},{32,160},{64,192},{96,224},{128,256},{160,288},{192,320},{... | collective-permute-start | bytes 172040 | tf_op jit(solution)/shard_map/ppermute | solution.py:31
  141.3 4.1 %collective-permute-start.4 = (bf16[224,128]{1,0:T(8,128)(2,1)S(1)}, bf16[224,128]{1,0:T(8,128)(2,1)S(1)}, u32[]{:S(2)}, u32[]{:S(2)}) collective-permute-start(bf16[224,128]{1,0:T(8,128)(2,1)S(1)} %get-tuple-element.9), channel_id=1, source_target_pairs={{0,160},{32,192},{64,224},{96,256},{128,288},{160,320},{192,352},{... | collective-permute-start | bytes 172040 | tf_op jit(solution)/shard_map/ppermute | solution.py:31
  145.5 1.3 collective-permute-start.5
  146.8 1.8 collective-permute-start.6
  148.6 1.3 collective-permute-start.7
  150.4 1.5 collective-permute-done.7
  152.0 2.1 collective-permute-start.8
  154.1 0.8 fusion.91
  155.8 1.1 fusion.93
  156.9 1.4 multiply_reduce_fusion
  158.3 1.2 fusion.13
  160.0 1.1 select_convert_fusion
  161.1 2.2 collective-permute-start.9
  165.1 1.3 collective-permute-start.10
  166.4 1.3 collective-permute-start.11
  167.7 1.3 collective-permute-start.12
  169.7 1.3 collective-permute-start.13
  171.0 1.3 collective-permute-start.14
  172.3 1.3 collective-permute-start.15
  173.9 1.3 collective-permute-start.16
  175.2 1.9 collective-permute-done.12
  177.1 1.5 collective-permute-start.17
  178.6 0.9 fusion.87
  179.5 2.8 collective-permute-done.13
  182.4 3.3 collective-permute-done.14
  185.6 9.1 %collective-permute-done.15 = bf16[224,128]{1,0:T(8,128)(2,1)S(1)} collective-permute-done((bf16[224,128]{1,0:T(8,128)(2,1)S(1)}, bf16[224,128]{1,0:T(8,128)(2,1)S(1)}, u32[]{:S(2)}, u32[]{:S(2)}) %collective-permute-start.15) | collective-permute-done | bytes 57376 | tf_op jit(solution)/shard_map/ppermute | solution.py:31
  195.4 0.9 fusion.85
  196.4 3.5 fusion.5
  199.9 1.7 maximum_maximum_fusion
  201.6 3.8 gather_fusion.2
  205.4 2.1 copy.47
  207.8 1.5 pad_maximum_fusion
  209.3 9.5 %all-to-all-start.3 = ((bf16[16,528,128]{2,1,0:T(8,128)(2,1)}), bf16[16,528,128]{2,1,0:T(8,128)(2,1)}, u32[]{:S(2)}, u32[]{:S(2)}) async-start(bf16[16,528,128]{2,1,0:T(8,128)(2,1)} %pad_maximum_fusion), calls=%async_computation.3 | async-start | bytes 4325376 | tf_op jit(solution)/shard_map/all_to_all | solution.py:255
  218.8 52.5 %all-to-all-done.3 = bf16[16,528,128]{2,1,0:T(8,128)(2,1)} async-done(((bf16[16,528,128]{2,1,0:T(8,128)(2,1)}), bf16[16,528,128]{2,1,0:T(8,128)(2,1)}, u32[]{:S(2)}, u32[]{:S(2)}) %all-to-all-start.3) | async-done | bytes 2162720 | tf_op jit(solution)/shard_map/all_to_all | solution.py:255
  271.3 1.9 convert_reduce_fusion
  274.5 7.2 %all-to-all-start.4 = ((bf16[32,32,128]{2,1,0:T(8,128)(2,1)}), bf16[32,32,128]{2,1,0:T(8,128)(2,1)S(1)}, u32[]{:S(2)}, u32[]{:S(2)}) async-start(bf16[32,32,128]{2,1,0:T(8,128)(2,1)} %pad_maximum_fusion.1), calls=%async_computation.4 | async-start | bytes 524288 | tf_op jit(solution)/shard_map/all_to_all | solution.py:282
  281.8 5.8 %copy.46 = f32[4608,224]{1,0:T(8,128)} copy(f32[4608,224]{0,1:T(8,128)} %get-tuple-element.51) | data formatting | bytes 8257536 | tf_op jit(solution)/shard_map/add | solution.py:203
  287.6 1.8 fusion.18
  289.4 2.0 collective-permute-start.18
  291.4 1.8 all-to-all-done.4
  294.8 2.0 fusion.15
  296.8 50.5 %all_to_all.30 = bf16[16,144,224]{2,1,0:T(8,128)(2,1)S(1)} all-to-all(bf16[16,144,224]{2,1,0:T(8,128)(2,1)S(1)} %fusion.15), channel_id=1, replica_groups=mesh['seq'=16,'chip'=16,'core'=2] {'chip'}, dimensions={0} | all-to-all | bytes 2064384 | tf_op jit(solution)/shard_map/all_to_all | solution.py:215
  348.4 42.1 %all-gather.5.cloned.1.call-done = bf16[65,128,128]{2,1,0:T(8,128)(2,1)} async-done(((bf16[65,8,128]{2,1,0:T(8,128)(2,1)}), bf16[65,128,128]{2,1,0:T(8,128)(2,1)}) %all-gather.5.cloned.1.call-update) | async-done | bytes 2129936 | tf_op jit(solution)/shard_map/all_gather | solution.py:304
  390.6 0.8 slice_convert_fusion.2
  392.0 3.2 slice_bitcast_fusion
  (136 shorter events, 16.6 us)
Async XLA Ops:
  7.2 15.3 %copy-start = (bf16[1,64,128,128]{3,2,1,0:T(8,128)(2,1)S(1)}, bf16[1,64,128,128]{3,2,1,0:T(8,128)(2,1)}, u32[]{:S(2)}) copy-start(bf16[1,64,128,128]{3,2,1,0:T(8,128)(2,1)} %param.9) | copy-start | bytes 6291460
  12.0 18.1 %all-to-all-start = ((bf16[32,1,2]{2,1,0:T(2,128)(2,1)}), bf16[32,1,2]{2,1,0:T(2,128)(2,1)S(1)}, u32[]{:S(2)}, u32[]{:S(2)}) async-start(bf16[32,1,2]{2,1,0:T(2,128)(2,1)} %all_to_all.24), calls=%async_computation | async-start | bytes 32768 | tf_op jit(solution)/shard_map/all_to_all | solution.py:105
  27.7 10.0 %copy-start.4 = (f32[144]{0:T(256)S(1)}, f32[144]{0:T(256)}, u32[]{:S(2)}) copy-start(f32[144]{0:T(256)} %param.7) | copy-start | bytes 1732
  27.7 10.3 %copy-start.3 = (bf16[224,144]{0,1:T(8,128)(2,1)S(1)}, bf16[224,144]{0,1:T(8,128)(2,1)}, u32[]{:S(2)}) copy-start(bf16[224,144]{0,1:T(8,128)(2,1)} %param.6) | copy-start | bytes 193540
  27.7 11.4 %copy-start.5 = (s32[224]{0:T(256)S(1)}, s32[224]{0:T(256)}, u32[]{:S(2)}) copy-start(s32[224]{0:T(256)} %param.8) | copy-start | bytes 2692
  30.1 60.2 %all-to-all-start.1 = ((bf16[32,2,128,128]{3,2,1,0:T(8,128)(2,1)}), bf16[32,2,128,128]{3,2,1,0:T(8,128)(2,1)S(1)}, u32[]{:S(2)}, u32[]{:S(2)}) async-start(bf16[32,2,128,128]{3,2,1,0:T(8,128)(2,1)} %broadcast_select_fusion.1), calls=%async_computation.1 | async-start | bytes 4194304 | tf_op jit(solution)/shard_map/all_to_all | solution.py:98
  37.7 78.5 %all-gather.3.cloned.1.call-start = ((), (), s32[]{:S(2)}) async-start(), calls=%async_computation.5 | async-start | bytes 2433024 | tf_op jit(solution)/shard_map/all_gather | solution.py:119
  121.1 2.2 copy-start.2
  124.8 20.7 %collective-permute-start = (bf16[224,128]{1,0:T(8,128)(2,1)S(1)}, bf16[224,128]{1,0:T(8,128)(2,1)S(1)}, u32[]{:S(2)}, u32[]{:S(2)}) collective-permute-start(bf16[224,128]{1,0:T(8,128)(2,1)S(1)} %get-tuple-element.9), channel_id=1, source_target_pairs={{0,32},{32,64},{64,96},{96,128},{128,160},{160,192},{192,224},{224... | collective-permute-start | bytes 172040 | tf_op jit(solution)/shard_map/ppermute | solution.py:31
  128.5 18.2 %collective-permute-start.1 = (bf16[224,128]{1,0:T(8,128)(2,1)S(1)}, bf16[224,128]{1,0:T(8,128)(2,1)S(1)}, u32[]{:S(2)}, u32[]{:S(2)}) collective-permute-start(bf16[224,128]{1,0:T(8,128)(2,1)S(1)} %get-tuple-element.9), channel_id=1, source_target_pairs={{0,64},{32,96},{64,128},{96,160},{128,192},{160,224},{192,256},{22... | collective-permute-start | bytes 172040 | tf_op jit(solution)/shard_map/ppermute | solution.py:31
  132.1 16.5 %collective-permute-start.2 = (bf16[224,128]{1,0:T(8,128)(2,1)S(1)}, bf16[224,128]{1,0:T(8,128)(2,1)S(1)}, u32[]{:S(2)}, u32[]{:S(2)}) collective-permute-start(bf16[224,128]{1,0:T(8,128)(2,1)S(1)} %get-tuple-element.9), channel_id=1, source_target_pairs={{0,96},{32,128},{64,160},{96,192},{128,224},{160,256},{192,288},{2... | collective-permute-start | bytes 172040 | tf_op jit(solution)/shard_map/ppermute | solution.py:31
  136.4 13.6 %collective-permute-start.3 = (bf16[224,128]{1,0:T(8,128)(2,1)S(1)}, bf16[224,128]{1,0:T(8,128)(2,1)S(1)}, u32[]{:S(2)}, u32[]{:S(2)}) collective-permute-start(bf16[224,128]{1,0:T(8,128)(2,1)S(1)} %get-tuple-element.9), channel_id=1, source_target_pairs={{0,128},{32,160},{64,192},{96,224},{128,256},{160,288},{192,320},{... | collective-permute-start | bytes 172040 | tf_op jit(solution)/shard_map/ppermute | solution.py:31
  141.3 8.7 %collective-permute-start.4 = (bf16[224,128]{1,0:T(8,128)(2,1)S(1)}, bf16[224,128]{1,0:T(8,128)(2,1)S(1)}, u32[]{:S(2)}, u32[]{:S(2)}) collective-permute-start(bf16[224,128]{1,0:T(8,128)(2,1)S(1)} %get-tuple-element.9), channel_id=1, source_target_pairs={{0,160},{32,192},{64,224},{96,256},{128,288},{160,320},{192,352},{... | collective-permute-start | bytes 172040 | tf_op jit(solution)/shard_map/ppermute | solution.py:31
  145.5 4.6 %collective-permute-start.5 = (bf16[224,128]{1,0:T(8,128)(2,1)S(1)}, bf16[224,128]{1,0:T(8,128)(2,1)S(1)}, u32[]{:S(2)}, u32[]{:S(2)}) collective-permute-start(bf16[224,128]{1,0:T(8,128)(2,1)S(1)} %get-tuple-element.9), channel_id=1, source_target_pairs={{0,192},{32,224},{64,256},{96,288},{128,320},{160,352},{192,384},{... | collective-permute-start | bytes 172040 | tf_op jit(solution)/shard_map/ppermute | solution.py:31
  146.8 3.6 collective-permute-start.6
  148.6 3.3 collective-permute-start.7
  152.0 3.8 collective-permute-start.8
  155.8 1.1 copy-start.6
  161.1 3.8 collective-permute-start.9
  165.1 7.2 %collective-permute-start.10 = (bf16[224,128]{1,0:T(8,128)(2,1)S(1)}, bf16[224,128]{1,0:T(8,128)(2,1)S(1)}, u32[]{:S(2)}, u32[]{:S(2)}) collective-permute-start(bf16[224,128]{1,0:T(8,128)(2,1)S(1)} %get-tuple-element.14), channel_id=1, source_target_pairs={{32,0},{64,32},{96,64},{128,96},{160,128},{192,160},{224,192},{256... | collective-permute-start | bytes 172040 | tf_op jit(solution)/shard_map/ppermute | solution.py:31
  166.4 7.5 %collective-permute-start.11 = (bf16[224,128]{1,0:T(8,128)(2,1)S(1)}, bf16[224,128]{1,0:T(8,128)(2,1)S(1)}, u32[]{:S(2)}, u32[]{:S(2)}) collective-permute-start(bf16[224,128]{1,0:T(8,128)(2,1)S(1)} %get-tuple-element.21), channel_id=1, source_target_pairs={{64,0},{96,32},{128,64},{160,96},{192,128},{224,160},{256,192},{28... | collective-permute-start | bytes 172040 | tf_op jit(solution)/shard_map/ppermute | solution.py:31
  167.7 9.4 %collective-permute-start.12 = (bf16[224,128]{1,0:T(8,128)(2,1)S(1)}, bf16[224,128]{1,0:T(8,128)(2,1)S(1)}, u32[]{:S(2)}, u32[]{:S(2)}) collective-permute-start(bf16[224,128]{1,0:T(8,128)(2,1)S(1)} %get-tuple-element.20), channel_id=1, source_target_pairs={{96,0},{128,32},{160,64},{192,96},{224,128},{256,160},{288,192},{3... | collective-permute-start | bytes 172040 | tf_op jit(solution)/shard_map/ppermute | solution.py:31
  169.7 12.7 %collective-permute-start.13 = (bf16[224,128]{1,0:T(8,128)(2,1)S(1)}, bf16[224,128]{1,0:T(8,128)(2,1)S(1)}, u32[]{:S(2)}, u32[]{:S(2)}) collective-permute-start(bf16[224,128]{1,0:T(8,128)(2,1)S(1)} %get-tuple-element.19), channel_id=1, source_target_pairs={{128,0},{160,32},{192,64},{224,96},{256,128},{288,160},{320,192},{... | collective-permute-start | bytes 172040 | tf_op jit(solution)/shard_map/ppermute | solution.py:31
  171.0 14.6 %collective-permute-start.14 = (bf16[224,128]{1,0:T(8,128)(2,1)S(1)}, bf16[224,128]{1,0:T(8,128)(2,1)S(1)}, u32[]{:S(2)}, u32[]{:S(2)}) collective-permute-start(bf16[224,128]{1,0:T(8,128)(2,1)S(1)} %get-tuple-element.18), channel_id=1, source_target_pairs={{160,0},{192,32},{224,64},{256,96},{288,128},{320,160},{352,192},{... | collective-permute-start | bytes 172040 | tf_op jit(solution)/shard_map/ppermute | solution.py:31
  172.3 22.4 %collective-permute-start.15 = (bf16[224,128]{1,0:T(8,128)(2,1)S(1)}, bf16[224,128]{1,0:T(8,128)(2,1)S(1)}, u32[]{:S(2)}, u32[]{:S(2)}) collective-permute-start(bf16[224,128]{1,0:T(8,128)(2,1)S(1)} %get-tuple-element.17), channel_id=1, source_target_pairs={{192,0},{224,32},{256,64},{288,96},{320,128},{352,160},{384,192},{... | collective-permute-start | bytes 172040 | tf_op jit(solution)/shard_map/ppermute | solution.py:31
  173.9 20.8 %collective-permute-start.16 = (bf16[224,128]{1,0:T(8,128)(2,1)S(1)}, bf16[224,128]{1,0:T(8,128)(2,1)S(1)}, u32[]{:S(2)}, u32[]{:S(2)}) collective-permute-start(bf16[224,128]{1,0:T(8,128)(2,1)S(1)} %get-tuple-element.16), channel_id=1, source_target_pairs={{224,0},{256,32},{288,64},{320,96},{352,128},{384,160},{416,192},{... | collective-permute-start | bytes 172040 | tf_op jit(solution)/shard_map/ppermute | solution.py:31
  177.1 17.7 %collective-permute-start.17 = (bf16[224,128]{1,0:T(8,128)(2,1)S(1)}, bf16[224,128]{1,0:T(8,128)(2,1)S(1)}, u32[]{:S(2)}, u32[]{:S(2)}) collective-permute-start(bf16[224,128]{1,0:T(8,128)(2,1)S(1)} %get-tuple-element.15), channel_id=1, source_target_pairs={{256,0},{288,32},{320,64},{352,96},{384,128},{416,160},{448,192},{... | collective-permute-start | bytes 172040 | tf_op jit(solution)/shard_map/ppermute | solution.py:31
  209.3 62.0 %all-to-all-start.3 = ((bf16[16,528,128]{2,1,0:T(8,128)(2,1)}), bf16[16,528,128]{2,1,0:T(8,128)(2,1)}, u32[]{:S(2)}, u32[]{:S(2)}) async-start(bf16[16,528,128]{2,1,0:T(8,128)(2,1)} %pad_maximum_fusion), calls=%async_computation.3 | async-start | bytes 4325376 | tf_op jit(solution)/shard_map/all_to_all | solution.py:255
  274.5 18.7 %all-to-all-start.4 = ((bf16[32,32,128]{2,1,0:T(8,128)(2,1)}), bf16[32,32,128]{2,1,0:T(8,128)(2,1)S(1)}, u32[]{:S(2)}, u32[]{:S(2)}) async-start(bf16[32,32,128]{2,1,0:T(8,128)(2,1)} %pad_maximum_fusion.1), calls=%async_computation.4 | async-start | bytes 524288 | tf_op jit(solution)/shard_map/all_to_all | solution.py:282
  281.7 108.8 %all-gather.5.cloned.1.call-start = ((), (), s32[]{:S(2)}) async-start(), calls=%async_computation.6 | async-start | bytes 2263040 | tf_op jit(solution)/shard_map/all_gather | solution.py:304
  289.4 5.4 %collective-permute-start.18 = (bf16[16,144,224]{2,1,0:T(8,128)(2,1)S(1)}, bf16[16,144,224]{2,1,0:T(8,128)(2,1)S(1)}, u32[]{:S(2)}, u32[]{:S(2)}) collective-permute-start(bf16[16,144,224]{2,1,0:T(8,128)(2,1)S(1)} %fusion.18), channel_id=1, source_target_pairs={{0,1},{1,0},{2,3},{3,2},{4,5},{5,4},{6,7},{7,6},{8,9},{9,8},{10,11... | collective-permute-start | bytes 3096584 | tf_op jit(solution)/shard_map/ppermute | solution.py:25
  391.4 3.8 copy-start.1
Sparse Core Ops, SparseCore 0:
  42.2 73.9 all-gather.2
  294.9 95.5 all-gather.4
